TPU v7x, 128 devices: a whole 4x4x4 slice. The times are simulated.
128 devices in a mesh: layer: 16 (over y, x), prow: 4 (over z), pcol: 2 (over core).
Axes of the slice: x: 4, y: 4, z: 4, core: 2. Of those that a mesh axis runs over, the one named last changes fastest.
Arguments:
- front: bfloat16 [16, 2048, 32768], P('layer', 'prow', 'pcol'), may hold values from -6 to 6
- pivots: bfloat16 [16, 2, 256, 32768], P('layer', None, 'prow', 'pcol'), may hold values from -0.8984375 to 0.8984375
- inverses: bfloat16 [16, 2, 256, 256], P('layer'), may hold values from -0.1875 to 0.1875
- slab_pattern: int32 [16, 8, 128], P('layer', 'prow', 'pcol'), may hold values 0 or 1
- pivot_pattern: int32 [16, 2, 128], P('layer', None, 'pcol'), may hold values from 0 to 1, as said below
Outputs:
- ancestor: float32 [4, 16, 32, 32768], P('prow', 'layer', None, 'pcol')
- lower: bfloat16 [16, 2048, 512], P('layer', 'prow')
- upper: bfloat16 [16, 256, 32768], P('layer', 'prow', 'pcol')
Inputs may be any that keep to these rules, and one draw needn't show every extreme that they name: `pivot_pattern`: each entry says whether that block of the pivot rows is structurally nonzero. `slab_pattern`: each entry says whether that block of the front rows is structurally nonzero.
All inputs are finite; a program needn't handle non-finite values.
Results may differ from a plain program's by a relative error of at most 0.014.
Values may be sent and summed in bfloat16 or wider, within the bound.
No kernel may reach another device: no remote copies, remote signals or barrier semaphores. Data moves between devices by JAX's collectives and lax.ppermute only.
A program may use at most 192 MiB of HBM per device.

v0:
```python
import jax
import jax.numpy as jnp
from jax import lax
from jax.sharding import PartitionSpec as P


def ring(value, axis, size, step):
    return lax.ppermute(value, axis, [(i, (i + step) % size) for i in range(size)])


def gather_relative(value, axis, size):
    from_prev = ring(value, axis, size, 1)
    from_next = ring(value, axis, size, -1)
    half = value.shape[1] // 2
    far_lo = ring(from_prev[:, :half], axis, size, 1)
    far_hi = ring(from_next[:, half:], axis, size, -1)
    far = jnp.concatenate([far_lo, far_hi], 1)
    return jnp.concatenate([value, from_next, far, from_prev], 1)


def grid_shift(value, axis, side, dy, dx):
    pairs = []
    for y in range(side):
        for x in range(side):
            pairs.append((y * side + x, ((y + dy) % side) * side + (x + dx) % side))
    return lax.ppermute(value, axis, pairs)


def ring_reduce(blocks, send):
    half = blocks.shape[1] // 2
    far = blocks[2].astype(jnp.bfloat16)
    fwd1 = send(far[:half], 1)
    bwd1 = send(far[half:], -1)
    next_block = blocks[1]
    prev_block = blocks[3]
    fwd2 = send(
        jnp.concatenate([next_block[:half] + fwd1.astype(jnp.float32), next_block[half:]], 0).astype(
            jnp.bfloat16
        ),
        1,
    )
    bwd2 = send(
        jnp.concatenate([prev_block[:half], prev_block[half:] + bwd1.astype(jnp.float32)], 0).astype(
            jnp.bfloat16
        ),
        -1,
    )
    return blocks[0] + fwd2.astype(jnp.float32) + bwd2.astype(jnp.float32)


def relative(value, own, axis):
    return jnp.stack(
        [lax.dynamic_index_in_dim(value, (own + j) % 4, axis, keepdims=False) for j in range(4)], 0
    )


def grid_reduce_scatter(schur, axis):
    side = 4
    index = lax.axis_index(axis)
    gy = index // side
    gx = index % side
    rows, width = schur.shape
    part = rows // (side * side)
    grid = schur.reshape(side, side, part, width)
    left = grid[..., : width // 2]
    right = grid[..., width // 2 :]

    def along_x(v, step):
        return grid_shift(v, axis, side, 0, step)

    def along_y(v, step):
        return grid_shift(v, axis, side, step, 0)

    left = ring_reduce(relative(left, gx, 1), along_x)
    left = ring_reduce(relative(left, gy, 0), along_y)
    right = ring_reduce(relative(right, gy, 0), along_y)
    right = ring_reduce(relative(right, gx, 0), along_x)
    return jnp.concatenate([left, right], 1)


def on_device(front, pivots, inverses, slab_pattern, pivot_pattern):
    block_size = inverses.shape[-1]
    panel_width = 2 * block_size
    row_count = front.shape[1]
    col_count = front.shape[2]
    own_rows = pivots.shape[2]
    masked = (
        front[0].reshape(row_count // block_size, block_size, col_count // block_size, block_size)
        * slab_pattern[0].astype(jnp.bfloat16)[:, None, :, None]
    ).reshape(row_count, col_count)
    pivot_masked = (
        pivots[0].reshape(2, own_rows, col_count // block_size, block_size)
        * pivot_pattern[0].astype(jnp.bfloat16)[:, None, :, None]
    ).reshape(2, own_rows, col_count)
    first_inverse = inverses[0, 0]
    second_inverse = inverses[0, 1]
    row_offset = lax.axis_index("prow") * own_rows
    pcol = lax.axis_index("pcol")
    n_prow = lax.axis_size("prow")
    n_pcol = lax.axis_size("pcol")
    assert n_prow == 4
    half = col_count // 2
    first_half = pivot_masked[:, :, :half]
    gathered = lax.all_gather(first_half, "prow", axis=1, tiled=True)
    second_half, gathered = lax.optimization_barrier((pivot_masked[:, :, half:], gathered))
    gathered_rel = gather_relative(second_half, "prow", n_prow)
    panel = jnp.roll(
        gather_relative(pivot_masked[:, :, :panel_width], "prow", n_prow), row_offset, axis=1
    )
    front_cols = masked[:, :panel_width]
    pivot_cols = panel[0]
    second_cols = panel[1]
    lower_pivot = jnp.dot(
        second_cols[:, :block_size], first_inverse, preferred_element_type=jnp.float32
    ).astype(jnp.bfloat16)
    lower_first = jnp.dot(
        front_cols[:, :block_size], first_inverse, preferred_element_type=jnp.float32
    ).astype(jnp.bfloat16)
    carried = (
        front_cols[:, block_size:].astype(jnp.float32)
        - jnp.dot(
            lower_first, pivot_cols[:, block_size:panel_width], preferred_element_type=jnp.float32
        )
    ).astype(jnp.bfloat16)
    lower_second = jnp.dot(carried, second_inverse, preferred_element_type=jnp.float32).astype(
        jnp.bfloat16
    )
    lower_panel = jnp.concatenate([lower_first, lower_second], 1)
    sent = lax.ppermute((lower_panel, lower_pivot), "pcol", [(0, i) for i in range(1, n_pcol)])
    on_root = pcol == 0
    lower_panel = jnp.where(on_root, lower_panel, sent[0])
    lower_pivot = jnp.where(on_root, lower_pivot, sent[1])
    own_pivot = lax.dynamic_slice_in_dim(lower_pivot, row_offset, own_rows, 0)
    upper_own = jnp.concatenate(
        [
            jnp.dot(own_pivot, gathered[0], preferred_element_type=jnp.float32),
            jnp.dot(
                jnp.roll(own_pivot, -row_offset, axis=1),
                gathered_rel[0],
                preferred_element_type=jnp.float32,
            ),
        ],
        1,
    )
    upper_own = (pivot_masked[1].astype(jnp.float32) - upper_own).astype(jnp.bfloat16)
    folded = (
        lower_panel[:, :block_size].astype(jnp.float32)
        - jnp.dot(lower_panel[:, block_size:], lower_pivot, preferred_element_type=jnp.float32)
    ).astype(jnp.bfloat16)
    multipliers = jnp.concatenate([folded, lower_panel[:, block_size:]], 1)
    multipliers_rel = jnp.concatenate(
        [
            jnp.roll(folded, -row_offset, axis=1),
            jnp.roll(lower_panel[:, block_size:], -row_offset, axis=1),
        ],
        1,
    )
    col_index = pcol * col_count + jnp.arange(col_count, dtype=jnp.int32)
    retained = col_index >= panel_width
    schur_first = masked[:, :half].astype(jnp.float32) - jnp.dot(
        multipliers, gathered.reshape(2 * block_size, half), preferred_element_type=jnp.float32
    )
    schur_first = jnp.where(retained[None, :half], schur_first, jnp.zeros_like(schur_first))
    summed_first = lax.psum_scatter(
        schur_first.astype(jnp.bfloat16), "layer", scatter_dimension=0, tiled=True
    ).astype(jnp.float32)
    schur_second = masked[:, half:].astype(jnp.float32) - jnp.dot(
        multipliers_rel,
        gathered_rel.reshape(2 * block_size, half),
        preferred_element_type=jnp.float32,
    )
    schur_second = jnp.where(retained[None, half:], schur_second, jnp.zeros_like(schur_second))
    summed = jnp.concatenate([summed_first, grid_reduce_scatter(schur_second, "layer")], 1)
    ancestor = summed.reshape(1, 1, summed.shape[0], col_count)
    return (ancestor, lower_panel[None], upper_own[None])


def solution(mesh):
    placed = (
        P("layer", "prow", "pcol"),
        P("layer", None, "prow", "pcol"),
        P("layer", None, None, None),
        P("layer", "prow", "pcol"),
        P("layer", None, "pcol"),
    )
    return jax.shard_map(
        on_device,
        mesh=mesh,
        in_specs=placed,
        out_specs=(
            P("prow", "layer", None, "pcol"),
            P("layer", "prow", None),
            P("layer", "prow", "pcol"),
        ),
        check_vma=False,
    )
```

profile of v0, /device:TPU:0, one launch (start us, length us, event | category | flops | bytes accessed | tf_op | source)
XLA Modules:
  0.0 292.0 jit_solution(1202727709748885770)
XLA Ops:
  7.2 0.7 convert_bitcast_fusion
  8.1 2.7 bitcast_multiply_fusion.1
  10.8 2.0 copy-done.2
  12.8 2.4 fusion.62
  15.3 0.9 fusion.61
  16.2 4.2 %collective-permute-start = (bf16[2,64,512]{2,1,0:T(8,128)(2,1)S(1)}, bf16[2,64,512]{2,1,0:T(8,128)(2,1)S(1)}, u32[]{:S(2)}, u32[]{:S(2)}) collective-permute-start(bf16[2,64,512]{2,1,0:T(8,128)(2,1)S(1)} %get-tuple-element.19), channel_id=1, source_target_pairs={{0,6},{2,0},{4,2},{6,4},{1,7},{3,1},{5,3},{7,5},{8,14},{10,8},{12,... | collective-permute-start | bytes 393224 | tf_op jit(solution)/shard_map/ppermute | solution.py:8
  20.4 3.4 %copy.16 = bf16[16,8,64,256]{3,2,1,0:T(8,128)(2,1)S(1)} copy(bf16[16,8,64,256]{3,1,2,0:T(8,128)(2,1)} %bitcast.160) | data formatting | bytes 8388608
  23.8 2.3 fusion.3
  26.2 5.3 %reshape.124 = f32[1,64,16384]{2,1,0:T(8,128)} reshape(f32[1,64,64,256]{3,2,1,0:T(8,128)} %fusion.3) | data formatting | bytes 8388608 | tf_op jit(solution)/shard_map/convert_element_type | solution.py:145
  31.5 2.7 mul.35
  34.3 12.5 %copy.14 = bf16[64,8,64,256]{3,1,2,0:T(8,128)(2,1)} copy(bf16[64,8,64,256]{3,2,1,0:T(8,128)(2,1)S(1)} %bitcast.158) | data formatting | bytes 33554432
  46.7 11.9 %bitcast_multiply_fusion = bf16[512,16384]{1,0:T(8,128)(2,1)S(1)} fusion(bf16[512,16384]{1,0:T(8,128)(2,1)} %bitcast.156, bf16[1,512,16384]{2,1,0:T(8,128)(2,1)} %param.7), kind=kLoop, calls=%fused_computation | loop fusion | flops 8388608 | bytes 50331648 | tf_op jit(solution)/shard_map/mul | solution.py:88
  58.7 5.8 %copy-done = bf16[512,16384]{1,0:T(8,128)(2,1)} copy-done((bf16[512,16384]{1,0:T(8,128)(2,1)}, bf16[512,16384]{1,0:T(8,128)(2,1)S(1)}, u32[]{:S(2)}) %copy-start) | copy-done | bytes 16777240
  64.9 3.3 %collective-permute-start.3 = (bf16[2,32,512]{2,1,0:T(8,128)(2,1)S(1)}, bf16[2,32,512]{2,1,0:T(8,128)(2,1)S(1)}, u32[]{:S(2)}, u32[]{:S(2)}) collective-permute-start(bf16[2,32,512]{2,1,0:T(8,128)(2,1)S(1)} %slice.316), channel_id=1, source_target_pairs={{0,6},{2,0},{4,2},{6,4},{1,7},{3,1},{5,3},{7,5},{8,14},{10,8},{12,... | collective-permute-start | bytes 196616 | tf_op jit(solution)/shard_map/ppermute | solution.py:8
  68.2 3.8 %collective-permute-done.2 = bf16[2,32,512]{2,1,0:T(8,128)(2,1)S(1)} collective-permute-done((bf16[2,32,512]{2,1,0:T(8,128)(2,1)S(1)}, bf16[2,32,512]{2,1,0:T(8,128)(2,1)S(1)}, u32[]{:S(2)}, u32[]{:S(2)}) %collective-permute-start.2) | collective-permute-done | bytes 65568 | tf_op jit(solution)/shard_map/ppermute | solution.py:8
  72.0 0.9 constant_dynamic-update-slice_fusion.4
  73.2 1.3 collective-permute-start.5
  74.5 1.4 convolution_convert_fusion
  76.0 1.3 collective-permute-start.4
  77.4 0.6 constant_dynamic-slice_fusion
  78.0 0.8 collective-permute-done.4
  79.0 1.0 copy.11
  80.7 21.9 %all-gather.2.cloned.1.call-done = bf16[2,256,8192]{2,1,0:T(8,128)(2,1)} async-done(((bf16[2,64,8192]{2,1,0:T(8,128)(2,1)}), bf16[2,256,8192]{2,1,0:T(8,128)(2,1)}) %all-gather.2.cloned.1.call-update) | async-done | bytes 8388624 | tf_op jit(solution)/shard_map/all_gather | solution.py:104
  102.6 1.3 collective-permute-start.6
  103.9 0.7 collective-permute-start.7
  104.6 3.1 %constant_dynamic-update-slice_fusion.14 = bf16[2,256,8192]{2,1,0:T(8,128)(2,1)} fusion(bf16[2,64,8192]{2,1,0:T(8,128)(2,1)} %get-tuple-element.7), kind=kLoop, calls=%fused_computation.134 | loop fusion | bytes 4194304
  107.7 12.2 %select_convert_fusion = bf16[512,8192]{1,0:T(8,128)(2,1)} fusion(bf16[512,8192]{1,0:T(8,128)(2,1)} %bitcast.163, bf16[512,16384]{1,0:T(8,128)(2,1)} %copy-done, pred[8192]{0:T(1024)(128)(4,1)S(1)} %get-tuple-element.41, bf16[512,256]{0,1:T(8,128)(2,1)S(1)} %slice.319, bf16[512,256]{0,1:T(8,128)(2,1)S(1)} %subtract_convert_fusion), kind=kOutput, calls=%fused_computation.2 | convolution fusion | flops 4312793088 | bytes 25698304 | tf_op jit(solution)/shard_map/dot_general | solution.py:160
  119.9 32.4 %collective-permute-done.7 = bf16[2,64,8192]{2,1,0:T(8,128)(2,1)S(1)} collective-permute-done((bf16[2,64,8192]{2,1,0:T(8,128)(2,1)}, bf16[2,64,8192]{2,1,0:T(8,128)(2,1)S(1)}, u32[]{:S(2)}, u32[]{:S(2)}) %collective-permute-start.7) | collective-permute-done | bytes 2097184 | tf_op jit(solution)/shard_map/ppermute | solution.py:8
  152.3 1.1 slice.325
  153.9 3.0 %convolution_bitcast_fusion.1 = f32[1,64,8192]{2,1,0:T(8,128)S(1)} fusion(bf16[64,256]{1,0:T(8,128)(2,1)} %constant_dynamic-slice_fusion, bf16[2,256,8192]{2,1,0:T(8,128)(2,1)} %all-gather.2.cloned.1.call-done), kind=kOutput, calls=%fused_computation.4 | convolution fusion | flops 268435456 | bytes 6324224 | tf_op jit(solution)/shard_map/dot_general | solution.py:136
  157.0 1.3 slice.326
  158.3 3.3 %collective-permute-start.9 = (bf16[2,32,8192]{2,1,0:T(8,128)(2,1)S(1)}, bf16[2,32,8192]{2,1,0:T(8,128)(2,1)S(1)}, u32[]{:S(2)}, u32[]{:S(2)}) collective-permute-start(bf16[2,32,8192]{2,1,0:T(8,128)(2,1)S(1)} %slice.326), channel_id=1, source_target_pairs={{0,6},{2,0},{4,2},{6,4},{1,7},{3,1},{5,3},{7,5},{8,14},{10,8},{12,... | collective-permute-start | bytes 3145736 | tf_op jit(solution)/shard_map/ppermute | solution.py:8
  161.6 3.1 %constant_dynamic-update-slice_fusion.13 = bf16[2,256,8192]{2,1,0:T(8,128)(2,1)} fusion(bf16[2,256,8192]{2,1,0:T(8,128)(2,1)} %constant_dynamic-update-slice_fusion.14, bf16[2,64,8192]{2,1,0:T(8,128)(2,1)} %collective-permute-done.6), kind=kLoop, calls=%fused_computation.133 | loop fusion | bytes 4194304
  164.7 14.3 %collective-permute-done.8 = bf16[2,32,8192]{2,1,0:T(8,128)(2,1)} collective-permute-done((bf16[2,32,8192]{2,1,0:T(8,128)(2,1)}, bf16[2,32,8192]{2,1,0:T(8,128)(2,1)}, u32[]{:S(2)}, u32[]{:S(2)}) %collective-permute-start.8) | collective-permute-done | bytes 1048608 | tf_op jit(solution)/shard_map/ppermute | solution.py:8
  179.0 2.3 constant_dynamic-update-slice_fusion.12
  181.3 1.2 collective-permute-done.9
  182.4 1.0 constant_dynamic-update-slice_fusion.11
  183.5 1.5 constant_dynamic-update-slice_fusion.10
  185.0 4.4 %convolution_bitcast_fusion = f32[1,64,8192]{2,1,0:T(8,128)} fusion(bf16[2,256,8192]{2,1,0:T(8,128)(2,1)} %constant_dynamic-update-slice_fusion.10, s32[]{:T(128)S(6)} %select_n.181, bf16[64,256]{1,0:T(8,128)(2,1)S(1)} %copy-done.7), kind=kOutput, calls=%fused_computation.3 | convolution fusion | flops 268500992 | bytes 6324228 | tf_op jit(solution)/shard_map/dot_general | solution.py:137
  189.4 10.5 %subtract_select_fusion = f32[512,8192]{1,0:T(8,128)S(1)} fusion(bf16[512,8192]{1,0:T(8,128)(2,1)} %bitcast.159, bf16[512,16384]{1,0:T(8,128)(2,1)} %copy-done, pred[8192]{0:T(1024)(128)(4,1)S(1)} %get-tuple-element.42, bf16[512,256]{0,1:T(8,128)(2,1)S(1)} %get-tuple-element.43, bf16[512,256]{0,1:T(8,128)(2,1)S(1)} %get-tuple-element.44), kind=kOutput, calls=%fused_computation.1 | convolution fusion | flops 4308598784 | bytes 34086912 | tf_op jit(solution)/shard_map/dot_general | solution.py:167
  199.9 6.4 %fusion.60 = (f32[4,4,32,4096]{3,2,1,0:T(8,128)}, f32[4,4,32,4096]{3,2,1,0:T(8,128)}) fusion(f32[4,4,32,8192]{3,2,1,0:T(8,128)S(1)} %bitcast.157), kind=kLoop, calls=%fused_computation.145 | loop fusion | bytes 33554432 | tf_op jit(solution)/shard_map/slice | solution.py:65
  206.3 2.8 dynamic-slice_bitcast_fusion
  209.2 2.4 collective-permute-start.10
  211.6 2.5 dynamic-slice_bitcast_fusion.1
  214.2 1.6 collective-permute-start.12
  216.0 2.0 collective-permute-start.18
  218.0 1.4 collective-permute-start.20
  219.4 1.8 fusion
  221.4 5.6 %collective-permute-done.10 = bf16[2,32,4096]{2,1,0:T(8,128)(2,1)S(1)} collective-permute-done((bf16[2,32,4096]{2,1,0:T(8,128)(2,1)S(1)}, bf16[2,32,4096]{2,1,0:T(8,128)(2,1)S(1)}, u32[]{:S(2)}, u32[]{:S(2)}) %collective-permute-start.10) | collective-permute-done | bytes 524320 | tf_op jit(solution)/shard_map/ppermute | solution.py:26
  227.5 1.3 fusion.12
  228.9 3.3 %collective-permute-start.13 = (bf16[4,32,4096]{2,1,0:T(8,128)(2,1)S(1)}, bf16[4,32,4096]{2,1,0:T(8,128)(2,1)S(1)}, u32[]{:S(2)}, u32[]{:S(2)}) collective-permute-start(bf16[4,32,4096]{2,1,0:T(8,128)(2,1)S(1)} %pad_maximum_fusion.1), channel_id=1, source_target_pairs={{0,24},{8,0},{16,8},{24,16},{32,56},{40,32},{48,40},{56,48},{64,88... | collective-permute-start | bytes 3145736 | tf_op jit(solution)/shard_map/ppermute | solution.py:26
  232.5 0.7 collective-permute-start.19
  233.3 2.6 collective-permute-start.21
  236.0 25.1 %collective-permute-done.11 = bf16[4,32,4096]{2,1,0:T(8,128)(2,1)S(1)} collective-permute-done((bf16[4,32,4096]{2,1,0:T(8,128)(2,1)S(1)}, bf16[4,32,4096]{2,1,0:T(8,128)(2,1)S(1)}, u32[]{:S(2)}, u32[]{:S(2)}) %collective-permute-start.11) | collective-permute-done | bytes 1048608 | tf_op jit(solution)/shard_map/ppermute | solution.py:26
  261.5 1.9 fusion.5
  263.7 3.1 %collective-permute-start.16 = (bf16[16,4096]{1,0:T(8,128)(2,1)S(1)}, bf16[16,4096]{1,0:T(8,128)(2,1)S(1)}, u32[]{:S(2)}, u32[]{:S(2)}) collective-permute-start(bf16[16,4096]{1,0:T(8,128)(2,1)S(1)} %get-tuple-element.38), channel_id=1, source_target_pairs={{0,96},{8,104},{16,112},{24,120},{32,0},{40,8},{48,16},{56,24},{64... | collective-permute-start | bytes 393224 | tf_op jit(solution)/shard_map/ppermute | solution.py:26
  267.5 3.7 %collective-permute-start.24 = (bf16[16,4096]{1,0:T(8,128)(2,1)S(1)}, bf16[16,4096]{1,0:T(8,128)(2,1)S(1)}, u32[]{:S(2)}, u32[]{:S(2)}) collective-permute-start(bf16[16,4096]{1,0:T(8,128)(2,1)S(1)} %get-tuple-element.40), channel_id=1, source_target_pairs={{0,24},{8,0},{16,8},{24,16},{32,56},{40,32},{48,40},{56,48},{64,88... | collective-permute-start | bytes 393224 | tf_op jit(solution)/shard_map/ppermute | solution.py:26
  271.4 3.3 %collective-permute-start.17 = (bf16[32,4096]{1,0:T(8,128)(2,1)S(1)}, bf16[32,4096]{1,0:T(8,128)(2,1)S(1)}, u32[]{:S(2)}, u32[]{:S(2)}) collective-permute-start(bf16[32,4096]{1,0:T(8,128)(2,1)S(1)} %pad_maximum_fusion.8), channel_id=1, source_target_pairs={{0,96},{8,104},{16,112},{24,120},{32,0},{40,8},{48,16},{56,24},{64... | collective-permute-start | bytes 786440 | tf_op jit(solution)/shard_map/ppermute | solution.py:26
  274.8 0.8 collective-permute-start.23
  275.6 2.5 collective-permute-start.25
  278.2 1.0 collective-permute-done.15
  279.3 3.1 %collective-permute-done.23 = bf16[32,4096]{1,0:T(8,128)(2,1)S(1)} collective-permute-done((bf16[32,4096]{1,0:T(8,128)(2,1)S(1)}, bf16[32,4096]{1,0:T(8,128)(2,1)S(1)}, u32[]{:S(2)}, u32[]{:S(2)}) %collective-permute-start.23) | collective-permute-done | bytes 262176 | tf_op jit(solution)/shard_map/ppermute | solution.py:26
  282.5 1.1 convert_element_type.161
  283.7 1.5 maximum_bitcast_fusion
  (99 shorter events, 5.9 us)
Async XLA Ops:
  7.2 95.4 %all-gather.2.cloned.1.call-start = ((), (), s32[]{:S(2)}) async-start(), calls=%async_computation.1 | async-start | bytes 10485760 | tf_op jit(solution)/shard_map/all_gather | solution.py:104
  10.8 2.0 copy-start.2
  15.2 267.3 %reduce-scatter.2.cloned.1.call-start = ((), (), s32[]{:S(2)}) async-start(), calls=%async_computation.2 | async-start | bytes 8912896 | tf_op jit(solution)/shard_map/reduce_scatter | solution.py:164
  16.2 48.6 %collective-permute-start = (bf16[2,64,512]{2,1,0:T(8,128)(2,1)S(1)}, bf16[2,64,512]{2,1,0:T(8,128)(2,1)S(1)}, u32[]{:S(2)}, u32[]{:S(2)}) collective-permute-start(bf16[2,64,512]{2,1,0:T(8,128)(2,1)S(1)} %get-tuple-element.19), channel_id=1, source_target_pairs={{0,6},{2,0},{4,2},{6,4},{1,7},{3,1},{5,3},{7,5},{8,14},{10,8},{12,... | collective-permute-start | bytes 393224 | tf_op jit(solution)/shard_map/ppermute | solution.py:8
  20.4 44.3 %collective-permute-start.1 = (bf16[2,64,512]{2,1,0:T(8,128)(2,1)S(1)}, bf16[2,64,512]{2,1,0:T(8,128)(2,1)S(1)}, u32[]{:S(2)}, u32[]{:S(2)}) collective-permute-start(bf16[2,64,512]{2,1,0:T(8,128)(2,1)S(1)} %get-tuple-element.19), channel_id=1, source_target_pairs={{0,2},{2,4},{4,6},{6,0},{1,3},{3,5},{5,7},{7,1},{8,10},{10,12},{12... | collective-permute-start | bytes 393224 | tf_op jit(solution)/shard_map/ppermute | solution.py:8
  26.2 5.3 %copy-start.9 = (s32[1,2,64]{2,1,0:T(2,128)S(1)}, s32[1,2,64]{2,1,0:T(2,128)}, u32[]{:S(2)}) copy-start(s32[1,2,64]{2,1,0:T(2,128)} %param.10) | copy-start | bytes 1540
  46.7 17.7 %copy-start.8 = (bf16[1,2,256,256]{3,2,1,0:T(8,128)(2,1)S(1)}, bf16[1,2,256,256]{3,2,1,0:T(8,128)(2,1)}, u32[]{:S(2)}) copy-start(bf16[1,2,256,256]{3,2,1,0:T(8,128)(2,1)} %param.9) | copy-start | bytes 786436
  58.6 5.8 %copy-start = (bf16[512,16384]{1,0:T(8,128)(2,1)}, bf16[512,16384]{1,0:T(8,128)(2,1)S(1)}, u32[]{:S(2)}) copy-start(bf16[512,16384]{1,0:T(8,128)(2,1)S(1)} %bitcast_multiply_fusion) | copy-start | bytes 50331652
  64.8 7.2 %collective-permute-start.2 = (bf16[2,32,512]{2,1,0:T(8,128)(2,1)S(1)}, bf16[2,32,512]{2,1,0:T(8,128)(2,1)S(1)}, u32[]{:S(2)}, u32[]{:S(2)}) collective-permute-start(bf16[2,32,512]{2,1,0:T(8,128)(2,1)S(1)} %slice.315), channel_id=1, source_target_pairs={{0,2},{2,4},{4,6},{6,0},{1,3},{3,5},{5,7},{7,1},{8,10},{10,12},{12... | collective-permute-start | bytes 196616 | tf_op jit(solution)/shard_map/ppermute | solution.py:8
  64.9 7.1 %collective-permute-start.3 = (bf16[2,32,512]{2,1,0:T(8,128)(2,1)S(1)}, bf16[2,32,512]{2,1,0:T(8,128)(2,1)S(1)}, u32[]{:S(2)}, u32[]{:S(2)}) collective-permute-start(bf16[2,32,512]{2,1,0:T(8,128)(2,1)S(1)} %slice.316), channel_id=1, source_target_pairs={{0,6},{2,0},{4,2},{6,4},{1,7},{3,1},{5,3},{7,5},{8,14},{10,8},{12,... | collective-permute-start | bytes 196616 | tf_op jit(solution)/shard_map/ppermute | solution.py:8
  73.2 4.1 %collective-permute-start.5 = (bf16[256,256]{1,0:T(8,128)(2,1)S(1)}, bf16[256,256]{1,0:T(8,128)(2,1)S(1)}, u32[]{:S(2)}, u32[]{:S(2)}) collective-permute-start(bf16[256,256]{1,0:T(8,128)(2,1)S(1)} %convolution_convert_fusion.2), channel_id=1, source_target_pairs={{0,1},{2,3},{4,5},{6,7},{8,9},{10,11},{12,13},{14,15},{16,17},{18,... | collective-permute-start | bytes 393224 | tf_op jit(solution)/shard_map/ppermute | solution.py:129
  76.0 2.8 collective-permute-start.4
  102.6 54.4 %collective-permute-start.6 = (bf16[2,64,8192]{2,1,0:T(8,128)(2,1)}, bf16[2,64,8192]{2,1,0:T(8,128)(2,1)}, u32[]{:S(2)}, u32[]{:S(2)}) collective-permute-start(bf16[2,64,8192]{2,1,0:T(8,128)(2,1)} %get-tuple-element.7), channel_id=1, source_target_pairs={{0,6},{2,0},{4,2},{6,4},{1,7},{3,1},{5,3},{7,5},{8,14},{10,8},{12,... | collective-permute-start | bytes 6291464 | tf_op jit(solution)/shard_map/ppermute | solution.py:8
  103.9 48.4 %collective-permute-start.7 = (bf16[2,64,8192]{2,1,0:T(8,128)(2,1)}, bf16[2,64,8192]{2,1,0:T(8,128)(2,1)S(1)}, u32[]{:S(2)}, u32[]{:S(2)}) collective-permute-start(bf16[2,64,8192]{2,1,0:T(8,128)(2,1)} %get-tuple-element.7), channel_id=1, source_target_pairs={{0,2},{2,4},{4,6},{6,0},{1,3},{3,5},{5,7},{7,1},{8,10},{10,12},{12... | collective-permute-start | bytes 6291464 | tf_op jit(solution)/shard_map/ppermute | solution.py:8
  152.2 1.7 copy-start.5
  153.9 25.1 %collective-permute-start.8 = (bf16[2,32,8192]{2,1,0:T(8,128)(2,1)}, bf16[2,32,8192]{2,1,0:T(8,128)(2,1)}, u32[]{:S(2)}, u32[]{:S(2)}) collective-permute-start(bf16[2,32,8192]{2,1,0:T(8,128)(2,1)} %slice.325), channel_id=1, source_target_pairs={{0,2},{2,4},{4,6},{6,0},{1,3},{3,5},{5,7},{7,1},{8,10},{10,12},{12... | collective-permute-start | bytes 3145736 | tf_op jit(solution)/shard_map/ppermute | solution.py:8
  158.3 25.1 %copy-start.6 = (bf16[2,64,8192]{2,1,0:T(8,128)(2,1)S(1)}, bf16[2,64,8192]{2,1,0:T(8,128)(2,1)}, u32[]{:S(2)}) copy-start(bf16[2,64,8192]{2,1,0:T(8,128)(2,1)} %copy-done.5) | copy-start | bytes 6291460
  158.3 24.1 %collective-permute-start.9 = (bf16[2,32,8192]{2,1,0:T(8,128)(2,1)S(1)}, bf16[2,32,8192]{2,1,0:T(8,128)(2,1)S(1)}, u32[]{:S(2)}, u32[]{:S(2)}) collective-permute-start(bf16[2,32,8192]{2,1,0:T(8,128)(2,1)S(1)} %slice.326), channel_id=1, source_target_pairs={{0,6},{2,0},{4,2},{6,4},{1,7},{3,1},{5,3},{7,5},{8,14},{10,8},{12,... | collective-permute-start | bytes 3145736 | tf_op jit(solution)/shard_map/ppermute | solution.py:8
  164.7 20.2 %copy-start.7 = (bf16[64,256]{1,0:T(8,128)(2,1)S(1)}, bf16[64,256]{1,0:T(8,128)(2,1)}, u32[]{:S(2)}) copy-start(bf16[64,256]{1,0:T(8,128)(2,1)} %constant_dynamic-slice_fusion) | copy-start | bytes 98308
  206.3 9.5 %copy-start.1 = (f32[4,4,32,4096]{3,2,1,0:T(8,128)S(1)}, f32[4,4,32,4096]{3,2,1,0:T(8,128)}, u32[]{:S(2)}) copy-start(f32[4,4,32,4096]{3,2,1,0:T(8,128)} %get-tuple-element.12) | copy-start | bytes 25165828
  209.2 10.2 %copy-start.3 = (f32[1,64,16384]{2,1,0:T(8,128)S(1)}, f32[1,64,16384]{2,1,0:T(8,128)}, u32[]{:S(2)}) copy-start(f32[1,64,16384]{2,1,0:T(8,128)} %reshape.124) | copy-start | bytes 12582916
  209.2 10.2 %copy-start.4 = (f32[1,64,8192]{2,1,0:T(8,128)S(1)}, f32[1,64,8192]{2,1,0:T(8,128)}, u32[]{:S(2)}) copy-start(f32[1,64,8192]{2,1,0:T(8,128)} %convolution_bitcast_fusion) | copy-start | bytes 6291460
  209.2 17.7 %collective-permute-start.10 = (bf16[2,32,4096]{2,1,0:T(8,128)(2,1)S(1)}, bf16[2,32,4096]{2,1,0:T(8,128)(2,1)S(1)}, u32[]{:S(2)}, u32[]{:S(2)}) collective-permute-start(bf16[2,32,4096]{2,1,0:T(8,128)(2,1)S(1)} %get-tuple-element.31), channel_id=1, source_target_pairs={{0,8},{8,16},{16,24},{24,0},{32,40},{40,48},{48,56},{56,32},{64,72... | collective-permute-start | bytes 1572872 | tf_op jit(solution)/shard_map/ppermute | solution.py:26
  214.2 13.3 %collective-permute-start.12 = (bf16[2,32,4096]{2,1,0:T(8,128)(2,1)S(1)}, bf16[2,32,4096]{2,1,0:T(8,128)(2,1)S(1)}, u32[]{:S(2)}, u32[]{:S(2)}) collective-permute-start(bf16[2,32,4096]{2,1,0:T(8,128)(2,1)S(1)} %get-tuple-element.32), channel_id=1, source_target_pairs={{0,24},{8,0},{16,8},{24,16},{32,56},{40,32},{48,40},{56,48},{64,88... | collective-permute-start | bytes 1572872 | tf_op jit(solution)/shard_map/ppermute | solution.py:26
  216.0 16.2 %collective-permute-start.18 = (bf16[2,32,4096]{2,1,0:T(8,128)(2,1)S(1)}, bf16[2,32,4096]{2,1,0:T(8,128)(2,1)S(1)}, u32[]{:S(2)}, u32[]{:S(2)}) collective-permute-start(bf16[2,32,4096]{2,1,0:T(8,128)(2,1)S(1)} %get-tuple-element.33), channel_id=1, source_target_pairs={{0,32},{8,40},{16,48},{24,56},{32,64},{40,72},{48,80},{56,88},{64,... | collective-permute-start | bytes 1572872 | tf_op jit(solution)/shard_map/ppermute | solution.py:26
  218.0 14.2 %collective-permute-start.20 = (bf16[2,32,4096]{2,1,0:T(8,128)(2,1)S(1)}, bf16[2,32,4096]{2,1,0:T(8,128)(2,1)S(1)}, u32[]{:S(2)}, u32[]{:S(2)}) collective-permute-start(bf16[2,32,4096]{2,1,0:T(8,128)(2,1)S(1)} %get-tuple-element.34), channel_id=1, source_target_pairs={{0,96},{8,104},{16,112},{24,120},{32,0},{40,8},{48,16},{56,24},{64... | collective-permute-start | bytes 1572872 | tf_op jit(solution)/shard_map/ppermute | solution.py:26
  227.1 33.9 %collective-permute-start.11 = (bf16[4,32,4096]{2,1,0:T(8,128)(2,1)S(1)}, bf16[4,32,4096]{2,1,0:T(8,128)(2,1)S(1)}, u32[]{:S(2)}, u32[]{:S(2)}) collective-permute-start(bf16[4,32,4096]{2,1,0:T(8,128)(2,1)S(1)} %pad_maximum_fusion), channel_id=1, source_target_pairs={{0,8},{8,16},{16,24},{24,0},{32,40},{40,48},{48,56},{56,32},{64,72... | collective-permute-start | bytes 3145736 | tf_op jit(solution)/shard_map/ppermute | solution.py:26
  228.9 32.6 %collective-permute-start.13 = (bf16[4,32,4096]{2,1,0:T(8,128)(2,1)S(1)}, bf16[4,32,4096]{2,1,0:T(8,128)(2,1)S(1)}, u32[]{:S(2)}, u32[]{:S(2)}) collective-permute-start(bf16[4,32,4096]{2,1,0:T(8,128)(2,1)S(1)} %pad_maximum_fusion.1), channel_id=1, source_target_pairs={{0,24},{8,0},{16,8},{24,16},{32,56},{40,32},{48,40},{56,48},{64,88... | collective-permute-start | bytes 3145736 | tf_op jit(solution)/shard_map/ppermute | solution.py:26
  232.5 34.3 %collective-permute-start.19 = (bf16[4,32,4096]{2,1,0:T(8,128)(2,1)S(1)}, bf16[4,32,4096]{2,1,0:T(8,128)(2,1)S(1)}, u32[]{:S(2)}, u32[]{:S(2)}) collective-permute-start(bf16[4,32,4096]{2,1,0:T(8,128)(2,1)S(1)} %pad_maximum_fusion.2), channel_id=1, source_target_pairs={{0,32},{8,40},{16,48},{24,56},{32,64},{40,72},{48,80},{56,88},{64,... | collective-permute-start | bytes 3145736 | tf_op jit(solution)/shard_map/ppermute | solution.py:26
  233.3 33.5 %collective-permute-start.21 = (bf16[4,32,4096]{2,1,0:T(8,128)(2,1)S(1)}, bf16[4,32,4096]{2,1,0:T(8,128)(2,1)S(1)}, u32[]{:S(2)}, u32[]{:S(2)}) collective-permute-start(bf16[4,32,4096]{2,1,0:T(8,128)(2,1)S(1)} %pad_maximum_fusion.3), channel_id=1, source_target_pairs={{0,96},{8,104},{16,112},{24,120},{32,0},{40,8},{48,16},{56,24},{64... | collective-permute-start | bytes 3145736 | tf_op jit(solution)/shard_map/ppermute | solution.py:26
  263.5 7.7 %collective-permute-start.14 = (bf16[16,4096]{1,0:T(8,128)(2,1)S(1)}, bf16[16,4096]{1,0:T(8,128)(2,1)S(1)}, u32[]{:S(2)}, u32[]{:S(2)}) collective-permute-start(bf16[16,4096]{1,0:T(8,128)(2,1)S(1)} %get-tuple-element.37), channel_id=1, source_target_pairs={{0,32},{8,40},{16,48},{24,56},{32,64},{40,72},{48,80},{56,88},{64,... | collective-permute-start | bytes 393224 | tf_op jit(solution)/shard_map/ppermute | solution.py:26
  263.7 7.5 %collective-permute-start.16 = (bf16[16,4096]{1,0:T(8,128)(2,1)S(1)}, bf16[16,4096]{1,0:T(8,128)(2,1)S(1)}, u32[]{:S(2)}, u32[]{:S(2)}) collective-permute-start(bf16[16,4096]{1,0:T(8,128)(2,1)S(1)} %get-tuple-element.38), channel_id=1, source_target_pairs={{0,96},{8,104},{16,112},{24,120},{32,0},{40,8},{48,16},{56,24},{64... | collective-permute-start | bytes 393224 | tf_op jit(solution)/shard_map/ppermute | solution.py:26
  267.3 7.3 %collective-permute-start.22 = (bf16[16,4096]{1,0:T(8,128)(2,1)S(1)}, bf16[16,4096]{1,0:T(8,128)(2,1)S(1)}, u32[]{:S(2)}, u32[]{:S(2)}) collective-permute-start(bf16[16,4096]{1,0:T(8,128)(2,1)S(1)} %get-tuple-element.39), channel_id=1, source_target_pairs={{0,8},{8,16},{16,24},{24,0},{32,40},{40,48},{48,56},{56,32},{64,72... | collective-permute-start | bytes 393224 | tf_op jit(solution)/shard_map/ppermute | solution.py:26
  267.5 7.2 %collective-permute-start.24 = (bf16[16,4096]{1,0:T(8,128)(2,1)S(1)}, bf16[16,4096]{1,0:T(8,128)(2,1)S(1)}, u32[]{:S(2)}, u32[]{:S(2)}) collective-permute-start(bf16[16,4096]{1,0:T(8,128)(2,1)S(1)} %get-tuple-element.40), channel_id=1, source_target_pairs={{0,24},{8,0},{16,8},{24,16},{32,56},{40,32},{48,40},{56,48},{64,88... | collective-permute-start | bytes 393224 | tf_op jit(solution)/shard_map/ppermute | solution.py:26
  271.3 7.9 %collective-permute-start.15 = (bf16[32,4096]{1,0:T(8,128)(2,1)S(1)}, bf16[32,4096]{1,0:T(8,128)(2,1)S(1)}, u32[]{:S(2)}, u32[]{:S(2)}) collective-permute-start(bf16[32,4096]{1,0:T(8,128)(2,1)S(1)} %pad_maximum_fusion.7), channel_id=1, source_target_pairs={{0,32},{8,40},{16,48},{24,56},{32,64},{40,72},{48,80},{56,88},{64,... | collective-permute-start | bytes 786440 | tf_op jit(solution)/shard_map/ppermute | solution.py:26
  271.4 7.8 %collective-permute-start.17 = (bf16[32,4096]{1,0:T(8,128)(2,1)S(1)}, bf16[32,4096]{1,0:T(8,128)(2,1)S(1)}, u32[]{:S(2)}, u32[]{:S(2)}) collective-permute-start(bf16[32,4096]{1,0:T(8,128)(2,1)S(1)} %pad_maximum_fusion.8), channel_id=1, source_target_pairs={{0,96},{8,104},{16,112},{24,120},{32,0},{40,8},{48,16},{56,24},{64... | collective-permute-start | bytes 786440 | tf_op jit(solution)/shard_map/ppermute | solution.py:26
  274.8 7.7 %collective-permute-start.23 = (bf16[32,4096]{1,0:T(8,128)(2,1)S(1)}, bf16[32,4096]{1,0:T(8,128)(2,1)S(1)}, u32[]{:S(2)}, u32[]{:S(2)}) collective-permute-start(bf16[32,4096]{1,0:T(8,128)(2,1)S(1)} %pad_maximum_fusion.9), channel_id=1, source_target_pairs={{0,8},{8,16},{16,24},{24,0},{32,40},{40,48},{48,56},{56,32},{64,72... | collective-permute-start | bytes 786440 | tf_op jit(solution)/shard_map/ppermute | solution.py:26
  275.6 6.8 %collective-permute-start.25 = (bf16[32,4096]{1,0:T(8,128)(2,1)S(1)}, bf16[32,4096]{1,0:T(8,128)(2,1)S(1)}, u32[]{:S(2)}, u32[]{:S(2)}) collective-permute-start(bf16[32,4096]{1,0:T(8,128)(2,1)S(1)} %pad_maximum_fusion.10), channel_id=1, source_target_pairs={{0,24},{8,0},{16,8},{24,16},{32,56},{40,32},{48,40},{56,48},{64,88... | collective-permute-start | bytes 786440 | tf_op jit(solution)/shard_map/ppermute | solution.py:26
Sparse Core Ops, SparseCore 0:
  15.4 87.1 all-gather.1
  157.1 95.2 reduce-scatter.1
where the time goes:
time: 293 us; the launch traced here: 292 us
  waiting for transfers between devices  110 us (38%)
  local copies, waits for them, and re-layouts  64.3 us (22%)
  starting transfers between devices  43.8 us (15%)
  matrix products  32.3 us (11%)
  other arithmetic  27.3 us (9%)
  between operations  14.6 us (5%)
    ppermute x8, waiting for transfers between devices, ring(): lax.ppermute(value, axis, [(i, (i + step) % size) for i in range(size)])  51.6 us
    unnamed x38, local copies, waits for them, and re-layouts  38.3 us
    ppermute x16, waiting for transfers between devices, grid_shift(): return lax.ppermute(value, axis, pairs)  35.3 us
    ppermute x16, starting transfers between devices, grid_shift(): return lax.ppermute(value, axis, pairs)  28.3 us
    all_gather x1, waiting for transfers between devices, on_device(): gathered = lax.all_gather(first_half, 'prow', axis=1, tiled=True)  21.9 us
    ppermute x8, starting transfers between devices, ring(): lax.ppermute(value, axis, [(i, (i + step) % size) for i in range(size)])  12.9 us
    dot_general x1, matrix products, on_device(): jnp.dot(multipliers, gathered.reshape(2 * block_size, half), preferred_el...  12.2 us
    mul x1, other arithmetic, on_device(): front[0]  11.9 us
  transfers between devices with their start and end apart: 28, of which 11 were waited for; matrix products, arithmetic and copies ran while one was open for 37% of the time, Pallas kernels for 0%

commit v1 on v0

--- a/solution.py
+++ b/solution.py
@@ -99,11 +99,8 @@
     n_prow = lax.axis_size("prow")
     n_pcol = lax.axis_size("pcol")
     assert n_prow == 4
-    half = col_count // 2
-    first_half = pivot_masked[:, :, :half]
-    gathered = lax.all_gather(first_half, "prow", axis=1, tiled=True)
-    second_half, gathered = lax.optimization_barrier((pivot_masked[:, :, half:], gathered))
-    gathered_rel = gather_relative(second_half, "prow", n_prow)
+    half = (col_count * 11 // 16) // block_size * block_size
+    gathered = lax.all_gather(pivot_masked[:, :, :half], "prow", axis=1, tiled=True)
     panel = jnp.roll(
         gather_relative(pivot_masked[:, :, :panel_width], "prow", n_prow), row_offset, axis=1
     )
@@ -130,19 +127,6 @@
     on_root = pcol == 0
     lower_panel = jnp.where(on_root, lower_panel, sent[0])
     lower_pivot = jnp.where(on_root, lower_pivot, sent[1])
-    own_pivot = lax.dynamic_slice_in_dim(lower_pivot, row_offset, own_rows, 0)
-    upper_own = jnp.concatenate(
-        [
-            jnp.dot(own_pivot, gathered[0], preferred_element_type=jnp.float32),
-            jnp.dot(
-                jnp.roll(own_pivot, -row_offset, axis=1),
-                gathered_rel[0],
-                preferred_element_type=jnp.float32,
-            ),
-        ],
-        1,
-    )
-    upper_own = (pivot_masked[1].astype(jnp.float32) - upper_own).astype(jnp.bfloat16)
     folded = (
         lower_panel[:, :block_size].astype(jnp.float32)
         - jnp.dot(lower_panel[:, block_size:], lower_pivot, preferred_element_type=jnp.float32)
@@ -161,12 +145,29 @@
         multipliers, gathered.reshape(2 * block_size, half), preferred_element_type=jnp.float32
     )
     schur_first = jnp.where(retained[None, :half], schur_first, jnp.zeros_like(schur_first))
+    second_half, schur_first = lax.optimization_barrier(
+        (pivot_masked[:, :, half:], schur_first.astype(jnp.bfloat16))
+    )
     summed_first = lax.psum_scatter(
-        schur_first.astype(jnp.bfloat16), "layer", scatter_dimension=0, tiled=True
+        schur_first, "layer", scatter_dimension=0, tiled=True
     ).astype(jnp.float32)
+    gathered_rel = gather_relative(second_half, "prow", n_prow)
+    own_pivot = lax.dynamic_slice_in_dim(lower_pivot, row_offset, own_rows, 0)
+    upper_own = jnp.concatenate(
+        [
+            jnp.dot(own_pivot, gathered[0], preferred_element_type=jnp.float32),
+            jnp.dot(
+                jnp.roll(own_pivot, -row_offset, axis=1),
+                gathered_rel[0],
+                preferred_element_type=jnp.float32,
+            ),
+        ],
+        1,
+    )
+    upper_own = (pivot_masked[1].astype(jnp.float32) - upper_own).astype(jnp.bfloat16)
     schur_second = masked[:, half:].astype(jnp.float32) - jnp.dot(
         multipliers_rel,
-        gathered_rel.reshape(2 * block_size, half),
+        gathered_rel.reshape(2 * block_size, col_count - half),
         preferred_element_type=jnp.float32,
     )
     schur_second = jnp.where(retained[None, half:], schur_second, jnp.zeros_like(schur_second))

time: 293 us -> 288 us (0.983)
  waiting for transfers between devices: 110 us -> 121 us
  local copies, waits for them, and re-layouts: 64.3 us -> 54.7 us
  other arithmetic: 27.3 us -> 23.7 us
    all_gather x1, waiting for transfers between devices: 21.9 us -> 59.1 us  [on_device(): lax.all_gather(pivot_masked[:, :, :half], 'prow', axis=1, tiled=True)]
    ppermute x8, waiting for transfers between devices: 51.6 us -> 30 us  [ring(): lax.ppermute(value, axis, [(i, (i + step) % size) for i in range(size)])]
    unnamed x38 -> x42, local copies, waits for them, and re-layouts: 38.3 us -> 31.4 us
    ppermute x16, waiting for transfers between devices: 35.3 us -> 31.1 us  [grid_shift(): return lax.ppermute(value, axis, pairs)]
    dot_general x1, matrix products: 12.2 us -> 15.9 us  [on_device(): jnp.dot(multipliers, gathered.reshape(2 * block_size, half), preferred_el...]
    ppermute x16, starting transfers between devices: 28.3 us -> 24.8 us  [grid_shift(): return lax.ppermute(value, axis, pairs)]
    dot_general x1, matrix products: 10.5 us -> 7.08 us  [on_device(): jnp.dot(multipliers_rel, gathered_rel.reshape(2 * block_size, col_count -...]
  transfers between devices with their start and end apart: 28 -> 28, of which waited for: 11 -> 14; matrix products, arithmetic and copies ran while one was open for 37% -> 26% of each run, Pallas kernels for 0% -> 0%
where the time goes in v1:
time: 288 us; the launch traced here: 287 us
  waiting for transfers between devices  121 us (42%)
  local copies, waits for them, and re-layouts  54.7 us (19%)
  starting transfers between devices  41.9 us (15%)
  matrix products  31.2 us (11%)
  other arithmetic  23.7 us (8%)
  between operations  14.7 us (5%)
    all_gather x1, waiting for transfers between devices, on_device(): lax.all_gather(pivot_masked[:, :, :half], 'prow', axis=1, tiled=True)  59.1 us
    unnamed x42, local copies, waits for them, and re-layouts  31.4 us
    ppermute x16, waiting for transfers between devices, grid_shift(): return lax.ppermute(value, axis, pairs)  31.1 us
    ppermute x8, waiting for transfers between devices, ring(): lax.ppermute(value, axis, [(i, (i + step) % size) for i in range(size)])  30 us
    ppermute x16, starting transfers between devices, grid_shift(): return lax.ppermute(value, axis, pairs)  24.8 us
    dot_general x1, matrix products, on_device(): jnp.dot(multipliers, gathered.reshape(2 * block_size, half), preferred_el...  15.9 us
    ppermute x8, starting transfers between devices, ring(): lax.ppermute(value, axis, [(i, (i + step) % size) for i in range(size)])  14.4 us
    mul x1, other arithmetic, on_device(): front[0]  11.8 us
  transfers between devices with their start and end apart: 28, of which 14 were waited for; matrix products, arithmetic and copies ran while one was open for 26% of the time, Pallas kernels for 0%

profile of v1, /device:TPU:0, one launch (start us, length us, event | category | flops | bytes accessed | tf_op | source)
XLA Modules:
  0.0 287.4 jit_solution(574102774831534783)
XLA Ops:
  7.2 0.7 convert_bitcast_fusion.1
  8.1 2.7 bitcast_multiply_fusion.1
  10.8 2.0 copy-done.2
  12.8 1.8 slice.322
  14.6 0.9 fusion.59
  15.6 2.1 collective-permute-start.1
  17.6 2.2 collective-permute-start
  19.8 2.5 slice.310
  22.3 2.7 mul.39
  25.0 12.4 %copy.14 = bf16[64,8,64,256]{3,1,2,0:T(8,128)(2,1)} copy(bf16[64,8,64,256]{3,2,1,0:T(8,128)(2,1)S(1)} %bitcast.157) | data formatting | bytes 33554432
  37.5 11.8 %bitcast_multiply_fusion = bf16[512,16384]{1,0:T(8,128)(2,1)S(1)} fusion(bf16[512,16384]{1,0:T(8,128)(2,1)} %bitcast.156, bf16[1,512,16384]{2,1,0:T(8,128)(2,1)} %param.7), kind=kLoop, calls=%fused_computation.1 | loop fusion | flops 8388608 | bytes 50331648 | tf_op jit(solution)/shard_map/mul | solution.py:88
  49.3 5.8 %copy-done = bf16[512,16384]{1,0:T(8,128)(2,1)} copy-done((bf16[512,16384]{1,0:T(8,128)(2,1)}, bf16[512,16384]{1,0:T(8,128)(2,1)S(1)}, u32[]{:S(2)}) %copy-start) | copy-done | bytes 16777240
  55.5 3.3 %collective-permute-start.3 = (bf16[2,32,512]{2,1,0:T(8,128)(2,1)S(1)}, bf16[2,32,512]{2,1,0:T(8,128)(2,1)S(1)}, u32[]{:S(2)}, u32[]{:S(2)}) collective-permute-start(bf16[2,32,512]{2,1,0:T(8,128)(2,1)S(1)} %slice.317), channel_id=1, source_target_pairs={{0,6},{2,0},{4,2},{6,4},{1,7},{3,1},{5,3},{7,5},{8,14},{10,8},{12,... | collective-permute-start | bytes 196616 | tf_op jit(solution)/shard_map/ppermute | solution.py:8
  58.8 3.7 %collective-permute-done.2 = bf16[2,32,512]{2,1,0:T(8,128)(2,1)S(1)} collective-permute-done((bf16[2,32,512]{2,1,0:T(8,128)(2,1)S(1)}, bf16[2,32,512]{2,1,0:T(8,128)(2,1)S(1)}, u32[]{:S(2)}, u32[]{:S(2)}) %collective-permute-start.2) | collective-permute-done | bytes 65568 | tf_op jit(solution)/shard_map/ppermute | solution.py:8
  62.6 0.9 constant_dynamic-update-slice_fusion.4
  63.6 1.4 convolution_convert_fusion
  65.1 1.3 collective-permute-start.4
  66.6 1.3 collective-permute-start.5
  68.0 0.9 collective-permute-done.5
  69.4 59.1 %all-gather.2.cloned.1.call-done = bf16[2,256,11264]{2,1,0:T(8,128)(2,1)} async-done(((bf16[2,64,11264]{2,1,0:T(8,128)(2,1)}), bf16[2,256,11264]{2,1,0:T(8,128)(2,1)}) %all-gather.2.cloned.1.call-update) | async-done | bytes 11534352 | tf_op jit(solution)/shard_map/all_gather | solution.py:103
  128.4 15.9 %select_convert_fusion = bf16[512,11264]{1,0:T(8,128)(2,1)} fusion(bf16[512,11264]{1,0:T(8,128)(2,1)} %bitcast.165, bf16[512,16384]{1,0:T(8,128)(2,1)} %copy-done, pred[11264]{0:T(1024)(128)(4,1)S(1)} %slice.311, bf16[512,256]{0,1:T(8,128)(2,1)S(1)} %slice.320, bf16[512,256]{0,1:T(8,128)(2,1)S(1)} %subtract_convert_fusion), kind=kOutput, calls=%fused_computation | convolution fusion | flops 5929697280 | bytes 35138560 | tf_op jit(solution)/shard_map/dot_general | solution.py:144
  144.3 1.6 collective-permute-start.7
  145.8 3.4 %copy.16 = bf16[16,8,64,256]{3,2,1,0:T(8,128)(2,1)S(1)} copy(bf16[16,8,64,256]{3,1,2,0:T(8,128)(2,1)} %bitcast.159) | data formatting | bytes 8388608
  149.2 1.9 collective-permute-start.6
  151.2 2.4 fusion.1
  153.5 5.0 %reshape.124 = f32[1,64,16384]{2,1,0:T(8,128)} reshape(f32[1,64,64,256]{3,2,1,0:T(8,128)} %fusion.1) | data formatting | bytes 8388608 | tf_op jit(solution)/shard_map/convert_element_type | solution.py:167
  158.5 1.0 copy.11
  159.5 0.4 fusion.23
  160.0 1.4 constant_dynamic-update-slice_fusion.14
  161.4 14.8 %collective-permute-done.7 = bf16[2,64,5120]{2,1,0:T(8,128)(2,1)S(1)} collective-permute-done((bf16[2,64,5120]{2,1,0:T(8,128)(2,1)}, bf16[2,64,5120]{2,1,0:T(8,128)(2,1)S(1)}, u32[]{:S(2)}, u32[]{:S(2)}) %collective-permute-start.7) | collective-permute-done | bytes 1310752 | tf_op jit(solution)/shard_map/ppermute | solution.py:8
  176.2 1.0 copy-done.5
  177.6 3.7 %convolution_bitcast_fusion = f32[1,64,11264]{2,1,0:T(8,128)S(1)} fusion(bf16[64,256]{1,0:T(8,128)(2,1)S(1)} %constant_dynamic-slice_fusion, bf16[2,256,11264]{2,1,0:T(8,128)(2,1)} %all-gather.2.cloned.1.call-done), kind=kOutput, calls=%fused_computation.2 | convolution fusion | flops 369098752 | bytes 8683520 | tf_op jit(solution)/shard_map/dot_general | solution.py:158
  181.4 1.2 slice.326
  182.7 3.0 %collective-permute-start.9 = (bf16[2,32,5120]{2,1,0:T(8,128)(2,1)S(1)}, bf16[2,32,5120]{2,1,0:T(8,128)(2,1)S(1)}, u32[]{:S(2)}, u32[]{:S(2)}) collective-permute-start(bf16[2,32,5120]{2,1,0:T(8,128)(2,1)S(1)} %slice.326), channel_id=1, source_target_pairs={{0,6},{2,0},{4,2},{6,4},{1,7},{3,1},{5,3},{7,5},{8,14},{10,8},{12,... | collective-permute-start | bytes 1966088 | tf_op jit(solution)/shard_map/ppermute | solution.py:8
  185.6 1.5 constant_dynamic-update-slice_fusion.13
  187.2 7.0 %collective-permute-done.8 = bf16[2,32,5120]{2,1,0:T(8,128)(2,1)S(1)} collective-permute-done((bf16[2,32,5120]{2,1,0:T(8,128)(2,1)S(1)}, bf16[2,32,5120]{2,1,0:T(8,128)(2,1)S(1)}, u32[]{:S(2)}, u32[]{:S(2)}) %collective-permute-start.8) | collective-permute-done | bytes 655392 | tf_op jit(solution)/shard_map/ppermute | solution.py:8
  194.2 4.4 %collective-permute-done.9 = bf16[2,32,5120]{2,1,0:T(8,128)(2,1)S(1)} collective-permute-done((bf16[2,32,5120]{2,1,0:T(8,128)(2,1)S(1)}, bf16[2,32,5120]{2,1,0:T(8,128)(2,1)S(1)}, u32[]{:S(2)}, u32[]{:S(2)}) %collective-permute-start.9) | collective-permute-done | bytes 655392 | tf_op jit(solution)/shard_map/ppermute | solution.py:8
  198.8 7.1 %subtract_select_fusion = f32[512,5120]{1,0:T(8,128)S(1)} fusion(bf16[512,5120]{1,0:T(8,128)(2,1)S(1)} %bitcast.162, bf16[512,16384]{1,0:T(8,128)(2,1)} %copy-done, pred[5120]{0:T(1024)(128)(4,1)S(1)} %slice-done.2, bf16[512,256]{0,1:T(8,128)(2,1)S(1)} %get-tuple-element.39, bf16[512,256]{0,1:T(8,128)(2,1)S(1)} %get-tuple-element.40), kind=kOutput, calls=%fused_computation.3 | convolution fusion | flops 2693267456 | bytes 21500928 | tf_op jit(solution)/shard_map/dot_general | solution.py:168
  205.9 5.1 %fusion.58 = (f32[4,4,32,2560]{3,2,1,0:T(8,128)}, f32[4,4,32,2560]{3,2,1,0:T(8,128)}) fusion(f32[4,4,32,5120]{3,2,1,0:T(8,128)S(1)} %bitcast.158), kind=kLoop, calls=%fused_computation.144 | loop fusion | bytes 20971520 | tf_op jit(solution)/shard_map/slice | solution.py:65
  211.0 1.6 dynamic-slice_convert_fusion
  212.7 1.5 collective-permute-start.18
  214.2 1.9 collective-permute-start.20
  216.0 1.8 dynamic-slice_bitcast_fusion
  217.9 1.5 collective-permute-start.10
  219.4 1.8 collective-permute-start.12
  221.2 2.4 convolution_bitcast_fusion.1
  223.8 1.7 fusion
  225.6 1.2 slice-done
  227.2 1.4 collective-permute-done.18
  228.8 2.3 collective-permute-start.21
  231.3 2.2 collective-permute-start.13
  233.7 16.5 %collective-permute-done.21 = bf16[4,32,2560]{2,1,0:T(8,128)(2,1)S(1)} collective-permute-done((bf16[4,32,2560]{2,1,0:T(8,128)(2,1)S(1)}, bf16[4,32,2560]{2,1,0:T(8,128)(2,1)S(1)}, u32[]{:S(2)}, u32[]{:S(2)}) %collective-permute-start.21) | collective-permute-done | bytes 655392 | tf_op jit(solution)/shard_map/ppermute | solution.py:26
  250.2 3.8 %collective-permute-done.19 = bf16[4,32,2560]{2,1,0:T(8,128)(2,1)S(1)} collective-permute-done((bf16[4,32,2560]{2,1,0:T(8,128)(2,1)S(1)}, bf16[4,32,2560]{2,1,0:T(8,128)(2,1)S(1)}, u32[]{:S(2)}, u32[]{:S(2)}) %collective-permute-start.19) | collective-permute-done | bytes 655392 | tf_op jit(solution)/shard_map/ppermute | solution.py:26
  254.3 1.8 collective-permute-start.22
  256.1 1.8 collective-permute-start.24
  258.0 2.8 collective-permute-done.11
  261.2 4.2 %collective-permute-start.16 = (bf16[16,2560]{1,0:T(8,128)(2,1)S(1)}, bf16[16,2560]{1,0:T(8,128)(2,1)S(1)}, u32[]{:S(2)}, u32[]{:S(2)}) collective-permute-start(bf16[16,2560]{1,0:T(8,128)(2,1)S(1)} %get-tuple-element.36), channel_id=1, source_target_pairs={{0,96},{8,104},{16,112},{24,120},{32,0},{40,8},{48,16},{56,24},{64... | collective-permute-start | bytes 245768 | tf_op jit(solution)/shard_map/ppermute | solution.py:26
  265.6 2.1 collective-permute-start.23
  267.8 3.4 %collective-permute-start.17 = (bf16[32,2560]{1,0:T(8,128)(2,1)S(1)}, bf16[32,2560]{1,0:T(8,128)(2,1)S(1)}, u32[]{:S(2)}, u32[]{:S(2)}) collective-permute-start(bf16[32,2560]{1,0:T(8,128)(2,1)S(1)} %pad_maximum_fusion.8), channel_id=1, source_target_pairs={{0,96},{8,104},{16,112},{24,120},{32,0},{40,8},{48,16},{56,24},{64... | collective-permute-start | bytes 491528 | tf_op jit(solution)/shard_map/ppermute | solution.py:26
  271.3 0.9 collective-permute-done.23
  272.2 1.8 collective-permute-done.17
  274.0 3.8 %collective-permute-done.15 = bf16[32,2560]{1,0:T(8,128)(2,1)S(1)} collective-permute-done((bf16[32,2560]{1,0:T(8,128)(2,1)S(1)}, bf16[32,2560]{1,0:T(8,128)(2,1)S(1)}, u32[]{:S(2)}, u32[]{:S(2)}) %collective-permute-start.15) | collective-permute-done | bytes 163872 | tf_op jit(solution)/shard_map/ppermute | solution.py:26
  277.9 1.2 convert_element_type.161
  279.1 1.5 maximum_bitcast_fusion
  (107 shorter events, 4.4 us)
Async XLA Ops:
  7.2 121.2 %all-gather.2.cloned.1.call-start = ((), (), s32[]{:S(2)}) async-start(), calls=%async_computation.1 | async-start | bytes 14417920 | tf_op jit(solution)/shard_map/all_gather | solution.py:103
  10.8 2.0 copy-start.2
  12.8 9.5 %copy-start.9 = (s32[1,2,64]{2,1,0:T(2,128)S(1)}, s32[1,2,64]{2,1,0:T(2,128)}, u32[]{:S(2)}) copy-start(s32[1,2,64]{2,1,0:T(2,128)} %param.10) | copy-start | bytes 1540
  14.6 263.3 %reduce-scatter.2.cloned.1.call-start = ((), (), s32[]{:S(2)}) async-start(), calls=%async_computation.2 | async-start | bytes 12255232 | tf_op jit(solution)/shard_map/reduce_scatter | solution.py:151
  15.6 39.8 %collective-permute-start.1 = (bf16[2,64,512]{2,1,0:T(8,128)(2,1)S(1)}, bf16[2,64,512]{2,1,0:T(8,128)(2,1)S(1)}, u32[]{:S(2)}, u32[]{:S(2)}) collective-permute-start(bf16[2,64,512]{2,1,0:T(8,128)(2,1)S(1)} %get-tuple-element.19), channel_id=1, source_target_pairs={{0,2},{2,4},{4,6},{6,0},{1,3},{3,5},{5,7},{7,1},{8,10},{10,12},{12... | collective-permute-start | bytes 393224 | tf_op jit(solution)/shard_map/ppermute | solution.py:8
  17.6 37.8 %collective-permute-start = (bf16[2,64,512]{2,1,0:T(8,128)(2,1)S(1)}, bf16[2,64,512]{2,1,0:T(8,128)(2,1)S(1)}, u32[]{:S(2)}, u32[]{:S(2)}) collective-permute-start(bf16[2,64,512]{2,1,0:T(8,128)(2,1)S(1)} %get-tuple-element.19), channel_id=1, source_target_pairs={{0,6},{2,0},{4,2},{6,4},{1,7},{3,1},{5,3},{7,5},{8,14},{10,8},{12,... | collective-permute-start | bytes 393224 | tf_op jit(solution)/shard_map/ppermute | solution.py:8
  37.5 17.6 %copy-start.7 = (bf16[1,2,256,256]{3,2,1,0:T(8,128)(2,1)S(1)}, bf16[1,2,256,256]{3,2,1,0:T(8,128)(2,1)}, u32[]{:S(2)}) copy-start(bf16[1,2,256,256]{3,2,1,0:T(8,128)(2,1)} %param.9) | copy-start | bytes 786436
  49.3 5.8 %copy-start = (bf16[512,16384]{1,0:T(8,128)(2,1)}, bf16[512,16384]{1,0:T(8,128)(2,1)S(1)}, u32[]{:S(2)}) copy-start(bf16[512,16384]{1,0:T(8,128)(2,1)S(1)} %bitcast_multiply_fusion) | copy-start | bytes 50331652
  55.4 7.1 %collective-permute-start.2 = (bf16[2,32,512]{2,1,0:T(8,128)(2,1)S(1)}, bf16[2,32,512]{2,1,0:T(8,128)(2,1)S(1)}, u32[]{:S(2)}, u32[]{:S(2)}) collective-permute-start(bf16[2,32,512]{2,1,0:T(8,128)(2,1)S(1)} %slice.316), channel_id=1, source_target_pairs={{0,2},{2,4},{4,6},{6,0},{1,3},{3,5},{5,7},{7,1},{8,10},{10,12},{12... | collective-permute-start | bytes 196616 | tf_op jit(solution)/shard_map/ppermute | solution.py:8
  55.5 7.0 %collective-permute-start.3 = (bf16[2,32,512]{2,1,0:T(8,128)(2,1)S(1)}, bf16[2,32,512]{2,1,0:T(8,128)(2,1)S(1)}, u32[]{:S(2)}, u32[]{:S(2)}) collective-permute-start(bf16[2,32,512]{2,1,0:T(8,128)(2,1)S(1)} %slice.317), channel_id=1, source_target_pairs={{0,6},{2,0},{4,2},{6,4},{1,7},{3,1},{5,3},{7,5},{8,14},{10,8},{12,... | collective-permute-start | bytes 196616 | tf_op jit(solution)/shard_map/ppermute | solution.py:8
  65.1 3.8 %collective-permute-start.4 = (bf16[512,512]{0,1:T(8,128)(2,1)S(1)}, bf16[512,512]{0,1:T(8,128)(2,1)S(1)}, u32[]{:S(2)}, u32[]{:S(2)}) collective-permute-start(bf16[512,512]{0,1:T(8,128)(2,1)S(1)} %pad_maximum_fusion.6), channel_id=1, source_target_pairs={{0,1},{2,3},{4,5},{6,7},{8,9},{10,11},{12,13},{14,15},{16,17},{18,... | collective-permute-start | bytes 1572872 | tf_op jit(solution)/shard_map/ppermute | solution.py:126
  66.6 2.3 collective-permute-start.5
  67.9 85.6 %copy-start.8 = (pred[16384]{0:T(1024)(128)(4,1)}, pred[16384]{0:T(1024)(128)(4,1)S(1)}, u32[]{:S(2)}) copy-start(pred[16384]{0:T(1024)(128)(4,1)S(1)} %add_compare_fusion) | copy-start | bytes 49156
  144.3 31.9 %collective-permute-start.7 = (bf16[2,64,5120]{2,1,0:T(8,128)(2,1)}, bf16[2,64,5120]{2,1,0:T(8,128)(2,1)S(1)}, u32[]{:S(2)}, u32[]{:S(2)}) collective-permute-start(bf16[2,64,5120]{2,1,0:T(8,128)(2,1)} %slice.310), channel_id=1, source_target_pairs={{0,2},{2,4},{4,6},{6,0},{1,3},{3,5},{5,7},{7,1},{8,10},{10,12},{12... | collective-permute-start | bytes 3932168 | tf_op jit(solution)/shard_map/ppermute | solution.py:8
  149.2 32.1 %collective-permute-start.6 = (bf16[2,64,5120]{2,1,0:T(8,128)(2,1)}, bf16[2,64,5120]{2,1,0:T(8,128)(2,1)}, u32[]{:S(2)}, u32[]{:S(2)}) collective-permute-start(bf16[2,64,5120]{2,1,0:T(8,128)(2,1)} %slice.310), channel_id=1, source_target_pairs={{0,6},{2,0},{4,2},{6,4},{1,7},{3,1},{5,3},{7,5},{8,14},{10,8},{12,... | collective-permute-start | bytes 3932168 | tf_op jit(solution)/shard_map/ppermute | solution.py:8
  176.2 1.1 copy-start.5
  177.3 16.9 %collective-permute-start.8 = (bf16[2,32,5120]{2,1,0:T(8,128)(2,1)S(1)}, bf16[2,32,5120]{2,1,0:T(8,128)(2,1)S(1)}, u32[]{:S(2)}, u32[]{:S(2)}) collective-permute-start(bf16[2,32,5120]{2,1,0:T(8,128)(2,1)S(1)} %slice.325), channel_id=1, source_target_pairs={{0,2},{2,4},{4,6},{6,0},{1,3},{3,5},{5,7},{7,1},{8,10},{10,12},{12... | collective-permute-start | bytes 1966088 | tf_op jit(solution)/shard_map/ppermute | solution.py:8
  181.4 17.3 %copy-start.6 = (bf16[2,64,5120]{2,1,0:T(8,128)(2,1)S(1)}, bf16[2,64,5120]{2,1,0:T(8,128)(2,1)}, u32[]{:S(2)}) copy-start(bf16[2,64,5120]{2,1,0:T(8,128)(2,1)} %copy-done.5) | copy-start | bytes 3932164
  181.4 17.4 %slice-start.2 = ((pred[16384]{0:T(1024)(128)(4,1)}), pred[5120]{0:T(1024)(128)(4,1)S(1)}, s32[]{:S(2)}) async-start(pred[16384]{0:T(1024)(128)(4,1)} %copy-done.8), calls=%async_computation.5 | async-start | bytes 10240 | tf_op jit(solution)/shard_map/slice | solution.py:173
  182.7 16.0 %collective-permute-start.9 = (bf16[2,32,5120]{2,1,0:T(8,128)(2,1)S(1)}, bf16[2,32,5120]{2,1,0:T(8,128)(2,1)S(1)}, u32[]{:S(2)}, u32[]{:S(2)}) collective-permute-start(bf16[2,32,5120]{2,1,0:T(8,128)(2,1)S(1)} %slice.326), channel_id=1, source_target_pairs={{0,6},{2,0},{4,2},{6,4},{1,7},{3,1},{5,3},{7,5},{8,14},{10,8},{12,... | collective-permute-start | bytes 1966088 | tf_op jit(solution)/shard_map/ppermute | solution.py:8
  198.8 7.1 %copy-start.4 = (bf16[2,256,5120]{2,1,0:T(8,128)(2,1)}, bf16[2,256,5120]{2,1,0:T(8,128)(2,1)S(1)}, u32[]{:S(2)}) copy-start(bf16[2,256,5120]{2,1,0:T(8,128)(2,1)S(1)} %constant_dynamic-update-slice_fusion.10) | copy-start | bytes 15728644
  211.0 12.6 %copy-start.1 = (f32[4,4,32,2560]{3,2,1,0:T(8,128)S(1)}, f32[4,4,32,2560]{3,2,1,0:T(8,128)}, u32[]{:S(2)}) copy-start(f32[4,4,32,2560]{3,2,1,0:T(8,128)} %get-tuple-element.11) | copy-start | bytes 15728644
  212.7 15.9 %collective-permute-start.18 = (bf16[2,32,2560]{2,1,0:T(8,128)(2,1)S(1)}, bf16[2,32,2560]{2,1,0:T(8,128)(2,1)S(1)}, u32[]{:S(2)}, u32[]{:S(2)}) collective-permute-start(bf16[2,32,2560]{2,1,0:T(8,128)(2,1)S(1)} %get-tuple-element.33), channel_id=1, source_target_pairs={{0,32},{8,40},{16,48},{24,56},{32,64},{40,72},{48,80},{56,88},{64,... | collective-permute-start | bytes 983048 | tf_op jit(solution)/shard_map/ppermute | solution.py:26
  214.2 14.4 %collective-permute-start.20 = (bf16[2,32,2560]{2,1,0:T(8,128)(2,1)S(1)}, bf16[2,32,2560]{2,1,0:T(8,128)(2,1)S(1)}, u32[]{:S(2)}, u32[]{:S(2)}) collective-permute-start(bf16[2,32,2560]{2,1,0:T(8,128)(2,1)S(1)} %get-tuple-element.34), channel_id=1, source_target_pairs={{0,96},{8,104},{16,112},{24,120},{32,0},{40,8},{48,16},{56,24},{64... | collective-permute-start | bytes 983048 | tf_op jit(solution)/shard_map/ppermute | solution.py:26
  217.9 6.0 %copy-start.3 = (f32[1,64,16384]{2,1,0:T(8,128)S(1)}, f32[1,64,16384]{2,1,0:T(8,128)}, u32[]{:S(2)}) copy-start(f32[1,64,16384]{2,1,0:T(8,128)} %reshape.124) | copy-start | bytes 12582916
  217.9 15.6 %collective-permute-start.10 = (bf16[2,32,2560]{2,1,0:T(8,128)(2,1)S(1)}, bf16[2,32,2560]{2,1,0:T(8,128)(2,1)S(1)}, u32[]{:S(2)}, u32[]{:S(2)}) collective-permute-start(bf16[2,32,2560]{2,1,0:T(8,128)(2,1)S(1)} %get-tuple-element.31), channel_id=1, source_target_pairs={{0,8},{8,16},{16,24},{24,0},{32,40},{40,48},{48,56},{56,32},{64,72... | collective-permute-start | bytes 983048 | tf_op jit(solution)/shard_map/ppermute | solution.py:26
  219.4 11.8 %collective-permute-start.12 = (bf16[2,32,2560]{2,1,0:T(8,128)(2,1)S(1)}, bf16[2,32,2560]{2,1,0:T(8,128)(2,1)S(1)}, u32[]{:S(2)}, u32[]{:S(2)}) collective-permute-start(bf16[2,32,2560]{2,1,0:T(8,128)(2,1)S(1)} %get-tuple-element.32), channel_id=1, source_target_pairs={{0,24},{8,0},{16,8},{24,16},{32,56},{40,32},{48,40},{56,48},{64,88... | collective-permute-start | bytes 983048 | tf_op jit(solution)/shard_map/ppermute | solution.py:26
  223.8 3.0 %slice-start = ((s8[5242880]{0:T(1024)(128)(4,1)}), s8[4194304]{0:T(1024)(128)(4,1)S(1)}, s32[]{:S(2)}) async-start(s8[5242880]{0:T(1024)(128)(4,1)} %bitcast.160), calls=%async_computation.3 | async-start | bytes 8388608
  223.8 3.2 %slice-start.1 = ((s8[5242880]{0:T(1024)(128)(4,1)}), s8[1048576]{0:T(1024)(128)(4,1)S(1)}, s32[]{:S(2)}) async-start(s8[5242880]{0:T(1024)(128)(4,1)} %bitcast.160), calls=%async_computation.4 | async-start | bytes 2097152
  228.8 21.5 %collective-permute-start.21 = (bf16[4,32,2560]{2,1,0:T(8,128)(2,1)S(1)}, bf16[4,32,2560]{2,1,0:T(8,128)(2,1)S(1)}, u32[]{:S(2)}, u32[]{:S(2)}) collective-permute-start(bf16[4,32,2560]{2,1,0:T(8,128)(2,1)S(1)} %pad_maximum_fusion.3), channel_id=1, source_target_pairs={{0,96},{8,104},{16,112},{24,120},{32,0},{40,8},{48,16},{56,24},{64... | collective-permute-start | bytes 1966088 | tf_op jit(solution)/shard_map/ppermute | solution.py:26
  231.1 22.9 %collective-permute-start.19 = (bf16[4,32,2560]{2,1,0:T(8,128)(2,1)S(1)}, bf16[4,32,2560]{2,1,0:T(8,128)(2,1)S(1)}, u32[]{:S(2)}, u32[]{:S(2)}) collective-permute-start(bf16[4,32,2560]{2,1,0:T(8,128)(2,1)S(1)} %pad_maximum_fusion.2), channel_id=1, source_target_pairs={{0,32},{8,40},{16,48},{24,56},{32,64},{40,72},{48,80},{56,88},{64,... | collective-permute-start | bytes 1966088 | tf_op jit(solution)/shard_map/ppermute | solution.py:26
  231.3 26.6 %collective-permute-start.13 = (bf16[4,32,2560]{2,1,0:T(8,128)(2,1)S(1)}, bf16[4,32,2560]{2,1,0:T(8,128)(2,1)S(1)}, u32[]{:S(2)}, u32[]{:S(2)}) collective-permute-start(bf16[4,32,2560]{2,1,0:T(8,128)(2,1)S(1)} %pad_maximum_fusion.1), channel_id=1, source_target_pairs={{0,24},{8,0},{16,8},{24,16},{32,56},{40,32},{48,40},{56,48},{64,88... | collective-permute-start | bytes 1966088 | tf_op jit(solution)/shard_map/ppermute | solution.py:26
  233.6 27.1 %collective-permute-start.11 = (bf16[4,32,2560]{2,1,0:T(8,128)(2,1)S(1)}, bf16[4,32,2560]{2,1,0:T(8,128)(2,1)S(1)}, u32[]{:S(2)}, u32[]{:S(2)}) collective-permute-start(bf16[4,32,2560]{2,1,0:T(8,128)(2,1)S(1)} %pad_maximum_fusion), channel_id=1, source_target_pairs={{0,8},{8,16},{16,24},{24,0},{32,40},{40,48},{48,56},{56,32},{64,72... | collective-permute-start | bytes 1966088 | tf_op jit(solution)/shard_map/ppermute | solution.py:26
  254.3 11.1 %collective-permute-start.22 = (bf16[16,2560]{1,0:T(8,128)(2,1)S(1)}, bf16[16,2560]{1,0:T(8,128)(2,1)S(1)}, u32[]{:S(2)}, u32[]{:S(2)}) collective-permute-start(bf16[16,2560]{1,0:T(8,128)(2,1)S(1)} %get-tuple-element.37), channel_id=1, source_target_pairs={{0,8},{8,16},{16,24},{24,0},{32,40},{40,48},{48,56},{56,32},{64,72... | collective-permute-start | bytes 245768 | tf_op jit(solution)/shard_map/ppermute | solution.py:26
  256.1 9.3 %collective-permute-start.24 = (bf16[16,2560]{1,0:T(8,128)(2,1)S(1)}, bf16[16,2560]{1,0:T(8,128)(2,1)S(1)}, u32[]{:S(2)}, u32[]{:S(2)}) collective-permute-start(bf16[16,2560]{1,0:T(8,128)(2,1)S(1)} %get-tuple-element.38), channel_id=1, source_target_pairs={{0,24},{8,0},{16,8},{24,16},{32,56},{40,32},{48,40},{56,48},{64,88... | collective-permute-start | bytes 245768 | tf_op jit(solution)/shard_map/ppermute | solution.py:26
  261.1 6.7 %collective-permute-start.14 = (bf16[16,2560]{1,0:T(8,128)(2,1)S(1)}, bf16[16,2560]{1,0:T(8,128)(2,1)S(1)}, u32[]{:S(2)}, u32[]{:S(2)}) collective-permute-start(bf16[16,2560]{1,0:T(8,128)(2,1)S(1)} %get-tuple-element.35), channel_id=1, source_target_pairs={{0,32},{8,40},{16,48},{24,56},{32,64},{40,72},{48,80},{56,88},{64,... | collective-permute-start | bytes 245768 | tf_op jit(solution)/shard_map/ppermute | solution.py:26
  261.2 6.6 %collective-permute-start.16 = (bf16[16,2560]{1,0:T(8,128)(2,1)S(1)}, bf16[16,2560]{1,0:T(8,128)(2,1)S(1)}, u32[]{:S(2)}, u32[]{:S(2)}) collective-permute-start(bf16[16,2560]{1,0:T(8,128)(2,1)S(1)} %get-tuple-element.36), channel_id=1, source_target_pairs={{0,96},{8,104},{16,112},{24,120},{32,0},{40,8},{48,16},{56,24},{64... | collective-permute-start | bytes 245768 | tf_op jit(solution)/shard_map/ppermute | solution.py:26
  265.5 5.8 %collective-permute-start.25 = (bf16[32,2560]{1,0:T(8,128)(2,1)S(1)}, bf16[32,2560]{1,0:T(8,128)(2,1)S(1)}, u32[]{:S(2)}, u32[]{:S(2)}) collective-permute-start(bf16[32,2560]{1,0:T(8,128)(2,1)S(1)} %pad_maximum_fusion.10), channel_id=1, source_target_pairs={{0,24},{8,0},{16,8},{24,16},{32,56},{40,32},{48,40},{56,48},{64,88... | collective-permute-start | bytes 491528 | tf_op jit(solution)/shard_map/ppermute | solution.py:26
  265.6 6.6 %collective-permute-start.23 = (bf16[32,2560]{1,0:T(8,128)(2,1)S(1)}, bf16[32,2560]{1,0:T(8,128)(2,1)S(1)}, u32[]{:S(2)}, u32[]{:S(2)}) collective-permute-start(bf16[32,2560]{1,0:T(8,128)(2,1)S(1)} %pad_maximum_fusion.9), channel_id=1, source_target_pairs={{0,8},{8,16},{16,24},{24,0},{32,40},{40,48},{48,56},{56,32},{64,72... | collective-permute-start | bytes 491528 | tf_op jit(solution)/shard_map/ppermute | solution.py:26
  267.8 6.2 %collective-permute-start.17 = (bf16[32,2560]{1,0:T(8,128)(2,1)S(1)}, bf16[32,2560]{1,0:T(8,128)(2,1)S(1)}, u32[]{:S(2)}, u32[]{:S(2)}) collective-permute-start(bf16[32,2560]{1,0:T(8,128)(2,1)S(1)} %pad_maximum_fusion.8), channel_id=1, source_target_pairs={{0,96},{8,104},{16,112},{24,120},{32,0},{40,8},{48,16},{56,24},{64... | collective-permute-start | bytes 491528 | tf_op jit(solution)/shard_map/ppermute | solution.py:26
  271.2 6.6 %collective-permute-start.15 = (bf16[32,2560]{1,0:T(8,128)(2,1)S(1)}, bf16[32,2560]{1,0:T(8,128)(2,1)S(1)}, u32[]{:S(2)}, u32[]{:S(2)}) collective-permute-start(bf16[32,2560]{1,0:T(8,128)(2,1)S(1)} %pad_maximum_fusion.7), channel_id=1, source_target_pairs={{0,32},{8,40},{16,48},{24,56},{32,64},{40,72},{48,80},{56,88},{64,... | collective-permute-start | bytes 491528 | tf_op jit(solution)/shard_map/ppermute | solution.py:26
Sparse Core Ops, SparseCore 0:
  14.7 113.6 all-gather.1
  160.1 103.3 reduce-scatter.1

commit v2 on v1

--- a/solution.py
+++ b/solution.py
@@ -101,6 +101,7 @@
     assert n_prow == 4
     half = (col_count * 11 // 16) // block_size * block_size
     gathered = lax.all_gather(pivot_masked[:, :, :half], "prow", axis=1, tiled=True)
+    later_cols, gathered = lax.optimization_barrier((pivot_masked[:, :, half:], gathered))
     panel = jnp.roll(
         gather_relative(pivot_masked[:, :, :panel_width], "prow", n_prow), row_offset, axis=1
     )
@@ -146,7 +147,7 @@
     )
     schur_first = jnp.where(retained[None, :half], schur_first, jnp.zeros_like(schur_first))
     second_half, schur_first = lax.optimization_barrier(
-        (pivot_masked[:, :, half:], schur_first.astype(jnp.bfloat16))
+        (later_cols, schur_first.astype(jnp.bfloat16))
     )
     summed_first = lax.psum_scatter(
         schur_first, "layer", scatter_dimension=0, tiled=True
@@ -155,16 +156,21 @@
     own_pivot = lax.dynamic_slice_in_dim(lower_pivot, row_offset, own_rows, 0)
     upper_own = jnp.concatenate(
         [
-            jnp.dot(own_pivot, gathered[0], preferred_element_type=jnp.float32),
-            jnp.dot(
-                jnp.roll(own_pivot, -row_offset, axis=1),
-                gathered_rel[0],
-                preferred_element_type=jnp.float32,
-            ),
+            (
+                pivot_masked[1, :, :half].astype(jnp.float32)
+                - jnp.dot(own_pivot, gathered[0], preferred_element_type=jnp.float32)
+            ).astype(jnp.bfloat16),
+            (
+                pivot_masked[1, :, half:].astype(jnp.float32)
+                - jnp.dot(
+                    jnp.roll(own_pivot, -row_offset, axis=1),
+                    gathered_rel[0],
+                    preferred_element_type=jnp.float32,
+                )
+            ).astype(jnp.bfloat16),
         ],
         1,
     )
-    upper_own = (pivot_masked[1].astype(jnp.float32) - upper_own).astype(jnp.bfloat16)
     schur_second = masked[:, half:].astype(jnp.float32) - jnp.dot(
         multipliers_rel,
         gathered_rel.reshape(2 * block_size, col_count - half),

time: 288 us -> 283 us (0.983)
  local copies, waits for them, and re-layouts: 54.7 us -> 42.6 us
  waiting for transfers between devices: 121 us -> 130 us
    ppermute x8, waiting for transfers between devices: 30 us -> 39.7 us  [ring(): lax.ppermute(value, axis, [(i, (i + step) % size) for i in range(size)])]
    unnamed x42 -> x45, local copies, waits for them, and re-layouts: 31.4 us -> 24.6 us
    convert_element_type x1 -> x0, local copies, waits for them, and re-layouts: 4.96 us -> none  [on_device(): pivot_masked[1].astype(jnp.float32) - upper_own]
    convert_element_type x2 -> x0, other arithmetic: 4.09 us -> none  [the longest x1 2.38 us: on_device(): pivot_masked[1].astype(jnp.float32) - upper_own]
  transfers between devices with their start and end apart: 28 -> 28, of which waited for: 14 -> 10; matrix products, arithmetic and copies ran while one was open for 26% -> 23% of each run, Pallas kernels for 0% -> 0%
where the time goes in v2:
time: 283 us; the launch traced here: 282 us
  waiting for transfers between devices  130 us (46%)
  local copies, waits for them, and re-layouts  42.6 us (15%)
  starting transfers between devices  40.9 us (14%)
  matrix products  31.3 us (11%)
  other arithmetic  22.8 us (8%)
  between operations  14.8 us (5%)
    all_gather x1, waiting for transfers between devices, on_device(): lax.all_gather(pivot_masked[:, :, :half], 'prow', axis=1, tiled=True)  59.5 us
    ppermute x8, waiting for transfers between devices, ring(): lax.ppermute(value, axis, [(i, (i + step) % size) for i in range(size)])  39.7 us
    ppermute x16, waiting for transfers between devices, grid_shift(): return lax.ppermute(value, axis, pairs)  29.5 us
    unnamed x45, local copies, waits for them, and re-layouts  24.6 us
    ppermute x16, starting transfers between devices, grid_shift(): return lax.ppermute(value, axis, pairs)  23.8 us
    dot_general x1, matrix products, on_device(): jnp.dot(multipliers, gathered.reshape(2 * block_size, half), preferred_el...  15.9 us
    ppermute x8, starting transfers between devices, ring(): lax.ppermute(value, axis, [(i, (i + step) % size) for i in range(size)])  14.4 us
    mul x1, other arithmetic, on_device(): front[0]  11.8 us
  transfers between devices with their start and end apart: 28, of which 10 were waited for; matrix products, arithmetic and copies ran while one was open for 23% of the time, Pallas kernels for 0%

profile of v2, /device:TPU:0, one launch (start us, length us, event | category | flops | bytes accessed | tf_op | source)
XLA Modules:
  0.0 282.2 jit_solution(3394525759007094801)
XLA Ops:
  7.2 0.7 convert_bitcast_fusion.1
  8.1 2.7 bitcast_multiply_fusion.1
  10.8 2.0 copy-done.1
  12.8 1.8 slice.314
  14.6 0.9 fusion.61
  15.6 2.1 collective-permute-start.1
  17.6 2.2 collective-permute-start
  19.8 1.4 slice.313
  21.3 2.7 mul.35
  24.0 12.5 %copy.14 = bf16[64,8,64,256]{3,1,2,0:T(8,128)(2,1)} copy(bf16[64,8,64,256]{3,2,1,0:T(8,128)(2,1)S(1)} %bitcast.158) | data formatting | bytes 33554432
  36.5 11.8 %bitcast_multiply_fusion = bf16[512,16384]{1,0:T(8,128)(2,1)S(1)} fusion(bf16[512,16384]{1,0:T(8,128)(2,1)} %bitcast.157, bf16[1,512,16384]{2,1,0:T(8,128)(2,1)} %param.7), kind=kLoop, calls=%fused_computation.1 | loop fusion | flops 8388608 | bytes 50331648 | tf_op jit(solution)/shard_map/mul | solution.py:88
  48.3 5.8 %copy-done = bf16[512,16384]{1,0:T(8,128)(2,1)} copy-done((bf16[512,16384]{1,0:T(8,128)(2,1)}, bf16[512,16384]{1,0:T(8,128)(2,1)S(1)}, u32[]{:S(2)}) %copy-start) | copy-done | bytes 16777240
  54.2 0.3 convolution_convert_fusion.1
  54.6 3.3 %collective-permute-start.3 = (bf16[2,32,512]{2,1,0:T(8,128)(2,1)S(1)}, bf16[2,32,512]{2,1,0:T(8,128)(2,1)S(1)}, u32[]{:S(2)}, u32[]{:S(2)}) collective-permute-start(bf16[2,32,512]{2,1,0:T(8,128)(2,1)S(1)} %slice.321), channel_id=1, source_target_pairs={{0,6},{2,0},{4,2},{6,4},{1,7},{3,1},{5,3},{7,5},{8,14},{10,8},{12,... | collective-permute-start | bytes 196616 | tf_op jit(solution)/shard_map/ppermute | solution.py:8
  57.9 3.7 %collective-permute-done.2 = bf16[2,32,512]{2,1,0:T(8,128)(2,1)S(1)} collective-permute-done((bf16[2,32,512]{2,1,0:T(8,128)(2,1)S(1)}, bf16[2,32,512]{2,1,0:T(8,128)(2,1)S(1)}, u32[]{:S(2)}, u32[]{:S(2)}) %collective-permute-start.2) | collective-permute-done | bytes 65568 | tf_op jit(solution)/shard_map/ppermute | solution.py:8
  61.6 0.9 constant_dynamic-update-slice_fusion.4
  62.7 1.4 convolution_convert_fusion
  64.2 1.3 collective-permute-start.4
  65.7 1.3 collective-permute-start.5
  67.0 0.9 collective-permute-done.5
  68.2 0.5 copy-done.9
  68.6 0.3 subtract_convert_fusion
  68.9 59.5 %all-gather.2.cloned.1.call-done = bf16[2,256,11264]{2,1,0:T(8,128)(2,1)} async-done(((bf16[2,64,11264]{2,1,0:T(8,128)(2,1)}), bf16[2,256,11264]{2,1,0:T(8,128)(2,1)}) %all-gather.2.cloned.1.call-update) | async-done | bytes 11534352 | tf_op jit(solution)/shard_map/all_gather | solution.py:103
  128.4 15.9 %select_convert_fusion = bf16[512,11264]{1,0:T(8,128)(2,1)} fusion(bf16[512,11264]{1,0:T(8,128)(2,1)} %bitcast.164, bf16[512,16384]{1,0:T(8,128)(2,1)} %copy-done, pred[11264]{0:T(1024)(128)(4,1)S(1)} %slice.315, bf16[512,256]{0,1:T(8,128)(2,1)S(1)} %slice.324, bf16[512,256]{0,1:T(8,128)(2,1)S(1)} %subtract_convert_fusion), kind=kOutput, calls=%fused_computation | convolution fusion | flops 5929697280 | bytes 35138560 | tf_op jit(solution)/shard_map/dot_general | solution.py:145
  144.3 1.6 collective-permute-start.7
  145.8 1.7 collective-permute-start.6
  147.5 0.8 constant_dynamic-slice_fusion
  148.3 1.0 copy.11
  149.3 2.2 fusion.25
  151.5 24.5 %collective-permute-done.7 = bf16[2,64,5120]{2,1,0:T(8,128)(2,1)S(1)} collective-permute-done((bf16[2,64,5120]{2,1,0:T(8,128)(2,1)S(1)}, bf16[2,64,5120]{2,1,0:T(8,128)(2,1)S(1)}, u32[]{:S(2)}, u32[]{:S(2)}) %collective-permute-start.7) | collective-permute-done | bytes 1310752 | tf_op jit(solution)/shard_map/ppermute | solution.py:8
  176.0 0.6 collective-permute-start.8
  176.6 4.6 %fusion = bf16[64,11264]{1,0:T(8,128)(2,1)S(1)} fusion(bf16[64,256]{1,0:T(8,128)(2,1)S(1)} %constant_dynamic-slice_fusion, bf16[2,256,11264]{2,1,0:T(8,128)(2,1)} %all-gather.2.cloned.1.call-done, bf16[2,64,16384]{2,1,0:T(8,128)(2,1)} %copy-done.1), kind=kOutput, calls=%fused_computation.3 | convolution fusion | flops 371261440 | bytes 8683520 | tf_op jit(solution)/shard_map/dot_general | solution.py:161
  181.3 1.2 slice.329
  182.5 3.0 %collective-permute-start.9 = (bf16[2,32,5120]{2,1,0:T(8,128)(2,1)S(1)}, bf16[2,32,5120]{2,1,0:T(8,128)(2,1)S(1)}, u32[]{:S(2)}, u32[]{:S(2)}) collective-permute-start(bf16[2,32,5120]{2,1,0:T(8,128)(2,1)S(1)} %slice.329), channel_id=1, source_target_pairs={{0,6},{2,0},{4,2},{6,4},{1,7},{3,1},{5,3},{7,5},{8,14},{10,8},{12,... | collective-permute-start | bytes 1966088 | tf_op jit(solution)/shard_map/ppermute | solution.py:8
  185.5 1.4 constant_dynamic-update-slice_fusion.13
  186.9 6.3 %collective-permute-done.8 = bf16[2,32,5120]{2,1,0:T(8,128)(2,1)S(1)} collective-permute-done((bf16[2,32,5120]{2,1,0:T(8,128)(2,1)S(1)}, bf16[2,32,5120]{2,1,0:T(8,128)(2,1)S(1)}, u32[]{:S(2)}, u32[]{:S(2)}) %collective-permute-start.8) | collective-permute-done | bytes 655392 | tf_op jit(solution)/shard_map/ppermute | solution.py:8
  193.3 5.2 %collective-permute-done.9 = bf16[2,32,5120]{2,1,0:T(8,128)(2,1)S(1)} collective-permute-done((bf16[2,32,5120]{2,1,0:T(8,128)(2,1)S(1)}, bf16[2,32,5120]{2,1,0:T(8,128)(2,1)S(1)}, u32[]{:S(2)}, u32[]{:S(2)}) %collective-permute-start.9) | collective-permute-done | bytes 655392 | tf_op jit(solution)/shard_map/ppermute | solution.py:8
  198.7 6.9 %subtract_select_fusion = f32[512,5120]{1,0:T(8,128)S(1)} fusion(bf16[512,5120]{1,0:T(8,128)(2,1)S(1)} %bitcast.162, bf16[512,16384]{1,0:T(8,128)(2,1)} %copy-done, pred[5120]{0:T(1024)(128)(4,1)S(1)} %slice-done.2, bf16[512,256]{0,1:T(8,128)(2,1)S(1)} %copy-done.5, bf16[512,256]{0,1:T(8,128)(2,1)S(1)} %copy-done.6), kind=kOutput, calls=%fused_computation.4 | convolution fusion | flops 2693267456 | bytes 21500928 | tf_op jit(solution)/shard_map/dot_general | solution.py:174
  205.6 5.2 %fusion.60 = (f32[4,4,32,2560]{3,2,1,0:T(8,128)}, f32[4,4,32,2560]{3,2,1,0:T(8,128)}) fusion(f32[4,4,32,5120]{3,2,1,0:T(8,128)S(1)} %bitcast.159), kind=kLoop, calls=%fused_computation.146 | loop fusion | bytes 20971520 | tf_op jit(solution)/shard_map/slice | solution.py:65
  210.8 1.6 dynamic-slice_convert_fusion
  212.4 1.4 collective-permute-start.18
  213.8 1.9 collective-permute-start.20
  215.7 1.9 dynamic-slice_bitcast_fusion
  217.7 1.3 collective-permute-start.10
  219.0 2.0 collective-permute-start.12
  221.0 1.7 fusion.1
  222.9 1.5 maximum_bitcast_fusion.1
  224.7 1.5 collective-permute-start.21
  226.2 0.7 collective-permute-start.19
  227.0 2.4 collective-permute-start.13
  229.7 20.6 %collective-permute-done.21 = bf16[4,32,2560]{2,1,0:T(8,128)(2,1)S(1)} collective-permute-done((bf16[4,32,2560]{2,1,0:T(8,128)(2,1)S(1)}, bf16[4,32,2560]{2,1,0:T(8,128)(2,1)S(1)}, u32[]{:S(2)}, u32[]{:S(2)}) %collective-permute-start.21) | collective-permute-done | bytes 655392 | tf_op jit(solution)/shard_map/ppermute | solution.py:26
  250.3 2.5 collective-permute-done.19
  252.7 0.2 fusion.4
  253.0 0.9 collective-permute-start.22
  253.9 2.4 collective-permute-start.24
  256.3 0.2 fusion.5
  256.7 0.3 collective-permute-start.14
  257.0 3.0 %collective-permute-start.16 = (bf16[16,2560]{1,0:T(8,128)(2,1)S(1)}, bf16[16,2560]{1,0:T(8,128)(2,1)S(1)}, u32[]{:S(2)}, u32[]{:S(2)}) collective-permute-start(bf16[16,2560]{1,0:T(8,128)(2,1)S(1)} %get-tuple-element.40), channel_id=1, source_target_pairs={{0,96},{8,104},{16,112},{24,120},{32,0},{40,8},{48,16},{56,24},{64... | collective-permute-start | bytes 245768 | tf_op jit(solution)/shard_map/ppermute | solution.py:26
  260.0 2.9 %collective-permute-start.25 = (bf16[32,2560]{1,0:T(8,128)(2,1)S(1)}, bf16[32,2560]{1,0:T(8,128)(2,1)S(1)}, u32[]{:S(2)}, u32[]{:S(2)}) collective-permute-start(bf16[32,2560]{1,0:T(8,128)(2,1)S(1)} %pad_maximum_fusion.10), channel_id=1, source_target_pairs={{0,24},{8,0},{16,8},{24,16},{32,56},{40,32},{48,40},{56,48},{64,88... | collective-permute-start | bytes 491528 | tf_op jit(solution)/shard_map/ppermute | solution.py:26
  263.1 2.8 %collective-permute-start.17 = (bf16[32,2560]{1,0:T(8,128)(2,1)S(1)}, bf16[32,2560]{1,0:T(8,128)(2,1)S(1)}, u32[]{:S(2)}, u32[]{:S(2)}) collective-permute-start(bf16[32,2560]{1,0:T(8,128)(2,1)S(1)} %pad_maximum_fusion.8), channel_id=1, source_target_pairs={{0,96},{8,104},{16,112},{24,120},{32,0},{40,8},{48,16},{56,24},{64... | collective-permute-start | bytes 491528 | tf_op jit(solution)/shard_map/ppermute | solution.py:26
  266.1 3.5 %collective-permute-done.23 = bf16[32,2560]{1,0:T(8,128)(2,1)S(1)} collective-permute-done((bf16[32,2560]{1,0:T(8,128)(2,1)S(1)}, bf16[32,2560]{1,0:T(8,128)(2,1)S(1)}, u32[]{:S(2)}, u32[]{:S(2)}) %collective-permute-start.23) | collective-permute-done | bytes 163872 | tf_op jit(solution)/shard_map/ppermute | solution.py:26
  269.6 3.0 %collective-permute-done.15 = bf16[32,2560]{1,0:T(8,128)(2,1)S(1)} collective-permute-done((bf16[32,2560]{1,0:T(8,128)(2,1)S(1)}, bf16[32,2560]{1,0:T(8,128)(2,1)S(1)}, u32[]{:S(2)}, u32[]{:S(2)}) %collective-permute-start.15) | collective-permute-done | bytes 163872 | tf_op jit(solution)/shard_map/ppermute | solution.py:26
  272.7 1.2 convert_element_type.156
  273.9 1.5 maximum_bitcast_fusion
  (107 shorter events, 2.7 us)
Async XLA Ops:
  7.2 121.2 %all-gather.2.cloned.1.call-start = ((), (), s32[]{:S(2)}) async-start(), calls=%async_computation.1 | async-start | bytes 14417920 | tf_op jit(solution)/shard_map/all_gather | solution.py:103
  10.8 2.0 copy-start.1
  12.8 8.5 %copy-start.11 = (s32[1,2,64]{2,1,0:T(2,128)S(1)}, s32[1,2,64]{2,1,0:T(2,128)}, u32[]{:S(2)}) copy-start(s32[1,2,64]{2,1,0:T(2,128)} %param.10) | copy-start | bytes 1540
  14.6 258.1 %reduce-scatter.2.cloned.1.call-start = ((), (), s32[]{:S(2)}) async-start(), calls=%async_computation.2 | async-start | bytes 12255232 | tf_op jit(solution)/shard_map/reduce_scatter | solution.py:152
  15.6 38.9 %collective-permute-start.1 = (bf16[2,64,512]{2,1,0:T(8,128)(2,1)S(1)}, bf16[2,64,512]{2,1,0:T(8,128)(2,1)S(1)}, u32[]{:S(2)}, u32[]{:S(2)}) collective-permute-start(bf16[2,64,512]{2,1,0:T(8,128)(2,1)S(1)} %get-tuple-element.23), channel_id=1, source_target_pairs={{0,2},{2,4},{4,6},{6,0},{1,3},{3,5},{5,7},{7,1},{8,10},{10,12},{12... | collective-permute-start | bytes 393224 | tf_op jit(solution)/shard_map/ppermute | solution.py:8
  17.6 36.9 %collective-permute-start = (bf16[2,64,512]{2,1,0:T(8,128)(2,1)S(1)}, bf16[2,64,512]{2,1,0:T(8,128)(2,1)S(1)}, u32[]{:S(2)}, u32[]{:S(2)}) collective-permute-start(bf16[2,64,512]{2,1,0:T(8,128)(2,1)S(1)} %get-tuple-element.23), channel_id=1, source_target_pairs={{0,6},{2,0},{4,2},{6,4},{1,7},{3,1},{5,3},{7,5},{8,14},{10,8},{12,... | collective-permute-start | bytes 393224 | tf_op jit(solution)/shard_map/ppermute | solution.py:8
  36.5 17.7 %copy-start.7 = (bf16[1,2,256,256]{3,2,1,0:T(8,128)(2,1)S(1)}, bf16[1,2,256,256]{3,2,1,0:T(8,128)(2,1)}, u32[]{:S(2)}) copy-start(bf16[1,2,256,256]{3,2,1,0:T(8,128)(2,1)} %param.9) | copy-start | bytes 786436
  48.3 5.8 %copy-start = (bf16[512,16384]{1,0:T(8,128)(2,1)}, bf16[512,16384]{1,0:T(8,128)(2,1)S(1)}, u32[]{:S(2)}) copy-start(bf16[512,16384]{1,0:T(8,128)(2,1)S(1)} %bitcast_multiply_fusion) | copy-start | bytes 50331652
  54.5 7.1 %collective-permute-start.2 = (bf16[2,32,512]{2,1,0:T(8,128)(2,1)S(1)}, bf16[2,32,512]{2,1,0:T(8,128)(2,1)S(1)}, u32[]{:S(2)}, u32[]{:S(2)}) collective-permute-start(bf16[2,32,512]{2,1,0:T(8,128)(2,1)S(1)} %slice.320), channel_id=1, source_target_pairs={{0,2},{2,4},{4,6},{6,0},{1,3},{3,5},{5,7},{7,1},{8,10},{10,12},{12... | collective-permute-start | bytes 196616 | tf_op jit(solution)/shard_map/ppermute | solution.py:8
  54.6 7.0 %collective-permute-start.3 = (bf16[2,32,512]{2,1,0:T(8,128)(2,1)S(1)}, bf16[2,32,512]{2,1,0:T(8,128)(2,1)S(1)}, u32[]{:S(2)}, u32[]{:S(2)}) collective-permute-start(bf16[2,32,512]{2,1,0:T(8,128)(2,1)S(1)} %slice.321), channel_id=1, source_target_pairs={{0,6},{2,0},{4,2},{6,4},{1,7},{3,1},{5,3},{7,5},{8,14},{10,8},{12,... | collective-permute-start | bytes 196616 | tf_op jit(solution)/shard_map/ppermute | solution.py:8
  64.2 3.8 %collective-permute-start.4 = (bf16[512,512]{0,1:T(8,128)(2,1)S(1)}, bf16[512,512]{0,1:T(8,128)(2,1)S(1)}, u32[]{:S(2)}, u32[]{:S(2)}) collective-permute-start(bf16[512,512]{0,1:T(8,128)(2,1)S(1)} %pad_maximum_fusion.6), channel_id=1, source_target_pairs={{0,1},{2,3},{4,5},{6,7},{8,9},{10,11},{12,13},{14,15},{16,17},{18,... | collective-permute-start | bytes 1572872 | tf_op jit(solution)/shard_map/ppermute | solution.py:127
  65.7 2.3 collective-permute-start.5
  67.0 78.8 %copy-start.10 = (pred[16384]{0:T(1024)(128)(4,1)}, pred[16384]{0:T(1024)(128)(4,1)S(1)}, u32[]{:S(2)}) copy-start(pred[16384]{0:T(1024)(128)(4,1)S(1)} %add_compare_fusion) | copy-start | bytes 49156
  68.0 0.7 copy-start.9
  68.9 75.4 %copy-start.8 = (bf16[512,256]{0,1:T(8,128)(2,1)}, bf16[512,256]{0,1:T(8,128)(2,1)S(1)}, u32[]{:S(2)}) copy-start(bf16[512,256]{0,1:T(8,128)(2,1)S(1)} %subtract_convert_fusion) | copy-start | bytes 786436
  144.3 31.7 %collective-permute-start.7 = (bf16[2,64,5120]{2,1,0:T(8,128)(2,1)S(1)}, bf16[2,64,5120]{2,1,0:T(8,128)(2,1)S(1)}, u32[]{:S(2)}, u32[]{:S(2)}) collective-permute-start(bf16[2,64,5120]{2,1,0:T(8,128)(2,1)S(1)} %slice.313), channel_id=1, source_target_pairs={{0,2},{2,4},{4,6},{6,0},{1,3},{3,5},{5,7},{7,1},{8,10},{10,12},{12... | collective-permute-start | bytes 3932168 | tf_op jit(solution)/shard_map/ppermute | solution.py:8
  145.8 35.5 %collective-permute-start.6 = (bf16[2,64,5120]{2,1,0:T(8,128)(2,1)S(1)}, bf16[2,64,5120]{2,1,0:T(8,128)(2,1)}, u32[]{:S(2)}, u32[]{:S(2)}) collective-permute-start(bf16[2,64,5120]{2,1,0:T(8,128)(2,1)S(1)} %slice.313), channel_id=1, source_target_pairs={{0,6},{2,0},{4,2},{6,4},{1,7},{3,1},{5,3},{7,5},{8,14},{10,8},{12,... | collective-permute-start | bytes 3932168 | tf_op jit(solution)/shard_map/ppermute | solution.py:8
  176.0 17.2 %collective-permute-start.8 = (bf16[2,32,5120]{2,1,0:T(8,128)(2,1)S(1)}, bf16[2,32,5120]{2,1,0:T(8,128)(2,1)S(1)}, u32[]{:S(2)}, u32[]{:S(2)}) collective-permute-start(bf16[2,32,5120]{2,1,0:T(8,128)(2,1)S(1)} %slice.328), channel_id=1, source_target_pairs={{0,2},{2,4},{4,6},{6,0},{1,3},{3,5},{5,7},{7,1},{8,10},{10,12},{12... | collective-permute-start | bytes 1966088 | tf_op jit(solution)/shard_map/ppermute | solution.py:8
  181.3 17.4 %copy-start.5 = (bf16[512,256]{0,1:T(8,128)(2,1)S(1)}, bf16[512,256]{0,1:T(8,128)(2,1)}, u32[]{:S(2)}) copy-start(bf16[512,256]{0,1:T(8,128)(2,1)} %get-tuple-element.43) | copy-start | bytes 786436
  181.3 17.4 %copy-start.6 = (bf16[512,256]{0,1:T(8,128)(2,1)S(1)}, bf16[512,256]{0,1:T(8,128)(2,1)}, u32[]{:S(2)}) copy-start(bf16[512,256]{0,1:T(8,128)(2,1)} %get-tuple-element.44) | copy-start | bytes 786436
  181.3 17.4 %slice-start.2 = ((pred[16384]{0:T(1024)(128)(4,1)}), pred[5120]{0:T(1024)(128)(4,1)S(1)}, s32[]{:S(2)}) async-start(pred[16384]{0:T(1024)(128)(4,1)} %copy-done.10), calls=%async_computation.5 | async-start | bytes 10240 | tf_op jit(solution)/shard_map/slice | solution.py:179
  182.5 16.0 %collective-permute-start.9 = (bf16[2,32,5120]{2,1,0:T(8,128)(2,1)S(1)}, bf16[2,32,5120]{2,1,0:T(8,128)(2,1)S(1)}, u32[]{:S(2)}, u32[]{:S(2)}) collective-permute-start(bf16[2,32,5120]{2,1,0:T(8,128)(2,1)S(1)} %slice.329), channel_id=1, source_target_pairs={{0,6},{2,0},{4,2},{6,4},{1,7},{3,1},{5,3},{7,5},{8,14},{10,8},{12,... | collective-permute-start | bytes 1966088 | tf_op jit(solution)/shard_map/ppermute | solution.py:8
  198.6 7.0 %copy-start.3 = (bf16[2,256,5120]{2,1,0:T(8,128)(2,1)}, bf16[2,256,5120]{2,1,0:T(8,128)(2,1)S(1)}, u32[]{:S(2)}) copy-start(bf16[2,256,5120]{2,1,0:T(8,128)(2,1)S(1)} %constant_dynamic-update-slice_fusion.10) | copy-start | bytes 15728644
  210.8 10.2 %copy-start.4 = (bf16[2,256,5120]{2,1,0:T(8,128)(2,1)S(1)}, bf16[2,256,5120]{2,1,0:T(8,128)(2,1)}, u32[]{:S(2)}) copy-start(bf16[2,256,5120]{2,1,0:T(8,128)(2,1)} %copy-done.3) | copy-start | bytes 15728644
  210.8 11.9 %copy-start.2 = (f32[4,4,32,2560]{3,2,1,0:T(8,128)S(1)}, f32[4,4,32,2560]{3,2,1,0:T(8,128)}, u32[]{:S(2)}) copy-start(f32[4,4,32,2560]{3,2,1,0:T(8,128)} %get-tuple-element.15) | copy-start | bytes 15728644
  212.4 12.0 %collective-permute-start.18 = (bf16[2,32,2560]{2,1,0:T(8,128)(2,1)S(1)}, bf16[2,32,2560]{2,1,0:T(8,128)(2,1)S(1)}, u32[]{:S(2)}, u32[]{:S(2)}) collective-permute-start(bf16[2,32,2560]{2,1,0:T(8,128)(2,1)S(1)} %get-tuple-element.37), channel_id=1, source_target_pairs={{0,32},{8,40},{16,48},{24,56},{32,64},{40,72},{48,80},{56,88},{64,... | collective-permute-start | bytes 983048 | tf_op jit(solution)/shard_map/ppermute | solution.py:26
  213.8 10.7 %collective-permute-start.20 = (bf16[2,32,2560]{2,1,0:T(8,128)(2,1)S(1)}, bf16[2,32,2560]{2,1,0:T(8,128)(2,1)S(1)}, u32[]{:S(2)}, u32[]{:S(2)}) collective-permute-start(bf16[2,32,2560]{2,1,0:T(8,128)(2,1)S(1)} %get-tuple-element.38), channel_id=1, source_target_pairs={{0,96},{8,104},{16,112},{24,120},{32,0},{40,8},{48,16},{56,24},{64... | collective-permute-start | bytes 983048 | tf_op jit(solution)/shard_map/ppermute | solution.py:26
  217.7 11.8 %collective-permute-start.10 = (bf16[2,32,2560]{2,1,0:T(8,128)(2,1)S(1)}, bf16[2,32,2560]{2,1,0:T(8,128)(2,1)S(1)}, u32[]{:S(2)}, u32[]{:S(2)}) collective-permute-start(bf16[2,32,2560]{2,1,0:T(8,128)(2,1)S(1)} %get-tuple-element.35), channel_id=1, source_target_pairs={{0,8},{8,16},{16,24},{24,0},{32,40},{40,48},{48,56},{56,32},{64,72... | collective-permute-start | bytes 983048 | tf_op jit(solution)/shard_map/ppermute | solution.py:26
  219.0 5.4 %slice-start = ((s8[5242880]{0:T(1024)(128)(4,1)}), s8[4194304]{0:T(1024)(128)(4,1)S(1)}, s32[]{:S(2)}) async-start(s8[5242880]{0:T(1024)(128)(4,1)} %bitcast.160), calls=%async_computation.3 | async-start | bytes 8388608
  219.0 8.0 %collective-permute-start.12 = (bf16[2,32,2560]{2,1,0:T(8,128)(2,1)S(1)}, bf16[2,32,2560]{2,1,0:T(8,128)(2,1)S(1)}, u32[]{:S(2)}, u32[]{:S(2)}) collective-permute-start(bf16[2,32,2560]{2,1,0:T(8,128)(2,1)S(1)} %get-tuple-element.36), channel_id=1, source_target_pairs={{0,24},{8,0},{16,8},{24,16},{32,56},{40,32},{48,40},{56,48},{64,88... | collective-permute-start | bytes 983048 | tf_op jit(solution)/shard_map/ppermute | solution.py:26
  222.7 1.6 slice-start.1
  224.7 25.6 %collective-permute-start.21 = (bf16[4,32,2560]{2,1,0:T(8,128)(2,1)S(1)}, bf16[4,32,2560]{2,1,0:T(8,128)(2,1)S(1)}, u32[]{:S(2)}, u32[]{:S(2)}) collective-permute-start(bf16[4,32,2560]{2,1,0:T(8,128)(2,1)S(1)} %pad_maximum_fusion.3), channel_id=1, source_target_pairs={{0,96},{8,104},{16,112},{24,120},{32,0},{40,8},{48,16},{56,24},{64... | collective-permute-start | bytes 1966088 | tf_op jit(solution)/shard_map/ppermute | solution.py:26
  226.2 26.5 %collective-permute-start.19 = (bf16[4,32,2560]{2,1,0:T(8,128)(2,1)S(1)}, bf16[4,32,2560]{2,1,0:T(8,128)(2,1)S(1)}, u32[]{:S(2)}, u32[]{:S(2)}) collective-permute-start(bf16[4,32,2560]{2,1,0:T(8,128)(2,1)S(1)} %pad_maximum_fusion.2), channel_id=1, source_target_pairs={{0,32},{8,40},{16,48},{24,56},{32,64},{40,72},{48,80},{56,88},{64,... | collective-permute-start | bytes 1966088 | tf_op jit(solution)/shard_map/ppermute | solution.py:26
  227.0 29.3 %collective-permute-start.13 = (bf16[4,32,2560]{2,1,0:T(8,128)(2,1)S(1)}, bf16[4,32,2560]{2,1,0:T(8,128)(2,1)S(1)}, u32[]{:S(2)}, u32[]{:S(2)}) collective-permute-start(bf16[4,32,2560]{2,1,0:T(8,128)(2,1)S(1)} %pad_maximum_fusion.1), channel_id=1, source_target_pairs={{0,24},{8,0},{16,8},{24,16},{32,56},{40,32},{48,40},{56,48},{64,88... | collective-permute-start | bytes 1966088 | tf_op jit(solution)/shard_map/ppermute | solution.py:26
  229.6 26.7 %collective-permute-start.11 = (bf16[4,32,2560]{2,1,0:T(8,128)(2,1)S(1)}, bf16[4,32,2560]{2,1,0:T(8,128)(2,1)S(1)}, u32[]{:S(2)}, u32[]{:S(2)}) collective-permute-start(bf16[4,32,2560]{2,1,0:T(8,128)(2,1)S(1)} %pad_maximum_fusion), channel_id=1, source_target_pairs={{0,8},{8,16},{16,24},{24,0},{32,40},{40,48},{48,56},{56,32},{64,72... | collective-permute-start | bytes 1966088 | tf_op jit(solution)/shard_map/ppermute | solution.py:26
  253.0 7.0 %collective-permute-start.22 = (bf16[16,2560]{1,0:T(8,128)(2,1)S(1)}, bf16[16,2560]{1,0:T(8,128)(2,1)S(1)}, u32[]{:S(2)}, u32[]{:S(2)}) collective-permute-start(bf16[16,2560]{1,0:T(8,128)(2,1)S(1)} %get-tuple-element.41), channel_id=1, source_target_pairs={{0,8},{8,16},{16,24},{24,0},{32,40},{40,48},{48,56},{56,32},{64,72... | collective-permute-start | bytes 245768 | tf_op jit(solution)/shard_map/ppermute | solution.py:26
  253.9 6.1 %collective-permute-start.24 = (bf16[16,2560]{1,0:T(8,128)(2,1)S(1)}, bf16[16,2560]{1,0:T(8,128)(2,1)S(1)}, u32[]{:S(2)}, u32[]{:S(2)}) collective-permute-start(bf16[16,2560]{1,0:T(8,128)(2,1)S(1)} %get-tuple-element.42), channel_id=1, source_target_pairs={{0,24},{8,0},{16,8},{24,16},{32,56},{40,32},{48,40},{56,48},{64,88... | collective-permute-start | bytes 245768 | tf_op jit(solution)/shard_map/ppermute | solution.py:26
  256.7 6.4 %collective-permute-start.14 = (bf16[16,2560]{1,0:T(8,128)(2,1)S(1)}, bf16[16,2560]{1,0:T(8,128)(2,1)S(1)}, u32[]{:S(2)}, u32[]{:S(2)}) collective-permute-start(bf16[16,2560]{1,0:T(8,128)(2,1)S(1)} %get-tuple-element.39), channel_id=1, source_target_pairs={{0,32},{8,40},{16,48},{24,56},{32,64},{40,72},{48,80},{56,88},{64,... | collective-permute-start | bytes 245768 | tf_op jit(solution)/shard_map/ppermute | solution.py:26
  257.0 6.1 %collective-permute-start.16 = (bf16[16,2560]{1,0:T(8,128)(2,1)S(1)}, bf16[16,2560]{1,0:T(8,128)(2,1)S(1)}, u32[]{:S(2)}, u32[]{:S(2)}) collective-permute-start(bf16[16,2560]{1,0:T(8,128)(2,1)S(1)} %get-tuple-element.40), channel_id=1, source_target_pairs={{0,96},{8,104},{16,112},{24,120},{32,0},{40,8},{48,16},{56,24},{64... | collective-permute-start | bytes 245768 | tf_op jit(solution)/shard_map/ppermute | solution.py:26
  260.0 6.0 %collective-permute-start.25 = (bf16[32,2560]{1,0:T(8,128)(2,1)S(1)}, bf16[32,2560]{1,0:T(8,128)(2,1)S(1)}, u32[]{:S(2)}, u32[]{:S(2)}) collective-permute-start(bf16[32,2560]{1,0:T(8,128)(2,1)S(1)} %pad_maximum_fusion.10), channel_id=1, source_target_pairs={{0,24},{8,0},{16,8},{24,16},{32,56},{40,32},{48,40},{56,48},{64,88... | collective-permute-start | bytes 491528 | tf_op jit(solution)/shard_map/ppermute | solution.py:26
  263.0 6.6 %collective-permute-start.23 = (bf16[32,2560]{1,0:T(8,128)(2,1)S(1)}, bf16[32,2560]{1,0:T(8,128)(2,1)S(1)}, u32[]{:S(2)}, u32[]{:S(2)}) collective-permute-start(bf16[32,2560]{1,0:T(8,128)(2,1)S(1)} %pad_maximum_fusion.9), channel_id=1, source_target_pairs={{0,8},{8,16},{16,24},{24,0},{32,40},{40,48},{48,56},{56,32},{64,72... | collective-permute-start | bytes 491528 | tf_op jit(solution)/shard_map/ppermute | solution.py:26
  263.1 6.5 %collective-permute-start.17 = (bf16[32,2560]{1,0:T(8,128)(2,1)S(1)}, bf16[32,2560]{1,0:T(8,128)(2,1)S(1)}, u32[]{:S(2)}, u32[]{:S(2)}) collective-permute-start(bf16[32,2560]{1,0:T(8,128)(2,1)S(1)} %pad_maximum_fusion.8), channel_id=1, source_target_pairs={{0,96},{8,104},{16,112},{24,120},{32,0},{40,8},{48,16},{56,24},{64... | collective-permute-start | bytes 491528 | tf_op jit(solution)/shard_map/ppermute | solution.py:26
  266.0 6.6 %collective-permute-start.15 = (bf16[32,2560]{1,0:T(8,128)(2,1)S(1)}, bf16[32,2560]{1,0:T(8,128)(2,1)S(1)}, u32[]{:S(2)}, u32[]{:S(2)}) collective-permute-start(bf16[32,2560]{1,0:T(8,128)(2,1)S(1)} %pad_maximum_fusion.7), channel_id=1, source_target_pairs={{0,32},{8,40},{16,48},{24,56},{32,64},{40,72},{48,80},{56,88},{64,... | collective-permute-start | bytes 491528 | tf_op jit(solution)/shard_map/ppermute | solution.py:26
Sparse Core Ops, SparseCore 0:
  14.7 113.6 all-gather.1
  151.6 101.0 reduce-scatter.1

commit v3 on v2

--- a/solution.py
+++ b/solution.py
@@ -99,7 +99,7 @@
     n_prow = lax.axis_size("prow")
     n_pcol = lax.axis_size("pcol")
     assert n_prow == 4
-    half = (col_count * 11 // 16) // block_size * block_size
+    half = (col_count * 10 // 16) // block_size * block_size
     gathered = lax.all_gather(pivot_masked[:, :, :half], "prow", axis=1, tiled=True)
     later_cols, gathered = lax.optimization_barrier((pivot_masked[:, :, half:], gathered))
     panel = jnp.roll(

time: 283 us -> 308 us (1.088)
  local copies, waits for them, and re-layouts: 42.6 us -> 54.1 us
  matrix products: 31.3 us -> 36.6 us
  waiting for transfers between devices: 130 us -> 134 us
    ppermute x16, waiting for transfers between devices: 29.5 us -> 41.5 us  [grid_shift(): return lax.ppermute(value, axis, pairs)]
    all_gather x1, waiting for transfers between devices: 59.5 us -> 48.5 us  [on_device(): lax.all_gather(pivot_masked[:, :, :half], 'prow', axis=1, tiled=True)]
    unnamed x45 -> x41, local copies, waits for them, and re-layouts: 24.6 us -> 32.3 us
    dot_general x1, matrix products: 6.94 us -> 10.7 us  [on_device(): jnp.dot(multipliers_rel, gathered_rel.reshape(2 * block_size, col_count -...]
    ppermute x8, waiting for transfers between devices: 39.7 us -> 43.4 us  [ring(): lax.ppermute(value, axis, [(i, (i + step) % size) for i in range(size)])]
    slice x1, local copies, waits for them, and re-layouts: 5.16 us -> 8.62 us  [grid_reduce_scatter(): left = grid[..., :width // 2]]
  transfers between devices with their start and end apart: 28 -> 28, of which waited for: 10 -> 18; matrix products, arithmetic and copies ran while one was open for 23% -> 27% of each run, Pallas kernels for 0% -> 0%
where the time goes in v3:
time: 308 us; the launch traced here: 304 us
  waiting for transfers between devices  134 us (44%)
  local copies, waits for them, and re-layouts  54.1 us (18%)
  starting transfers between devices  41.8 us (14%)
  matrix products  36.6 us (12%)
  other arithmetic  22.9 us (7%)
  between operations  14.7 us (5%)
    all_gather x1, waiting for transfers between devices, on_device(): lax.all_gather(pivot_masked[:, :, :half], 'prow', axis=1, tiled=True)  48.5 us
    ppermute x8, waiting for transfers between devices, ring(): lax.ppermute(value, axis, [(i, (i + step) % size) for i in range(size)])  43.4 us
    ppermute x16, waiting for transfers between devices, grid_shift(): return lax.ppermute(value, axis, pairs)  41.5 us
    unnamed x41, local copies, waits for them, and re-layouts  32.3 us
    ppermute x16, starting transfers between devices, grid_shift(): return lax.ppermute(value, axis, pairs)  24.9 us
    dot_general x1, matrix products, on_device(): jnp.dot(multipliers, gathered.reshape(2 * block_size, half), preferred_el...  14.7 us
    ppermute x8, starting transfers between devices, ring(): lax.ppermute(value, axis, [(i, (i + step) % size) for i in range(size)])  14.2 us
    mul x1, other arithmetic, on_device(): front[0]  11.8 us
  transfers between devices with their start and end apart: 28, of which 18 were waited for; matrix products, arithmetic and copies ran while one was open for 27% of the time, Pallas kernels for 0%

profile of v3, /device:TPU:0, one launch (start us, length us, event | category | flops | bytes accessed | tf_op | source)
XLA Modules:
  0.0 304.4 jit_solution(7121621436375573634)
XLA Ops:
  8.1 2.7 bitcast_multiply_fusion.1
  10.8 2.0 copy-done.1
  12.8 1.7 slice.314
  14.5 0.9 fusion.61
  15.4 2.1 collective-permute-start.1
  17.5 2.2 collective-permute-start
  19.7 1.5 slice.313
  21.3 2.7 mul.35
  24.0 12.5 %copy.14 = bf16[64,8,64,256]{3,1,2,0:T(8,128)(2,1)} copy(bf16[64,8,64,256]{3,2,1,0:T(8,128)(2,1)S(1)} %bitcast.158) | data formatting | bytes 33554432
  36.5 11.8 %bitcast_multiply_fusion = bf16[512,16384]{1,0:T(8,128)(2,1)S(1)} fusion(bf16[512,16384]{1,0:T(8,128)(2,1)} %bitcast.157, bf16[1,512,16384]{2,1,0:T(8,128)(2,1)} %param.7), kind=kLoop, calls=%fused_computation.1 | loop fusion | flops 8388608 | bytes 50331648 | tf_op jit(solution)/shard_map/mul | solution.py:88
  48.4 5.8 %copy-done = bf16[512,16384]{1,0:T(8,128)(2,1)} copy-done((bf16[512,16384]{1,0:T(8,128)(2,1)}, bf16[512,16384]{1,0:T(8,128)(2,1)S(1)}, u32[]{:S(2)}) %copy-start) | copy-done | bytes 16777240
  54.6 3.3 %collective-permute-start.3 = (bf16[2,32,512]{2,1,0:T(8,128)(2,1)S(1)}, bf16[2,32,512]{2,1,0:T(8,128)(2,1)S(1)}, u32[]{:S(2)}, u32[]{:S(2)}) collective-permute-start(bf16[2,32,512]{2,1,0:T(8,128)(2,1)S(1)} %slice.321), channel_id=1, source_target_pairs={{0,6},{2,0},{4,2},{6,4},{1,7},{3,1},{5,3},{7,5},{8,14},{10,8},{12,... | collective-permute-start | bytes 196616 | tf_op jit(solution)/shard_map/ppermute | solution.py:8
  57.9 3.7 %collective-permute-done.2 = bf16[2,32,512]{2,1,0:T(8,128)(2,1)S(1)} collective-permute-done((bf16[2,32,512]{2,1,0:T(8,128)(2,1)S(1)}, bf16[2,32,512]{2,1,0:T(8,128)(2,1)S(1)}, u32[]{:S(2)}, u32[]{:S(2)}) %collective-permute-start.2) | collective-permute-done | bytes 65568 | tf_op jit(solution)/shard_map/ppermute | solution.py:8
  61.7 0.9 constant_dynamic-update-slice_fusion.4
  63.4 1.5 convolution_convert_fusion
  65.0 1.3 collective-permute-start.4
  66.3 1.1 convolution_convert_fusion.2
  67.4 1.3 collective-permute-start.5
  68.8 0.9 collective-permute-done.5
  71.0 48.5 %all-gather.2.cloned.1.call-done = bf16[2,256,10240]{2,1,0:T(8,128)(2,1)} async-done(((bf16[2,64,10240]{2,1,0:T(8,128)(2,1)}), bf16[2,256,10240]{2,1,0:T(8,128)(2,1)}) %all-gather.2.cloned.1.call-update) | async-done | bytes 10485776 | tf_op jit(solution)/shard_map/all_gather | solution.py:103
  119.4 14.7 %select_convert_fusion = bf16[512,10240]{1,0:T(8,128)(2,1)} fusion(bf16[512,10240]{1,0:T(8,128)(2,1)} %bitcast.164, bf16[512,16384]{1,0:T(8,128)(2,1)} %copy-done, pred[10240]{0:T(1024)(128)(4,1)S(1)} %slice.315, bf16[512,256]{0,1:T(8,128)(2,1)S(1)} %slice.324, bf16[512,256]{0,1:T(8,128)(2,1)S(1)} %subtract_convert_fusion), kind=kOutput, calls=%fused_computation | convolution fusion | flops 5390729216 | bytes 31991808 | tf_op jit(solution)/shard_map/dot_general | solution.py:145
  134.1 1.6 collective-permute-start.7
  135.7 1.7 collective-permute-start.6
  137.4 2.0 copy.11
  139.4 2.0 fusion.25
  141.4 1.3 constant_dynamic-update-slice_fusion.14
  142.7 28.8 %collective-permute-done.7 = bf16[2,64,6144]{2,1,0:T(8,128)(2,1)S(1)} collective-permute-done((bf16[2,64,6144]{2,1,0:T(8,128)(2,1)S(1)}, bf16[2,64,6144]{2,1,0:T(8,128)(2,1)S(1)}, u32[]{:S(2)}, u32[]{:S(2)}) %collective-permute-start.7) | collective-permute-done | bytes 1572896 | tf_op jit(solution)/shard_map/ppermute | solution.py:8
  171.5 0.9 slice.328
  172.8 5.0 %fusion = bf16[64,10240]{1,0:T(8,128)(2,1)} fusion(bf16[64,256]{1,0:T(8,128)(2,1)S(1)} %constant_dynamic-slice_fusion, bf16[2,256,10240]{2,1,0:T(8,128)(2,1)} %all-gather.2.cloned.1.call-done, bf16[2,64,16384]{2,1,0:T(8,128)(2,1)} %copy-done.1), kind=kOutput, calls=%fused_computation.4 | convolution fusion | flops 337510400 | bytes 7897088 | tf_op jit(solution)/shard_map/dot_general | solution.py:161
  177.8 1.2 slice.329
  179.0 3.0 collective-permute-start.9
  182.0 2.7 constant_dynamic-update-slice_fusion.13
  184.7 7.7 %collective-permute-done.8 = bf16[2,32,6144]{2,1,0:T(8,128)(2,1)} collective-permute-done((bf16[2,32,6144]{2,1,0:T(8,128)(2,1)}, bf16[2,32,6144]{2,1,0:T(8,128)(2,1)}, u32[]{:S(2)}, u32[]{:S(2)}) %collective-permute-start.8) | collective-permute-done | bytes 786464 | tf_op jit(solution)/shard_map/ppermute | solution.py:8
  192.3 2.1 constant_dynamic-update-slice_fusion.12
  194.4 3.2 %collective-permute-done.9 = bf16[2,32,6144]{2,1,0:T(8,128)(2,1)S(1)} collective-permute-done((bf16[2,32,6144]{2,1,0:T(8,128)(2,1)S(1)}, bf16[2,32,6144]{2,1,0:T(8,128)(2,1)S(1)}, u32[]{:S(2)}, u32[]{:S(2)}) %collective-permute-start.9) | collective-permute-done | bytes 786464 | tf_op jit(solution)/shard_map/ppermute | solution.py:8
  197.6 0.9 constant_dynamic-update-slice_fusion.11
  198.6 1.3 constant_dynamic-update-slice_fusion.10
  199.8 10.7 %subtract_select_fusion = f32[512,6144]{1,0:T(8,128)} fusion(bf16[512,6144]{1,0:T(8,128)(2,1)} %bitcast.162, bf16[512,16384]{1,0:T(8,128)(2,1)} %copy-done, pred[6144]{0:T(1024)(128)(4,1)S(1)} %slice-done.2, bf16[512,256]{0,1:T(8,128)(2,1)S(1)} %get-tuple-element.43, bf16[512,256]{0,1:T(8,128)(2,1)S(1)} %copy-done.4), kind=kOutput, calls=%fused_computation.2 | convolution fusion | flops 3231711232 | bytes 25696256 | tf_op jit(solution)/shard_map/dot_general | solution.py:174
  210.6 8.6 %fusion.60 = (f32[4,4,32,3072]{3,2,1,0:T(8,128)S(1)}, f32[4,4,32,3072]{3,2,1,0:T(8,128)}) fusion(f32[4,4,32,6144]{3,2,1,0:T(8,128)} %bitcast.159), kind=kLoop, calls=%fused_computation.146 | loop fusion | bytes 25165824 | tf_op jit(solution)/shard_map/slice | solution.py:65
  219.2 1.6 dynamic-slice_convert_fusion
  220.8 1.7 collective-permute-start.18
  222.5 1.6 collective-permute-start.20
  224.1 3.0 fusion.1
  228.5 1.5 maximum_bitcast_fusion.1
  229.9 1.6 collective-permute-start.10
  231.6 1.7 collective-permute-start.12
  233.4 8.0 %collective-permute-done.18 = bf16[2,32,3072]{2,1,0:T(8,128)(2,1)S(1)} collective-permute-done((bf16[2,32,3072]{2,1,0:T(8,128)(2,1)S(1)}, bf16[2,32,3072]{2,1,0:T(8,128)(2,1)S(1)}, u32[]{:S(2)}, u32[]{:S(2)}) %collective-permute-start.18) | collective-permute-done | bytes 393248 | tf_op jit(solution)/shard_map/ppermute | solution.py:26
  241.9 2.5 collective-permute-start.21
  244.6 2.8 collective-permute-done.12
  247.6 3.5 %collective-permute-start.13 = (bf16[4,32,3072]{2,1,0:T(8,128)(2,1)S(1)}, bf16[4,32,3072]{2,1,0:T(8,128)(2,1)S(1)}, u32[]{:S(2)}, u32[]{:S(2)}) collective-permute-start(bf16[4,32,3072]{2,1,0:T(8,128)(2,1)S(1)} %pad_maximum_fusion.1), channel_id=1, source_target_pairs={{0,24},{8,0},{16,8},{24,16},{32,56},{40,32},{48,40},{56,48},{64,88... | collective-permute-start | bytes 2359304 | tf_op jit(solution)/shard_map/ppermute | solution.py:26
  251.4 12.0 %collective-permute-done.21 = bf16[4,32,3072]{2,1,0:T(8,128)(2,1)S(1)} collective-permute-done((bf16[4,32,3072]{2,1,0:T(8,128)(2,1)S(1)}, bf16[4,32,3072]{2,1,0:T(8,128)(2,1)S(1)}, u32[]{:S(2)}, u32[]{:S(2)}) %collective-permute-start.21) | collective-permute-done | bytes 786464 | tf_op jit(solution)/shard_map/ppermute | solution.py:26
  263.4 1.1 collective-permute-done.19
  264.8 1.3 collective-permute-start.22
  266.1 2.0 collective-permute-start.24
  268.2 6.4 %collective-permute-done.13 = bf16[4,32,3072]{2,1,0:T(8,128)(2,1)S(1)} collective-permute-done((bf16[4,32,3072]{2,1,0:T(8,128)(2,1)S(1)}, bf16[4,32,3072]{2,1,0:T(8,128)(2,1)S(1)}, u32[]{:S(2)}, u32[]{:S(2)}) %collective-permute-start.13) | collective-permute-done | bytes 786464 | tf_op jit(solution)/shard_map/ppermute | solution.py:26
  274.6 3.7 %collective-permute-done.11 = bf16[4,32,3072]{2,1,0:T(8,128)(2,1)S(1)} collective-permute-done((bf16[4,32,3072]{2,1,0:T(8,128)(2,1)S(1)}, bf16[4,32,3072]{2,1,0:T(8,128)(2,1)S(1)}, u32[]{:S(2)}, u32[]{:S(2)}) %collective-permute-start.11) | collective-permute-done | bytes 786464 | tf_op jit(solution)/shard_map/ppermute | solution.py:26
  278.7 3.2 %collective-permute-start.16 = (bf16[16,3072]{1,0:T(8,128)(2,1)S(1)}, bf16[16,3072]{1,0:T(8,128)(2,1)S(1)}, u32[]{:S(2)}, u32[]{:S(2)}) collective-permute-start(bf16[16,3072]{1,0:T(8,128)(2,1)S(1)} %get-tuple-element.40), channel_id=1, source_target_pairs={{0,96},{8,104},{16,112},{24,120},{32,0},{40,8},{48,16},{56,24},{64... | collective-permute-start | bytes 294920 | tf_op jit(solution)/shard_map/ppermute | solution.py:26
  282.6 1.7 collective-permute-start.23
  284.6 3.3 %collective-permute-start.17 = (bf16[32,3072]{1,0:T(8,128)(2,1)S(1)}, bf16[32,3072]{1,0:T(8,128)(2,1)S(1)}, u32[]{:S(2)}, u32[]{:S(2)}) collective-permute-start(bf16[32,3072]{1,0:T(8,128)(2,1)S(1)} %pad_maximum_fusion.8), channel_id=1, source_target_pairs={{0,96},{8,104},{16,112},{24,120},{32,0},{40,8},{48,16},{56,24},{64... | collective-permute-start | bytes 589832 | tf_op jit(solution)/shard_map/ppermute | solution.py:26
  288.0 1.5 collective-permute-done.23
  289.6 1.5 collective-permute-done.17
  291.1 3.8 %collective-permute-done.15 = bf16[32,3072]{1,0:T(8,128)(2,1)S(1)} collective-permute-done((bf16[32,3072]{1,0:T(8,128)(2,1)S(1)}, bf16[32,3072]{1,0:T(8,128)(2,1)S(1)}, u32[]{:S(2)}, u32[]{:S(2)}) %collective-permute-start.15) | collective-permute-done | bytes 196640 | tf_op jit(solution)/shard_map/ppermute | solution.py:26
  295.0 1.2 convert_element_type.156
  296.1 1.5 maximum_bitcast_fusion
  (103 shorter events, 8.3 us)
Async XLA Ops:
  7.2 112.3 %all-gather.2.cloned.1.call-start = ((), (), s32[]{:S(2)}) async-start(), calls=%async_computation.1 | async-start | bytes 13107200 | tf_op jit(solution)/shard_map/all_gather | solution.py:103
  10.8 2.0 copy-start.1
  12.8 8.5 %copy-start.9 = (s32[1,2,64]{2,1,0:T(2,128)S(1)}, s32[1,2,64]{2,1,0:T(2,128)}, u32[]{:S(2)}) copy-start(s32[1,2,64]{2,1,0:T(2,128)} %param.10) | copy-start | bytes 1540
  14.5 280.5 %reduce-scatter.2.cloned.1.call-start = ((), (), s32[]{:S(2)}) async-start(), calls=%async_computation.2 | async-start | bytes 11141120 | tf_op jit(solution)/shard_map/reduce_scatter | solution.py:152
  15.4 39.0 %collective-permute-start.1 = (bf16[2,64,512]{2,1,0:T(8,128)(2,1)S(1)}, bf16[2,64,512]{2,1,0:T(8,128)(2,1)S(1)}, u32[]{:S(2)}, u32[]{:S(2)}) collective-permute-start(bf16[2,64,512]{2,1,0:T(8,128)(2,1)S(1)} %get-tuple-element.23), channel_id=1, source_target_pairs={{0,2},{2,4},{4,6},{6,0},{1,3},{3,5},{5,7},{7,1},{8,10},{10,12},{12... | collective-permute-start | bytes 393224 | tf_op jit(solution)/shard_map/ppermute | solution.py:8
  17.5 37.1 %collective-permute-start = (bf16[2,64,512]{2,1,0:T(8,128)(2,1)S(1)}, bf16[2,64,512]{2,1,0:T(8,128)(2,1)S(1)}, u32[]{:S(2)}, u32[]{:S(2)}) collective-permute-start(bf16[2,64,512]{2,1,0:T(8,128)(2,1)S(1)} %get-tuple-element.23), channel_id=1, source_target_pairs={{0,6},{2,0},{4,2},{6,4},{1,7},{3,1},{5,3},{7,5},{8,14},{10,8},{12,... | collective-permute-start | bytes 393224 | tf_op jit(solution)/shard_map/ppermute | solution.py:8
  36.5 17.7 %copy-start.6 = (bf16[1,2,256,256]{3,2,1,0:T(8,128)(2,1)S(1)}, bf16[1,2,256,256]{3,2,1,0:T(8,128)(2,1)}, u32[]{:S(2)}) copy-start(bf16[1,2,256,256]{3,2,1,0:T(8,128)(2,1)} %param.9) | copy-start | bytes 786436
  48.4 5.8 %copy-start = (bf16[512,16384]{1,0:T(8,128)(2,1)}, bf16[512,16384]{1,0:T(8,128)(2,1)S(1)}, u32[]{:S(2)}) copy-start(bf16[512,16384]{1,0:T(8,128)(2,1)S(1)} %bitcast_multiply_fusion) | copy-start | bytes 50331652
  54.5 7.1 %collective-permute-start.2 = (bf16[2,32,512]{2,1,0:T(8,128)(2,1)S(1)}, bf16[2,32,512]{2,1,0:T(8,128)(2,1)S(1)}, u32[]{:S(2)}, u32[]{:S(2)}) collective-permute-start(bf16[2,32,512]{2,1,0:T(8,128)(2,1)S(1)} %slice.320), channel_id=1, source_target_pairs={{0,2},{2,4},{4,6},{6,0},{1,3},{3,5},{5,7},{7,1},{8,10},{10,12},{12... | collective-permute-start | bytes 196616 | tf_op jit(solution)/shard_map/ppermute | solution.py:8
  54.6 7.0 %collective-permute-start.3 = (bf16[2,32,512]{2,1,0:T(8,128)(2,1)S(1)}, bf16[2,32,512]{2,1,0:T(8,128)(2,1)S(1)}, u32[]{:S(2)}, u32[]{:S(2)}) collective-permute-start(bf16[2,32,512]{2,1,0:T(8,128)(2,1)S(1)} %slice.321), channel_id=1, source_target_pairs={{0,6},{2,0},{4,2},{6,4},{1,7},{3,1},{5,3},{7,5},{8,14},{10,8},{12,... | collective-permute-start | bytes 196616 | tf_op jit(solution)/shard_map/ppermute | solution.py:8
  65.0 4.7 %collective-permute-start.4 = (bf16[512,512]{0,1:T(8,128)(2,1)S(1)}, bf16[512,512]{0,1:T(8,128)(2,1)S(1)}, u32[]{:S(2)}, u32[]{:S(2)}) collective-permute-start(bf16[512,512]{0,1:T(8,128)(2,1)S(1)} %pad_maximum_fusion.6), channel_id=1, source_target_pairs={{0,1},{2,3},{4,5},{6,7},{8,9},{10,11},{12,13},{14,15},{16,17},{18,... | collective-permute-start | bytes 1572872 | tf_op jit(solution)/shard_map/ppermute | solution.py:127
  67.4 2.3 collective-permute-start.5
  68.8 68.6 %copy-start.8 = (pred[16384]{0:T(1024)(128)(4,1)}, pred[16384]{0:T(1024)(128)(4,1)S(1)}, u32[]{:S(2)}) copy-start(pred[16384]{0:T(1024)(128)(4,1)S(1)} %add_compare_fusion) | copy-start | bytes 49156
  69.9 0.8 copy-start.3
  70.7 63.4 %copy-start.5 = (bf16[512,256]{0,1:T(8,128)(2,1)}, bf16[512,256]{0,1:T(8,128)(2,1)S(1)}, u32[]{:S(2)}) copy-start(bf16[512,256]{0,1:T(8,128)(2,1)S(1)} %slice.324) | copy-start | bytes 786436
  70.9 63.2 %copy-start.7 = (bf16[512,256]{0,1:T(8,128)(2,1)}, bf16[512,256]{0,1:T(8,128)(2,1)S(1)}, u32[]{:S(2)}) copy-start(bf16[512,256]{0,1:T(8,128)(2,1)S(1)} %subtract_convert_fusion) | copy-start | bytes 786436
  134.1 37.3 %collective-permute-start.7 = (bf16[2,64,6144]{2,1,0:T(8,128)(2,1)S(1)}, bf16[2,64,6144]{2,1,0:T(8,128)(2,1)S(1)}, u32[]{:S(2)}, u32[]{:S(2)}) collective-permute-start(bf16[2,64,6144]{2,1,0:T(8,128)(2,1)S(1)} %slice.313), channel_id=1, source_target_pairs={{0,2},{2,4},{4,6},{6,0},{1,3},{3,5},{5,7},{7,1},{8,10},{10,12},{12... | collective-permute-start | bytes 4718600 | tf_op jit(solution)/shard_map/ppermute | solution.py:8
  135.7 42.1 %collective-permute-start.6 = (bf16[2,64,6144]{2,1,0:T(8,128)(2,1)S(1)}, bf16[2,64,6144]{2,1,0:T(8,128)(2,1)}, u32[]{:S(2)}, u32[]{:S(2)}) collective-permute-start(bf16[2,64,6144]{2,1,0:T(8,128)(2,1)S(1)} %slice.313), channel_id=1, source_target_pairs={{0,6},{2,0},{4,2},{6,4},{1,7},{3,1},{5,3},{7,5},{8,14},{10,8},{12,... | collective-permute-start | bytes 4718600 | tf_op jit(solution)/shard_map/ppermute | solution.py:8
  172.4 19.9 %collective-permute-start.8 = (bf16[2,32,6144]{2,1,0:T(8,128)(2,1)}, bf16[2,32,6144]{2,1,0:T(8,128)(2,1)}, u32[]{:S(2)}, u32[]{:S(2)}) collective-permute-start(bf16[2,32,6144]{2,1,0:T(8,128)(2,1)} %slice.328), channel_id=1, source_target_pairs={{0,2},{2,4},{4,6},{6,0},{1,3},{3,5},{5,7},{7,1},{8,10},{10,12},{12... | collective-permute-start | bytes 2359304 | tf_op jit(solution)/shard_map/ppermute | solution.py:8
  177.7 22.1 %copy-start.4 = (bf16[512,256]{0,1:T(8,128)(2,1)S(1)}, bf16[512,256]{0,1:T(8,128)(2,1)}, u32[]{:S(2)}) copy-start(bf16[512,256]{0,1:T(8,128)(2,1)} %get-tuple-element.44) | copy-start | bytes 786436
  177.7 22.1 %slice-start.2 = ((pred[16384]{0:T(1024)(128)(4,1)}), pred[6144]{0:T(1024)(128)(4,1)S(1)}, s32[]{:S(2)}) async-start(pred[16384]{0:T(1024)(128)(4,1)} %copy-done.8), calls=%async_computation.5 | async-start | bytes 12288 | tf_op jit(solution)/shard_map/slice | solution.py:179
  179.0 18.6 %collective-permute-start.9 = (bf16[2,32,6144]{2,1,0:T(8,128)(2,1)S(1)}, bf16[2,32,6144]{2,1,0:T(8,128)(2,1)S(1)}, u32[]{:S(2)}, u32[]{:S(2)}) collective-permute-start(bf16[2,32,6144]{2,1,0:T(8,128)(2,1)S(1)} %slice.329), channel_id=1, source_target_pairs={{0,6},{2,0},{4,2},{6,4},{1,7},{3,1},{5,3},{7,5},{8,14},{10,8},{12,... | collective-permute-start | bytes 2359304 | tf_op jit(solution)/shard_map/ppermute | solution.py:8
  220.8 20.5 %collective-permute-start.18 = (bf16[2,32,3072]{2,1,0:T(8,128)(2,1)S(1)}, bf16[2,32,3072]{2,1,0:T(8,128)(2,1)S(1)}, u32[]{:S(2)}, u32[]{:S(2)}) collective-permute-start(bf16[2,32,3072]{2,1,0:T(8,128)(2,1)S(1)} %get-tuple-element.37), channel_id=1, source_target_pairs={{0,32},{8,40},{16,48},{24,56},{32,64},{40,72},{48,80},{56,88},{64,... | collective-permute-start | bytes 1179656 | tf_op jit(solution)/shard_map/ppermute | solution.py:26
  222.5 19.2 %collective-permute-start.20 = (bf16[2,32,3072]{2,1,0:T(8,128)(2,1)S(1)}, bf16[2,32,3072]{2,1,0:T(8,128)(2,1)S(1)}, u32[]{:S(2)}, u32[]{:S(2)}) collective-permute-start(bf16[2,32,3072]{2,1,0:T(8,128)(2,1)S(1)} %get-tuple-element.38), channel_id=1, source_target_pairs={{0,96},{8,104},{16,112},{24,120},{32,0},{40,8},{48,16},{56,24},{64... | collective-permute-start | bytes 1179656 | tf_op jit(solution)/shard_map/ppermute | solution.py:26
  224.1 9.1 %slice-start = ((s8[6291456]{0:T(1024)(128)(4,1)}), s8[4194304]{0:T(1024)(128)(4,1)S(1)}, s32[]{:S(2)}) async-start(s8[6291456]{0:T(1024)(128)(4,1)} %bitcast.160), calls=%async_computation.3 | async-start | bytes 8388608
  227.1 1.3 copy-start.2
  227.3 6.0 %slice-start.1 = ((s8[6291456]{0:T(1024)(128)(4,1)}), s8[2097152]{0:T(1024)(128)(4,1)S(1)}, s32[]{:S(2)}) async-start(s8[6291456]{0:T(1024)(128)(4,1)} %bitcast.160), calls=%async_computation.4 | async-start | bytes 4194304
  229.9 21.2 %collective-permute-start.10 = (bf16[2,32,3072]{2,1,0:T(8,128)(2,1)S(1)}, bf16[2,32,3072]{2,1,0:T(8,128)(2,1)S(1)}, u32[]{:S(2)}, u32[]{:S(2)}) collective-permute-start(bf16[2,32,3072]{2,1,0:T(8,128)(2,1)S(1)} %get-tuple-element.35), channel_id=1, source_target_pairs={{0,8},{8,16},{16,24},{24,0},{32,40},{40,48},{48,56},{56,32},{64,72... | collective-permute-start | bytes 1179656 | tf_op jit(solution)/shard_map/ppermute | solution.py:26
  231.6 15.9 %collective-permute-start.12 = (bf16[2,32,3072]{2,1,0:T(8,128)(2,1)S(1)}, bf16[2,32,3072]{2,1,0:T(8,128)(2,1)S(1)}, u32[]{:S(2)}, u32[]{:S(2)}) collective-permute-start(bf16[2,32,3072]{2,1,0:T(8,128)(2,1)S(1)} %get-tuple-element.36), channel_id=1, source_target_pairs={{0,24},{8,0},{16,8},{24,16},{32,56},{40,32},{48,40},{56,48},{64,88... | collective-permute-start | bytes 1179656 | tf_op jit(solution)/shard_map/ppermute | solution.py:26
  241.9 21.4 %collective-permute-start.21 = (bf16[4,32,3072]{2,1,0:T(8,128)(2,1)S(1)}, bf16[4,32,3072]{2,1,0:T(8,128)(2,1)S(1)}, u32[]{:S(2)}, u32[]{:S(2)}) collective-permute-start(bf16[4,32,3072]{2,1,0:T(8,128)(2,1)S(1)} %pad_maximum_fusion.3), channel_id=1, source_target_pairs={{0,96},{8,104},{16,112},{24,120},{32,0},{40,8},{48,16},{56,24},{64... | collective-permute-start | bytes 2359304 | tf_op jit(solution)/shard_map/ppermute | solution.py:26
  244.5 20.0 %collective-permute-start.19 = (bf16[4,32,3072]{2,1,0:T(8,128)(2,1)S(1)}, bf16[4,32,3072]{2,1,0:T(8,128)(2,1)S(1)}, u32[]{:S(2)}, u32[]{:S(2)}) collective-permute-start(bf16[4,32,3072]{2,1,0:T(8,128)(2,1)S(1)} %pad_maximum_fusion.2), channel_id=1, source_target_pairs={{0,32},{8,40},{16,48},{24,56},{32,64},{40,72},{48,80},{56,88},{64,... | collective-permute-start | bytes 2359304 | tf_op jit(solution)/shard_map/ppermute | solution.py:26
  247.6 27.0 %collective-permute-start.13 = (bf16[4,32,3072]{2,1,0:T(8,128)(2,1)S(1)}, bf16[4,32,3072]{2,1,0:T(8,128)(2,1)S(1)}, u32[]{:S(2)}, u32[]{:S(2)}) collective-permute-start(bf16[4,32,3072]{2,1,0:T(8,128)(2,1)S(1)} %pad_maximum_fusion.1), channel_id=1, source_target_pairs={{0,24},{8,0},{16,8},{24,16},{32,56},{40,32},{48,40},{56,48},{64,88... | collective-permute-start | bytes 2359304 | tf_op jit(solution)/shard_map/ppermute | solution.py:26
  251.3 26.9 %collective-permute-start.11 = (bf16[4,32,3072]{2,1,0:T(8,128)(2,1)S(1)}, bf16[4,32,3072]{2,1,0:T(8,128)(2,1)S(1)}, u32[]{:S(2)}, u32[]{:S(2)}) collective-permute-start(bf16[4,32,3072]{2,1,0:T(8,128)(2,1)S(1)} %pad_maximum_fusion), channel_id=1, source_target_pairs={{0,8},{8,16},{16,24},{24,0},{32,40},{40,48},{48,56},{56,32},{64,72... | collective-permute-start | bytes 2359304 | tf_op jit(solution)/shard_map/ppermute | solution.py:26
  264.8 17.3 %collective-permute-start.22 = (bf16[16,3072]{1,0:T(8,128)(2,1)S(1)}, bf16[16,3072]{1,0:T(8,128)(2,1)S(1)}, u32[]{:S(2)}, u32[]{:S(2)}) collective-permute-start(bf16[16,3072]{1,0:T(8,128)(2,1)S(1)} %get-tuple-element.41), channel_id=1, source_target_pairs={{0,8},{8,16},{16,24},{24,0},{32,40},{40,48},{48,56},{56,32},{64,72... | collective-permute-start | bytes 294920 | tf_op jit(solution)/shard_map/ppermute | solution.py:26
  266.1 16.0 %collective-permute-start.24 = (bf16[16,3072]{1,0:T(8,128)(2,1)S(1)}, bf16[16,3072]{1,0:T(8,128)(2,1)S(1)}, u32[]{:S(2)}, u32[]{:S(2)}) collective-permute-start(bf16[16,3072]{1,0:T(8,128)(2,1)S(1)} %get-tuple-element.42), channel_id=1, source_target_pairs={{0,24},{8,0},{16,8},{24,16},{32,56},{40,32},{48,40},{56,48},{64,88... | collective-permute-start | bytes 294920 | tf_op jit(solution)/shard_map/ppermute | solution.py:26
  278.6 5.9 %collective-permute-start.14 = (bf16[16,3072]{1,0:T(8,128)(2,1)S(1)}, bf16[16,3072]{1,0:T(8,128)(2,1)S(1)}, u32[]{:S(2)}, u32[]{:S(2)}) collective-permute-start(bf16[16,3072]{1,0:T(8,128)(2,1)S(1)} %get-tuple-element.39), channel_id=1, source_target_pairs={{0,32},{8,40},{16,48},{24,56},{32,64},{40,72},{48,80},{56,88},{64,... | collective-permute-start | bytes 294920 | tf_op jit(solution)/shard_map/ppermute | solution.py:26
  278.7 5.8 %collective-permute-start.16 = (bf16[16,3072]{1,0:T(8,128)(2,1)S(1)}, bf16[16,3072]{1,0:T(8,128)(2,1)S(1)}, u32[]{:S(2)}, u32[]{:S(2)}) collective-permute-start(bf16[16,3072]{1,0:T(8,128)(2,1)S(1)} %get-tuple-element.40), channel_id=1, source_target_pairs={{0,96},{8,104},{16,112},{24,120},{32,0},{40,8},{48,16},{56,24},{64... | collective-permute-start | bytes 294920 | tf_op jit(solution)/shard_map/ppermute | solution.py:26
  282.2 5.8 %collective-permute-start.25 = (bf16[32,3072]{1,0:T(8,128)(2,1)S(1)}, bf16[32,3072]{1,0:T(8,128)(2,1)S(1)}, u32[]{:S(2)}, u32[]{:S(2)}) collective-permute-start(bf16[32,3072]{1,0:T(8,128)(2,1)S(1)} %pad_maximum_fusion.10), channel_id=1, source_target_pairs={{0,24},{8,0},{16,8},{24,16},{32,56},{40,32},{48,40},{56,48},{64,88... | collective-permute-start | bytes 589832 | tf_op jit(solution)/shard_map/ppermute | solution.py:26
  282.6 6.9 %collective-permute-start.23 = (bf16[32,3072]{1,0:T(8,128)(2,1)S(1)}, bf16[32,3072]{1,0:T(8,128)(2,1)S(1)}, u32[]{:S(2)}, u32[]{:S(2)}) collective-permute-start(bf16[32,3072]{1,0:T(8,128)(2,1)S(1)} %pad_maximum_fusion.9), channel_id=1, source_target_pairs={{0,8},{8,16},{16,24},{24,0},{32,40},{40,48},{48,56},{56,32},{64,72... | collective-permute-start | bytes 589832 | tf_op jit(solution)/shard_map/ppermute | solution.py:26
  284.6 6.5 %collective-permute-start.17 = (bf16[32,3072]{1,0:T(8,128)(2,1)S(1)}, bf16[32,3072]{1,0:T(8,128)(2,1)S(1)}, u32[]{:S(2)}, u32[]{:S(2)}) collective-permute-start(bf16[32,3072]{1,0:T(8,128)(2,1)S(1)} %pad_maximum_fusion.8), channel_id=1, source_target_pairs={{0,96},{8,104},{16,112},{24,120},{32,0},{40,8},{48,16},{56,24},{64... | collective-permute-start | bytes 589832 | tf_op jit(solution)/shard_map/ppermute | solution.py:26
  287.9 6.9 %collective-permute-start.15 = (bf16[32,3072]{1,0:T(8,128)(2,1)S(1)}, bf16[32,3072]{1,0:T(8,128)(2,1)S(1)}, u32[]{:S(2)}, u32[]{:S(2)}) collective-permute-start(bf16[32,3072]{1,0:T(8,128)(2,1)S(1)} %pad_maximum_fusion.7), channel_id=1, source_target_pairs={{0,32},{8,40},{16,48},{24,56},{32,64},{40,72},{48,80},{56,88},{64,... | collective-permute-start | bytes 589832 | tf_op jit(solution)/shard_map/ppermute | solution.py:26
Sparse Core Ops, SparseCore 0:
  14.6 104.7 all-gather.1
  177.9 105.0 reduce-scatter.1

commit v4 on v2

--- a/solution.py
+++ b/solution.py
@@ -146,9 +146,8 @@
         multipliers, gathered.reshape(2 * block_size, half), preferred_element_type=jnp.float32
     )
     schur_first = jnp.where(retained[None, :half], schur_first, jnp.zeros_like(schur_first))
-    second_half, schur_first = lax.optimization_barrier(
-        (later_cols, schur_first.astype(jnp.bfloat16))
-    )
+    second_half = later_cols
+    schur_first = schur_first.astype(jnp.bfloat16)
     summed_first = lax.psum_scatter(
         schur_first, "layer", scatter_dimension=0, tiled=True
     ).astype(jnp.float32)

time: 283 us -> 271 us (0.958)
  waiting for transfers between devices: 130 us -> 117 us
  starting transfers between devices: 40.9 us -> 43.9 us
    ppermute x8, waiting for transfers between devices: 39.7 us -> 31.4 us  [ring(): lax.ppermute(value, axis, [(i, (i + step) % size) for i in range(size)])]
    all_gather x1, waiting for transfers between devices: 59.5 us -> 55.7 us  [on_device(): lax.all_gather(pivot_masked[:, :, :half], 'prow', axis=1, tiled=True)]
    ppermute x16, starting transfers between devices: 23.8 us -> 27.5 us  [grid_shift(): return lax.ppermute(value, axis, pairs)]
  transfers between devices with their start and end apart: 28 -> 28, of which waited for: 10 -> 12; matrix products, arithmetic and copies ran while one was open for 23% -> 29% of each run, Pallas kernels for 0% -> 0%
where the time goes in v4:
time: 271 us; the launch traced here: 270 us
  waiting for transfers between devices  117 us (43%)
  starting transfers between devices  43.9 us (16%)
  local copies, waits for them, and re-layouts  42 us (15%)
  matrix products  30 us (11%)
  other arithmetic  22 us (8%)
  between operations  14.9 us (5%)
    all_gather x1, waiting for transfers between devices, on_device(): lax.all_gather(pivot_masked[:, :, :half], 'prow', axis=1, tiled=True)  55.7 us
    ppermute x8, waiting for transfers between devices, ring(): lax.ppermute(value, axis, [(i, (i + step) % size) for i in range(size)])  31.4 us
    ppermute x16, waiting for transfers between devices, grid_shift(): return lax.ppermute(value, axis, pairs)  29.4 us
    ppermute x16, starting transfers between devices, grid_shift(): return lax.ppermute(value, axis, pairs)  27.5 us
    unnamed x45, local copies, waits for them, and re-layouts  24.8 us
    dot_general x1, matrix products, on_device(): jnp.dot(multipliers, gathered.reshape(2 * block_size, half), preferred_el...  13.8 us
    ppermute x8, starting transfers between devices, ring(): lax.ppermute(value, axis, [(i, (i + step) % size) for i in range(size)])  13.1 us
    mul x1, other arithmetic, on_device(): front[0]  11.8 us
  transfers between devices with their start and end apart: 28, of which 12 were waited for; matrix products, arithmetic and copies ran while one was open for 29% of the time, Pallas kernels for 0%

profile of v4, /device:TPU:0, one launch (start us, length us, event | category | flops | bytes accessed | tf_op | source)
XLA Modules:
  0.0 270.1 jit_solution(3533029268124355230)
XLA Ops:
  7.2 0.7 convert_bitcast_fusion
  8.1 2.7 %bitcast_multiply_fusion.1 = bf16[2,64,16384]{2,1,0:T(8,128)(2,1)S(1)} fusion(bf16[1,2,64,16384]{3,2,1,0:T(8,128)(2,1)} %param.8, bf16[2,16384]{1,0:T(2,128)(2,1)S(1)} %bitcast.165), kind=kLoop, calls=%fused_computation.9 | loop fusion | flops 2097152 | bytes 8454144 | tf_op jit(solution)/shard_map/mul | solution.py:92
  10.8 2.0 copy-done.1
  12.8 1.8 slice.325
  14.6 0.9 fusion.61
  15.6 4.2 %collective-permute-start = (bf16[2,64,512]{2,1,0:T(8,128)(2,1)S(1)}, bf16[2,64,512]{2,1,0:T(8,128)(2,1)S(1)}, u32[]{:S(2)}, u32[]{:S(2)}) collective-permute-start(bf16[2,64,512]{2,1,0:T(8,128)(2,1)S(1)} %get-tuple-element.19), channel_id=1, source_target_pairs={{0,6},{2,0},{4,2},{6,4},{1,7},{3,1},{5,3},{7,5},{8,14},{10,8},{12,... | collective-permute-start | bytes 393224 | tf_op jit(solution)/shard_map/ppermute | solution.py:8
  19.8 1.4 slice.324
  21.2 2.7 %mul.31 = bf16[2,256,64,256]{3,2,1,0:T(8,128)(2,1)S(1)} broadcast(bf16[2,64]{1,0:T(2,128)(2,1)S(1)} %convert_bitcast_fusion.1), dimensions={0,2} | broadcast | bytes 16777472 | tf_op jit(solution)/shard_map/mul | solution.py:88
  23.9 12.5 %copy.14 = bf16[64,8,64,256]{3,1,2,0:T(8,128)(2,1)} copy(bf16[64,8,64,256]{3,2,1,0:T(8,128)(2,1)S(1)} %bitcast.158) | data formatting | bytes 33554432
  36.4 11.8 %bitcast_multiply_fusion = bf16[512,16384]{1,0:T(8,128)(2,1)S(1)} fusion(bf16[512,16384]{1,0:T(8,128)(2,1)} %bitcast.157, bf16[1,512,16384]{2,1,0:T(8,128)(2,1)} %param.7), kind=kLoop, calls=%fused_computation.1 | loop fusion | flops 8388608 | bytes 50331648 | tf_op jit(solution)/shard_map/mul | solution.py:88
  48.3 5.8 %copy-done = bf16[512,16384]{1,0:T(8,128)(2,1)} copy-done((bf16[512,16384]{1,0:T(8,128)(2,1)}, bf16[512,16384]{1,0:T(8,128)(2,1)S(1)}, u32[]{:S(2)}) %copy-start) | copy-done | bytes 16777240
  54.1 0.3 convolution_convert_fusion.1
  54.5 3.3 %collective-permute-start.3 = (bf16[2,32,512]{2,1,0:T(8,128)(2,1)S(1)}, bf16[2,32,512]{2,1,0:T(8,128)(2,1)S(1)}, u32[]{:S(2)}, u32[]{:S(2)}) collective-permute-start(bf16[2,32,512]{2,1,0:T(8,128)(2,1)S(1)} %slice.319), channel_id=1, source_target_pairs={{0,6},{2,0},{4,2},{6,4},{1,7},{3,1},{5,3},{7,5},{8,14},{10,8},{12,... | collective-permute-start | bytes 196616 | tf_op jit(solution)/shard_map/ppermute | solution.py:8
  57.8 3.7 %collective-permute-done.2 = bf16[2,32,512]{2,1,0:T(8,128)(2,1)S(1)} collective-permute-done((bf16[2,32,512]{2,1,0:T(8,128)(2,1)S(1)}, bf16[2,32,512]{2,1,0:T(8,128)(2,1)S(1)}, u32[]{:S(2)}, u32[]{:S(2)}) %collective-permute-start.2) | collective-permute-done | bytes 65568 | tf_op jit(solution)/shard_map/ppermute | solution.py:8
  61.6 0.9 constant_dynamic-update-slice_fusion.4
  62.8 1.9 collective-permute-start.5
  64.7 1.4 convolution_convert_fusion
  66.2 1.3 collective-permute-start.4
  67.8 0.6 copy-done.9
  68.5 0.6 collective-permute-done.4
  69.2 1.0 copy.11
  70.2 1.2 subtract_convert_fusion
  71.4 1.3 fusion.25
  72.7 55.7 %all-gather.2.cloned.1.call-done = bf16[2,256,11264]{2,1,0:T(8,128)(2,1)} async-done(((bf16[2,64,11264]{2,1,0:T(8,128)(2,1)}), bf16[2,256,11264]{2,1,0:T(8,128)(2,1)}) %all-gather.2.cloned.1.call-update) | async-done | bytes 11534352 | tf_op jit(solution)/shard_map/all_gather | solution.py:103
  128.4 1.4 collective-permute-start.6
  129.9 0.6 collective-permute-start.7
  130.4 13.8 %select_convert_fusion = bf16[512,11264]{1,0:T(8,128)(2,1)} fusion(bf16[512,11264]{1,0:T(8,128)(2,1)} %bitcast.164, bf16[512,16384]{1,0:T(8,128)(2,1)} %copy-done, pred[11264]{0:T(1024)(128)(4,1)S(1)} %slice.313, bf16[512,256]{0,1:T(8,128)(2,1)S(1)} %slice.322, bf16[512,256]{0,1:T(8,128)(2,1)} %copy-done.8), kind=kOutput, calls=%fused_computation | convolution fusion | flops 5929697280 | bytes 35138560 | tf_op jit(solution)/shard_map/dot_general | solution.py:145
  144.4 16.8 %collective-permute-done.7 = bf16[2,64,5120]{2,1,0:T(8,128)(2,1)S(1)} collective-permute-done((bf16[2,64,5120]{2,1,0:T(8,128)(2,1)S(1)}, bf16[2,64,5120]{2,1,0:T(8,128)(2,1)S(1)}, u32[]{:S(2)}, u32[]{:S(2)}) %collective-permute-start.7) | collective-permute-done | bytes 1310752 | tf_op jit(solution)/shard_map/ppermute | solution.py:8
  161.2 0.3 collective-permute-start.8
  161.5 4.3 %fusion = bf16[64,11264]{1,0:T(8,128)(2,1)S(1)} fusion(bf16[64,256]{1,0:T(8,128)(2,1)S(1)} %constant_dynamic-slice_fusion, bf16[2,256,11264]{2,1,0:T(8,128)(2,1)} %all-gather.2.cloned.1.call-done, bf16[2,64,16384]{2,1,0:T(8,128)(2,1)} %copy-done.1), kind=kOutput, calls=%fused_computation.3 | convolution fusion | flops 371261440 | bytes 8683520 | tf_op jit(solution)/shard_map/dot_general | solution.py:160
  165.8 1.2 slice.329
  167.0 3.3 %collective-permute-start.9 = (bf16[2,32,5120]{2,1,0:T(8,128)(2,1)S(1)}, bf16[2,32,5120]{2,1,0:T(8,128)(2,1)S(1)}, u32[]{:S(2)}, u32[]{:S(2)}) collective-permute-start(bf16[2,32,5120]{2,1,0:T(8,128)(2,1)S(1)} %slice.329), channel_id=1, source_target_pairs={{0,6},{2,0},{4,2},{6,4},{1,7},{3,1},{5,3},{7,5},{8,14},{10,8},{12,... | collective-permute-start | bytes 1966088 | tf_op jit(solution)/shard_map/ppermute | solution.py:8
  170.3 1.5 constant_dynamic-update-slice_fusion.13
  171.8 6.1 %collective-permute-done.8 = bf16[2,32,5120]{2,1,0:T(8,128)(2,1)S(1)} collective-permute-done((bf16[2,32,5120]{2,1,0:T(8,128)(2,1)S(1)}, bf16[2,32,5120]{2,1,0:T(8,128)(2,1)S(1)}, u32[]{:S(2)}, u32[]{:S(2)}) %collective-permute-start.8) | collective-permute-done | bytes 655392 | tf_op jit(solution)/shard_map/ppermute | solution.py:8
  177.9 4.9 %collective-permute-done.9 = bf16[2,32,5120]{2,1,0:T(8,128)(2,1)S(1)} collective-permute-done((bf16[2,32,5120]{2,1,0:T(8,128)(2,1)S(1)}, bf16[2,32,5120]{2,1,0:T(8,128)(2,1)S(1)}, u32[]{:S(2)}, u32[]{:S(2)}) %collective-permute-start.9) | collective-permute-done | bytes 655392 | tf_op jit(solution)/shard_map/ppermute | solution.py:8
  183.0 7.0 %subtract_select_fusion = f32[512,5120]{1,0:T(8,128)S(1)} fusion(bf16[512,5120]{1,0:T(8,128)(2,1)S(1)} %bitcast.162, bf16[512,16384]{1,0:T(8,128)(2,1)} %copy-done, pred[5120]{0:T(1024)(128)(4,1)S(1)} %slice-done.2, bf16[512,256]{0,1:T(8,128)(2,1)S(1)} %copy-done.5, bf16[512,256]{0,1:T(8,128)(2,1)S(1)} %copy-done.6), kind=kOutput, calls=%fused_computation.4 | convolution fusion | flops 2693267456 | bytes 21500928 | tf_op jit(solution)/shard_map/dot_general | solution.py:173
  190.0 5.2 %fusion.60 = (f32[4,4,32,2560]{3,2,1,0:T(8,128)}, f32[4,4,32,2560]{3,2,1,0:T(8,128)}) fusion(f32[4,4,32,5120]{3,2,1,0:T(8,128)S(1)} %bitcast.159), kind=kLoop, calls=%fused_computation.146 | loop fusion | bytes 20971520 | tf_op jit(solution)/shard_map/slice | solution.py:65
  195.2 2.0 dynamic-slice_bitcast_fusion
  197.2 2.3 collective-permute-start.10
  199.5 1.3 collective-permute-start.12
  200.8 1.4 dynamic-slice_convert_fusion
  202.3 2.1 collective-permute-start.18
  204.3 1.3 collective-permute-start.20
  205.6 1.8 fusion.1
  207.6 1.5 maximum_bitcast_fusion.1
  209.1 4.5 %collective-permute-done.10 = bf16[2,32,2560]{2,1,0:T(8,128)(2,1)S(1)} collective-permute-done((bf16[2,32,2560]{2,1,0:T(8,128)(2,1)S(1)}, bf16[2,32,2560]{2,1,0:T(8,128)(2,1)S(1)}, u32[]{:S(2)}, u32[]{:S(2)}) %collective-permute-start.10) | collective-permute-done | bytes 327712 | tf_op jit(solution)/shard_map/ppermute | solution.py:26
  213.8 0.8 collective-permute-start.11
  214.8 2.6 collective-permute-start.13
  217.5 1.4 collective-permute-start.19
  219.0 2.0 collective-permute-start.21
  221.0 13.5 %collective-permute-done.11 = bf16[4,32,2560]{2,1,0:T(8,128)(2,1)S(1)} collective-permute-done((bf16[4,32,2560]{2,1,0:T(8,128)(2,1)S(1)}, bf16[4,32,2560]{2,1,0:T(8,128)(2,1)S(1)}, u32[]{:S(2)}, u32[]{:S(2)}) %collective-permute-start.11) | collective-permute-done | bytes 655392 | tf_op jit(solution)/shard_map/ppermute | solution.py:26
  234.5 1.8 collective-permute-done.13
  236.3 0.2 fusion.5
  236.5 2.8 %collective-permute-start.14 = (bf16[16,2560]{1,0:T(8,128)(2,1)S(1)}, bf16[16,2560]{1,0:T(8,128)(2,1)S(1)}, u32[]{:S(2)}, u32[]{:S(2)}) collective-permute-start(bf16[16,2560]{1,0:T(8,128)(2,1)S(1)} %get-tuple-element.35), channel_id=1, source_target_pairs={{0,32},{8,40},{16,48},{24,56},{32,64},{40,72},{48,80},{56,88},{64,... | collective-permute-start | bytes 245768 | tf_op jit(solution)/shard_map/ppermute | solution.py:26
  239.3 0.5 collective-permute-start.16
  239.9 3.1 %collective-permute-done.19 = bf16[4,32,2560]{2,1,0:T(8,128)(2,1)S(1)} collective-permute-done((bf16[4,32,2560]{2,1,0:T(8,128)(2,1)S(1)}, bf16[4,32,2560]{2,1,0:T(8,128)(2,1)S(1)}, u32[]{:S(2)}, u32[]{:S(2)}) %collective-permute-start.19) | collective-permute-done | bytes 655392 | tf_op jit(solution)/shard_map/ppermute | solution.py:26
  243.0 3.3 %collective-permute-done.21 = bf16[4,32,2560]{2,1,0:T(8,128)(2,1)S(1)} collective-permute-done((bf16[4,32,2560]{2,1,0:T(8,128)(2,1)S(1)}, bf16[4,32,2560]{2,1,0:T(8,128)(2,1)S(1)}, u32[]{:S(2)}, u32[]{:S(2)}) %collective-permute-start.21) | collective-permute-done | bytes 655392 | tf_op jit(solution)/shard_map/ppermute | solution.py:26
  246.3 0.2 fusion.4
  246.7 3.2 %collective-permute-start.24 = (bf16[16,2560]{1,0:T(8,128)(2,1)S(1)}, bf16[16,2560]{1,0:T(8,128)(2,1)S(1)}, u32[]{:S(2)}, u32[]{:S(2)}) collective-permute-start(bf16[16,2560]{1,0:T(8,128)(2,1)S(1)} %get-tuple-element.38), channel_id=1, source_target_pairs={{0,24},{8,0},{16,8},{24,16},{32,56},{40,32},{48,40},{56,48},{64,88... | collective-permute-start | bytes 245768 | tf_op jit(solution)/shard_map/ppermute | solution.py:26
  250.0 3.8 %collective-permute-start.17 = (bf16[32,2560]{1,0:T(8,128)(2,1)S(1)}, bf16[32,2560]{1,0:T(8,128)(2,1)S(1)}, u32[]{:S(2)}, u32[]{:S(2)}) collective-permute-start(bf16[32,2560]{1,0:T(8,128)(2,1)S(1)} %pad_maximum_fusion.8), channel_id=1, source_target_pairs={{0,96},{8,104},{16,112},{24,120},{32,0},{40,8},{48,16},{56,24},{64... | collective-permute-start | bytes 491528 | tf_op jit(solution)/shard_map/ppermute | solution.py:26
  254.0 3.3 %collective-permute-start.25 = (bf16[32,2560]{1,0:T(8,128)(2,1)S(1)}, bf16[32,2560]{1,0:T(8,128)(2,1)S(1)}, u32[]{:S(2)}, u32[]{:S(2)}) collective-permute-start(bf16[32,2560]{1,0:T(8,128)(2,1)S(1)} %pad_maximum_fusion.10), channel_id=1, source_target_pairs={{0,24},{8,0},{16,8},{24,16},{32,56},{40,32},{48,40},{56,48},{64,88... | collective-permute-start | bytes 491528 | tf_op jit(solution)/shard_map/ppermute | solution.py:26
  257.3 3.1 %collective-permute-done.23 = bf16[32,2560]{1,0:T(8,128)(2,1)S(1)} collective-permute-done((bf16[32,2560]{1,0:T(8,128)(2,1)S(1)}, bf16[32,2560]{1,0:T(8,128)(2,1)S(1)}, u32[]{:S(2)}, u32[]{:S(2)}) %collective-permute-start.23) | collective-permute-done | bytes 163872 | tf_op jit(solution)/shard_map/ppermute | solution.py:26
  260.6 1.2 convert_element_type.156
  261.8 1.5 maximum_bitcast_fusion
  (107 shorter events, 2.7 us)
Async XLA Ops:
  7.2 121.2 %all-gather.2.cloned.1.call-start = ((), (), s32[]{:S(2)}) async-start(), calls=%async_computation.1 | async-start | bytes 14417920 | tf_op jit(solution)/shard_map/all_gather | solution.py:103
  10.8 2.0 copy-start.1
  12.8 8.4 %copy-start.11 = (s32[1,2,64]{2,1,0:T(2,128)S(1)}, s32[1,2,64]{2,1,0:T(2,128)}, u32[]{:S(2)}) copy-start(s32[1,2,64]{2,1,0:T(2,128)} %param.10) | copy-start | bytes 1540
  14.6 246.0 %reduce-scatter.2.cloned.1.call-start = ((), (), s32[]{:S(2)}) async-start(), calls=%async_computation.2 | async-start | bytes 12255232 | tf_op jit(solution)/shard_map/reduce_scatter | solution.py:151
  15.6 38.9 %collective-permute-start = (bf16[2,64,512]{2,1,0:T(8,128)(2,1)S(1)}, bf16[2,64,512]{2,1,0:T(8,128)(2,1)S(1)}, u32[]{:S(2)}, u32[]{:S(2)}) collective-permute-start(bf16[2,64,512]{2,1,0:T(8,128)(2,1)S(1)} %get-tuple-element.19), channel_id=1, source_target_pairs={{0,6},{2,0},{4,2},{6,4},{1,7},{3,1},{5,3},{7,5},{8,14},{10,8},{12,... | collective-permute-start | bytes 393224 | tf_op jit(solution)/shard_map/ppermute | solution.py:8
  19.7 34.6 %collective-permute-start.1 = (bf16[2,64,512]{2,1,0:T(8,128)(2,1)S(1)}, bf16[2,64,512]{2,1,0:T(8,128)(2,1)S(1)}, u32[]{:S(2)}, u32[]{:S(2)}) collective-permute-start(bf16[2,64,512]{2,1,0:T(8,128)(2,1)S(1)} %get-tuple-element.19), channel_id=1, source_target_pairs={{0,2},{2,4},{4,6},{6,0},{1,3},{3,5},{5,7},{7,1},{8,10},{10,12},{12... | collective-permute-start | bytes 393224 | tf_op jit(solution)/shard_map/ppermute | solution.py:8
  36.4 17.7 %copy-start.7 = (bf16[1,2,256,256]{3,2,1,0:T(8,128)(2,1)S(1)}, bf16[1,2,256,256]{3,2,1,0:T(8,128)(2,1)}, u32[]{:S(2)}) copy-start(bf16[1,2,256,256]{3,2,1,0:T(8,128)(2,1)} %param.9) | copy-start | bytes 786436
  48.3 5.8 %copy-start = (bf16[512,16384]{1,0:T(8,128)(2,1)}, bf16[512,16384]{1,0:T(8,128)(2,1)S(1)}, u32[]{:S(2)}) copy-start(bf16[512,16384]{1,0:T(8,128)(2,1)S(1)} %bitcast_multiply_fusion) | copy-start | bytes 50331652
  54.4 7.1 %collective-permute-start.2 = (bf16[2,32,512]{2,1,0:T(8,128)(2,1)S(1)}, bf16[2,32,512]{2,1,0:T(8,128)(2,1)S(1)}, u32[]{:S(2)}, u32[]{:S(2)}) collective-permute-start(bf16[2,32,512]{2,1,0:T(8,128)(2,1)S(1)} %slice.318), channel_id=1, source_target_pairs={{0,2},{2,4},{4,6},{6,0},{1,3},{3,5},{5,7},{7,1},{8,10},{10,12},{12... | collective-permute-start | bytes 196616 | tf_op jit(solution)/shard_map/ppermute | solution.py:8
  54.5 7.0 %collective-permute-start.3 = (bf16[2,32,512]{2,1,0:T(8,128)(2,1)S(1)}, bf16[2,32,512]{2,1,0:T(8,128)(2,1)S(1)}, u32[]{:S(2)}, u32[]{:S(2)}) collective-permute-start(bf16[2,32,512]{2,1,0:T(8,128)(2,1)S(1)} %slice.319), channel_id=1, source_target_pairs={{0,6},{2,0},{4,2},{6,4},{1,7},{3,1},{5,3},{7,5},{8,14},{10,8},{12,... | collective-permute-start | bytes 196616 | tf_op jit(solution)/shard_map/ppermute | solution.py:8
  62.8 5.0 %collective-permute-start.5 = (bf16[256,256]{1,0:T(8,128)(2,1)S(1)}, bf16[256,256]{1,0:T(8,128)(2,1)}, u32[]{:S(2)}, u32[]{:S(2)}) collective-permute-start(bf16[256,256]{1,0:T(8,128)(2,1)S(1)} %convolution_convert_fusion.2), channel_id=1, source_target_pairs={{0,1},{2,3},{4,5},{6,7},{8,9},{10,11},{12,13},{14,15},{16,17},{18,... | collective-permute-start | bytes 393224 | tf_op jit(solution)/shard_map/ppermute | solution.py:127
  66.2 2.8 %collective-permute-start.4 = (bf16[512,512]{0,1:T(8,128)(2,1)S(1)}, bf16[512,512]{0,1:T(8,128)(2,1)S(1)}, u32[]{:S(2)}, u32[]{:S(2)}) collective-permute-start(bf16[512,512]{0,1:T(8,128)(2,1)S(1)} %pad_maximum_fusion.6), channel_id=1, source_target_pairs={{0,1},{2,3},{4,5},{6,7},{8,9},{10,11},{12,13},{14,15},{16,17},{18,... | collective-permute-start | bytes 1572872 | tf_op jit(solution)/shard_map/ppermute | solution.py:127
  67.6 76.7 %copy-start.10 = (pred[16384]{0:T(1024)(128)(4,1)}, pred[16384]{0:T(1024)(128)(4,1)S(1)}, u32[]{:S(2)}) copy-start(pred[16384]{0:T(1024)(128)(4,1)S(1)} %add_compare_fusion) | copy-start | bytes 49156
  67.8 0.7 copy-start.9
  71.4 57.0 %copy-start.8 = (bf16[512,256]{0,1:T(8,128)(2,1)}, bf16[512,256]{0,1:T(8,128)(2,1)S(1)}, u32[]{:S(2)}) copy-start(bf16[512,256]{0,1:T(8,128)(2,1)S(1)} %subtract_convert_fusion) | copy-start | bytes 786436
  128.4 37.4 %collective-permute-start.6 = (bf16[2,64,5120]{2,1,0:T(8,128)(2,1)S(1)}, bf16[2,64,5120]{2,1,0:T(8,128)(2,1)}, u32[]{:S(2)}, u32[]{:S(2)}) collective-permute-start(bf16[2,64,5120]{2,1,0:T(8,128)(2,1)S(1)} %slice.324), channel_id=1, source_target_pairs={{0,6},{2,0},{4,2},{6,4},{1,7},{3,1},{5,3},{7,5},{8,14},{10,8},{12,... | collective-permute-start | bytes 3932168 | tf_op jit(solution)/shard_map/ppermute | solution.py:8
  129.9 31.3 %collective-permute-start.7 = (bf16[2,64,5120]{2,1,0:T(8,128)(2,1)S(1)}, bf16[2,64,5120]{2,1,0:T(8,128)(2,1)S(1)}, u32[]{:S(2)}, u32[]{:S(2)}) collective-permute-start(bf16[2,64,5120]{2,1,0:T(8,128)(2,1)S(1)} %slice.324), channel_id=1, source_target_pairs={{0,2},{2,4},{4,6},{6,0},{1,3},{3,5},{5,7},{7,1},{8,10},{10,12},{12... | collective-permute-start | bytes 3932168 | tf_op jit(solution)/shard_map/ppermute | solution.py:8
  161.2 16.7 %collective-permute-start.8 = (bf16[2,32,5120]{2,1,0:T(8,128)(2,1)S(1)}, bf16[2,32,5120]{2,1,0:T(8,128)(2,1)S(1)}, u32[]{:S(2)}, u32[]{:S(2)}) collective-permute-start(bf16[2,32,5120]{2,1,0:T(8,128)(2,1)S(1)} %slice.328), channel_id=1, source_target_pairs={{0,2},{2,4},{4,6},{6,0},{1,3},{3,5},{5,7},{7,1},{8,10},{10,12},{12... | collective-permute-start | bytes 1966088 | tf_op jit(solution)/shard_map/ppermute | solution.py:8
  165.8 17.2 %copy-start.5 = (bf16[512,256]{0,1:T(8,128)(2,1)S(1)}, bf16[512,256]{0,1:T(8,128)(2,1)}, u32[]{:S(2)}) copy-start(bf16[512,256]{0,1:T(8,128)(2,1)} %get-tuple-element.39) | copy-start | bytes 786436
  165.8 17.2 %copy-start.6 = (bf16[512,256]{0,1:T(8,128)(2,1)S(1)}, bf16[512,256]{0,1:T(8,128)(2,1)}, u32[]{:S(2)}) copy-start(bf16[512,256]{0,1:T(8,128)(2,1)} %get-tuple-element.40) | copy-start | bytes 786436
  165.8 17.2 %slice-start.2 = ((pred[16384]{0:T(1024)(128)(4,1)}), pred[5120]{0:T(1024)(128)(4,1)S(1)}, s32[]{:S(2)}) async-start(pred[16384]{0:T(1024)(128)(4,1)} %copy-done.10), calls=%async_computation.5 | async-start | bytes 10240 | tf_op jit(solution)/shard_map/slice | solution.py:178
  167.0 15.8 %collective-permute-start.9 = (bf16[2,32,5120]{2,1,0:T(8,128)(2,1)S(1)}, bf16[2,32,5120]{2,1,0:T(8,128)(2,1)S(1)}, u32[]{:S(2)}, u32[]{:S(2)}) collective-permute-start(bf16[2,32,5120]{2,1,0:T(8,128)(2,1)S(1)} %slice.329), channel_id=1, source_target_pairs={{0,6},{2,0},{4,2},{6,4},{1,7},{3,1},{5,3},{7,5},{8,14},{10,8},{12,... | collective-permute-start | bytes 1966088 | tf_op jit(solution)/shard_map/ppermute | solution.py:8
  182.9 7.1 %copy-start.3 = (bf16[2,256,5120]{2,1,0:T(8,128)(2,1)}, bf16[2,256,5120]{2,1,0:T(8,128)(2,1)S(1)}, u32[]{:S(2)}) copy-start(bf16[2,256,5120]{2,1,0:T(8,128)(2,1)S(1)} %constant_dynamic-update-slice_fusion.10) | copy-start | bytes 15728644
  195.2 10.5 %copy-start.4 = (bf16[2,256,5120]{2,1,0:T(8,128)(2,1)S(1)}, bf16[2,256,5120]{2,1,0:T(8,128)(2,1)}, u32[]{:S(2)}) copy-start(bf16[2,256,5120]{2,1,0:T(8,128)(2,1)} %copy-done.3) | copy-start | bytes 15728644
  195.2 12.2 %copy-start.2 = (f32[4,4,32,2560]{3,2,1,0:T(8,128)S(1)}, f32[4,4,32,2560]{3,2,1,0:T(8,128)}, u32[]{:S(2)}) copy-start(f32[4,4,32,2560]{3,2,1,0:T(8,128)} %get-tuple-element.11) | copy-start | bytes 15728644
  197.2 16.4 %collective-permute-start.10 = (bf16[2,32,2560]{2,1,0:T(8,128)(2,1)S(1)}, bf16[2,32,2560]{2,1,0:T(8,128)(2,1)S(1)}, u32[]{:S(2)}, u32[]{:S(2)}) collective-permute-start(bf16[2,32,2560]{2,1,0:T(8,128)(2,1)S(1)} %get-tuple-element.31), channel_id=1, source_target_pairs={{0,8},{8,16},{16,24},{24,0},{32,40},{40,48},{48,56},{56,32},{64,72... | collective-permute-start | bytes 983048 | tf_op jit(solution)/shard_map/ppermute | solution.py:26
  199.5 15.1 %collective-permute-start.12 = (bf16[2,32,2560]{2,1,0:T(8,128)(2,1)S(1)}, bf16[2,32,2560]{2,1,0:T(8,128)(2,1)S(1)}, u32[]{:S(2)}, u32[]{:S(2)}) collective-permute-start(bf16[2,32,2560]{2,1,0:T(8,128)(2,1)S(1)} %get-tuple-element.32), channel_id=1, source_target_pairs={{0,24},{8,0},{16,8},{24,16},{32,56},{40,32},{48,40},{56,48},{64,88... | collective-permute-start | bytes 983048 | tf_op jit(solution)/shard_map/ppermute | solution.py:26
  202.3 15.1 %collective-permute-start.18 = (bf16[2,32,2560]{2,1,0:T(8,128)(2,1)S(1)}, bf16[2,32,2560]{2,1,0:T(8,128)(2,1)S(1)}, u32[]{:S(2)}, u32[]{:S(2)}) collective-permute-start(bf16[2,32,2560]{2,1,0:T(8,128)(2,1)S(1)} %get-tuple-element.33), channel_id=1, source_target_pairs={{0,32},{8,40},{16,48},{24,56},{32,64},{40,72},{48,80},{56,88},{64,... | collective-permute-start | bytes 983048 | tf_op jit(solution)/shard_map/ppermute | solution.py:26
  204.3 4.7 %slice-start = ((s8[5242880]{0:T(1024)(128)(4,1)}), s8[4194304]{0:T(1024)(128)(4,1)S(1)}, s32[]{:S(2)}) async-start(s8[5242880]{0:T(1024)(128)(4,1)} %bitcast.160), calls=%async_computation.3 | async-start | bytes 8388608
  204.3 13.0 %collective-permute-start.20 = (bf16[2,32,2560]{2,1,0:T(8,128)(2,1)S(1)}, bf16[2,32,2560]{2,1,0:T(8,128)(2,1)S(1)}, u32[]{:S(2)}, u32[]{:S(2)}) collective-permute-start(bf16[2,32,2560]{2,1,0:T(8,128)(2,1)S(1)} %get-tuple-element.34), channel_id=1, source_target_pairs={{0,96},{8,104},{16,112},{24,120},{32,0},{40,8},{48,16},{56,24},{64... | collective-permute-start | bytes 983048 | tf_op jit(solution)/shard_map/ppermute | solution.py:26
  207.4 1.6 slice-start.1
  213.8 20.7 %collective-permute-start.11 = (bf16[4,32,2560]{2,1,0:T(8,128)(2,1)S(1)}, bf16[4,32,2560]{2,1,0:T(8,128)(2,1)S(1)}, u32[]{:S(2)}, u32[]{:S(2)}) collective-permute-start(bf16[4,32,2560]{2,1,0:T(8,128)(2,1)S(1)} %pad_maximum_fusion), channel_id=1, source_target_pairs={{0,8},{8,16},{16,24},{24,0},{32,40},{40,48},{48,56},{56,32},{64,72... | collective-permute-start | bytes 1966088 | tf_op jit(solution)/shard_map/ppermute | solution.py:26
  214.8 21.5 %collective-permute-start.13 = (bf16[4,32,2560]{2,1,0:T(8,128)(2,1)S(1)}, bf16[4,32,2560]{2,1,0:T(8,128)(2,1)S(1)}, u32[]{:S(2)}, u32[]{:S(2)}) collective-permute-start(bf16[4,32,2560]{2,1,0:T(8,128)(2,1)S(1)} %pad_maximum_fusion.1), channel_id=1, source_target_pairs={{0,24},{8,0},{16,8},{24,16},{32,56},{40,32},{48,40},{56,48},{64,88... | collective-permute-start | bytes 1966088 | tf_op jit(solution)/shard_map/ppermute | solution.py:26
  217.5 25.4 %collective-permute-start.19 = (bf16[4,32,2560]{2,1,0:T(8,128)(2,1)S(1)}, bf16[4,32,2560]{2,1,0:T(8,128)(2,1)S(1)}, u32[]{:S(2)}, u32[]{:S(2)}) collective-permute-start(bf16[4,32,2560]{2,1,0:T(8,128)(2,1)S(1)} %pad_maximum_fusion.2), channel_id=1, source_target_pairs={{0,32},{8,40},{16,48},{24,56},{32,64},{40,72},{48,80},{56,88},{64,... | collective-permute-start | bytes 1966088 | tf_op jit(solution)/shard_map/ppermute | solution.py:26
  219.0 27.3 %collective-permute-start.21 = (bf16[4,32,2560]{2,1,0:T(8,128)(2,1)S(1)}, bf16[4,32,2560]{2,1,0:T(8,128)(2,1)S(1)}, u32[]{:S(2)}, u32[]{:S(2)}) collective-permute-start(bf16[4,32,2560]{2,1,0:T(8,128)(2,1)S(1)} %pad_maximum_fusion.3), channel_id=1, source_target_pairs={{0,96},{8,104},{16,112},{24,120},{32,0},{40,8},{48,16},{56,24},{64... | collective-permute-start | bytes 1966088 | tf_op jit(solution)/shard_map/ppermute | solution.py:26
  236.5 13.4 %collective-permute-start.14 = (bf16[16,2560]{1,0:T(8,128)(2,1)S(1)}, bf16[16,2560]{1,0:T(8,128)(2,1)S(1)}, u32[]{:S(2)}, u32[]{:S(2)}) collective-permute-start(bf16[16,2560]{1,0:T(8,128)(2,1)S(1)} %get-tuple-element.35), channel_id=1, source_target_pairs={{0,32},{8,40},{16,48},{24,56},{32,64},{40,72},{48,80},{56,88},{64,... | collective-permute-start | bytes 245768 | tf_op jit(solution)/shard_map/ppermute | solution.py:26
  239.3 10.5 %collective-permute-start.16 = (bf16[16,2560]{1,0:T(8,128)(2,1)S(1)}, bf16[16,2560]{1,0:T(8,128)(2,1)S(1)}, u32[]{:S(2)}, u32[]{:S(2)}) collective-permute-start(bf16[16,2560]{1,0:T(8,128)(2,1)S(1)} %get-tuple-element.36), channel_id=1, source_target_pairs={{0,96},{8,104},{16,112},{24,120},{32,0},{40,8},{48,16},{56,24},{64... | collective-permute-start | bytes 245768 | tf_op jit(solution)/shard_map/ppermute | solution.py:26
  246.6 7.2 %collective-permute-start.22 = (bf16[16,2560]{1,0:T(8,128)(2,1)S(1)}, bf16[16,2560]{1,0:T(8,128)(2,1)S(1)}, u32[]{:S(2)}, u32[]{:S(2)}) collective-permute-start(bf16[16,2560]{1,0:T(8,128)(2,1)S(1)} %get-tuple-element.37), channel_id=1, source_target_pairs={{0,8},{8,16},{16,24},{24,0},{32,40},{40,48},{48,56},{56,32},{64,72... | collective-permute-start | bytes 245768 | tf_op jit(solution)/shard_map/ppermute | solution.py:26
  246.7 7.2 %collective-permute-start.24 = (bf16[16,2560]{1,0:T(8,128)(2,1)S(1)}, bf16[16,2560]{1,0:T(8,128)(2,1)S(1)}, u32[]{:S(2)}, u32[]{:S(2)}) collective-permute-start(bf16[16,2560]{1,0:T(8,128)(2,1)S(1)} %get-tuple-element.38), channel_id=1, source_target_pairs={{0,24},{8,0},{16,8},{24,16},{32,56},{40,32},{48,40},{56,48},{64,88... | collective-permute-start | bytes 245768 | tf_op jit(solution)/shard_map/ppermute | solution.py:26
  249.9 7.3 %collective-permute-start.15 = (bf16[32,2560]{1,0:T(8,128)(2,1)S(1)}, bf16[32,2560]{1,0:T(8,128)(2,1)S(1)}, u32[]{:S(2)}, u32[]{:S(2)}) collective-permute-start(bf16[32,2560]{1,0:T(8,128)(2,1)S(1)} %pad_maximum_fusion.7), channel_id=1, source_target_pairs={{0,32},{8,40},{16,48},{24,56},{32,64},{40,72},{48,80},{56,88},{64,... | collective-permute-start | bytes 491528 | tf_op jit(solution)/shard_map/ppermute | solution.py:26
  250.0 7.2 %collective-permute-start.17 = (bf16[32,2560]{1,0:T(8,128)(2,1)S(1)}, bf16[32,2560]{1,0:T(8,128)(2,1)S(1)}, u32[]{:S(2)}, u32[]{:S(2)}) collective-permute-start(bf16[32,2560]{1,0:T(8,128)(2,1)S(1)} %pad_maximum_fusion.8), channel_id=1, source_target_pairs={{0,96},{8,104},{16,112},{24,120},{32,0},{40,8},{48,16},{56,24},{64... | collective-permute-start | bytes 491528 | tf_op jit(solution)/shard_map/ppermute | solution.py:26
  253.9 6.6 %collective-permute-start.23 = (bf16[32,2560]{1,0:T(8,128)(2,1)S(1)}, bf16[32,2560]{1,0:T(8,128)(2,1)S(1)}, u32[]{:S(2)}, u32[]{:S(2)}) collective-permute-start(bf16[32,2560]{1,0:T(8,128)(2,1)S(1)} %pad_maximum_fusion.9), channel_id=1, source_target_pairs={{0,8},{8,16},{16,24},{24,0},{32,40},{40,48},{48,56},{56,32},{64,72... | collective-permute-start | bytes 491528 | tf_op jit(solution)/shard_map/ppermute | solution.py:26
  254.0 6.5 %collective-permute-start.25 = (bf16[32,2560]{1,0:T(8,128)(2,1)S(1)}, bf16[32,2560]{1,0:T(8,128)(2,1)S(1)}, u32[]{:S(2)}, u32[]{:S(2)}) collective-permute-start(bf16[32,2560]{1,0:T(8,128)(2,1)S(1)} %pad_maximum_fusion.10), channel_id=1, source_target_pairs={{0,24},{8,0},{16,8},{24,16},{32,56},{40,32},{48,40},{56,48},{64,88... | collective-permute-start | bytes 491528 | tf_op jit(solution)/shard_map/ppermute | solution.py:26
Sparse Core Ops, SparseCore 0:
  14.7 113.6 all-gather.1
  144.4 104.5 reduce-scatter.1

commit v5 on v4

--- a/solution.py
+++ b/solution.py
@@ -54,16 +54,15 @@
     )
 
 
-def grid_reduce_scatter(schur, axis):
+def grid_reduce_scatter(left, right, axis):
     side = 4
     index = lax.axis_index(axis)
     gy = index // side
     gx = index % side
-    rows, width = schur.shape
+    rows, width = left.shape
     part = rows // (side * side)
-    grid = schur.reshape(side, side, part, width)
-    left = grid[..., : width // 2]
-    right = grid[..., width // 2 :]
+    left = left.reshape(side, side, part, width)
+    right = right.reshape(side, side, part, width)
 
     def along_x(v, step):
         return grid_shift(v, axis, side, 0, step)
@@ -170,13 +169,18 @@
         ],
         1,
     )
-    schur_second = masked[:, half:].astype(jnp.float32) - jnp.dot(
-        multipliers_rel,
-        gathered_rel.reshape(2 * block_size, col_count - half),
-        preferred_element_type=jnp.float32,
-    )
-    schur_second = jnp.where(retained[None, half:], schur_second, jnp.zeros_like(schur_second))
-    summed = jnp.concatenate([summed_first, grid_reduce_scatter(schur_second, "layer")], 1)
+    split = (col_count - half) // 2
+    stacked_rel = gathered_rel.reshape(2 * block_size, col_count - half)
+    schur_halves = []
+    for start in (0, split):
+        cols = slice(half + start, half + start + split)
+        schur_half = masked[:, cols].astype(jnp.float32) - jnp.dot(
+            multipliers_rel, stacked_rel[:, start : start + split], preferred_element_type=jnp.float32
+        )
+        schur_halves.append(
+            jnp.where(retained[None, cols], schur_half, jnp.zeros_like(schur_half))
+        )
+    summed = jnp.concatenate([summed_first, grid_reduce_scatter(*schur_halves, "layer")], 1)
     ancestor = summed.reshape(1, 1, summed.shape[0], col_count)
     return (ancestor, lower_panel[None], upper_own[None])
 

time: 271 us -> 266 us (0.982)
  local copies, waits for them, and re-layouts: 42 us -> 33.7 us
  waiting for transfers between devices: 117 us -> 122 us
    slice x3 -> x1, local copies, waits for them, and re-layouts: 5.16 us -> 0.01 us  [on_device(): retained[None, cols]]
    reduce_scatter x1, waiting for transfers between devices: 0.02 us -> 3.68 us  [on_device(): lax.psum_scatter(schur_first, 'layer', scatter_dimension=0, tiled=True)]
    unnamed x45 -> x29, local copies, waits for them, and re-layouts: 24.8 us -> 24.2 us
    dot_general x1 -> x2, matrix products: 7.05 us -> 6.82 us  [on_device(): jnp.dot(multipliers_rel, stacked_rel[:, start:start + split], preferred_e...]
  transfers between devices with their start and end apart: 28 -> 28, of which waited for: 12 -> 13; matrix products, arithmetic and copies ran while one was open for 29% -> 26% of each run, Pallas kernels for 0% -> 0%
where the time goes in v5:
time: 266 us; the launch traced here: 265 us
  waiting for transfers between devices  122 us (46%)
  starting transfers between devices  43.3 us (16%)
  local copies, waits for them, and re-layouts  33.7 us (13%)
  matrix products  29.4 us (11%)
  other arithmetic  21.2 us (8%)
  between operations  14.9 us (6%)
    all_gather x1, waiting for transfers between devices, on_device(): lax.all_gather(pivot_masked[:, :, :half], 'prow', axis=1, tiled=True)  57.6 us
    ppermute x16, waiting for transfers between devices, grid_shift(): return lax.ppermute(value, axis, pairs)  30.9 us
    ppermute x8, waiting for transfers between devices, ring(): lax.ppermute(value, axis, [(i, (i + step) % size) for i in range(size)])  28.8 us
    ppermute x16, starting transfers between devices, grid_shift(): return lax.ppermute(value, axis, pairs)  27.4 us
    unnamed x29, local copies, waits for them, and re-layouts  24.2 us
    dot_general x1, matrix products, on_device(): jnp.dot(multipliers, gathered.reshape(2 * block_size, half), preferred_el...  15.9 us
    ppermute x8, starting transfers between devices, ring(): lax.ppermute(value, axis, [(i, (i + step) % size) for i in range(size)])  13.1 us
    mul x1, other arithmetic, on_device(): front[0]  11.8 us
  transfers between devices with their start and end apart: 28, of which 13 were waited for; matrix products, arithmetic and copies ran while one was open for 26% of the time, Pallas kernels for 0%

profile of v5, /device:TPU:0, one launch (start us, length us, event | category | flops | bytes accessed | tf_op | source)
XLA Modules:
  0.0 264.9 jit_solution(17646600619364398353)
XLA Ops:
  7.2 0.7 convert_bitcast_fusion
  8.1 2.7 %bitcast_multiply_fusion.1 = bf16[2,64,16384]{2,1,0:T(8,128)(2,1)S(1)} fusion(bf16[1,2,64,16384]{3,2,1,0:T(8,128)(2,1)} %param.8, bf16[2,16384]{1,0:T(2,128)(2,1)S(1)} %bitcast.170), kind=kLoop, calls=%fused_computation.10 | loop fusion | flops 2097152 | bytes 8454144 | tf_op jit(solution)/shard_map/mul | solution.py:91
  10.8 2.0 copy-done
  12.8 1.8 slice.333
  14.7 0.9 fusion.60
  15.6 4.2 %collective-permute-start = (bf16[2,64,512]{2,1,0:T(8,128)(2,1)S(1)}, bf16[2,64,512]{2,1,0:T(8,128)(2,1)S(1)}, u32[]{:S(2)}, u32[]{:S(2)}) collective-permute-start(bf16[2,64,512]{2,1,0:T(8,128)(2,1)S(1)} %get-tuple-element.20), channel_id=1, source_target_pairs={{0,6},{2,0},{4,2},{6,4},{1,7},{3,1},{5,3},{7,5},{8,14},{10,8},{12,... | collective-permute-start | bytes 393224 | tf_op jit(solution)/shard_map/ppermute | solution.py:8
  19.8 1.4 slice.332
  21.4 2.7 %mul.31 = bf16[2,256,64,256]{3,2,1,0:T(8,128)(2,1)S(1)} broadcast(bf16[2,64]{1,0:T(2,128)(2,1)S(1)} %convert_bitcast_fusion.1), dimensions={0,2} | broadcast | bytes 16777472 | tf_op jit(solution)/shard_map/mul | solution.py:87
  24.1 12.4 %copy.16 = bf16[64,8,64,256]{3,1,2,0:T(8,128)(2,1)} copy(bf16[64,8,64,256]{3,2,1,0:T(8,128)(2,1)S(1)} %bitcast.158) | data formatting | bytes 33554432
  36.7 11.8 %bitcast_multiply_fusion = bf16[512,16384]{1,0:T(8,128)(2,1)S(1)} fusion(bf16[512,16384]{1,0:T(8,128)(2,1)} %bitcast.157, bf16[1,512,16384]{2,1,0:T(8,128)(2,1)} %param.7), kind=kLoop, calls=%fused_computation.1 | loop fusion | flops 8388608 | bytes 50331648 | tf_op jit(solution)/shard_map/mul | solution.py:87
  48.5 5.8 %copy-done.2 = bf16[512,16384]{1,0:T(8,128)(2,1)} copy-done((bf16[512,16384]{1,0:T(8,128)(2,1)}, bf16[512,16384]{1,0:T(8,128)(2,1)S(1)}, u32[]{:S(2)}) %copy-start.2) | copy-done | bytes 16777240
  54.3 0.3 convolution_convert_fusion.1
  54.7 3.3 %collective-permute-start.3 = (bf16[2,32,512]{2,1,0:T(8,128)(2,1)S(1)}, bf16[2,32,512]{2,1,0:T(8,128)(2,1)S(1)}, u32[]{:S(2)}, u32[]{:S(2)}) collective-permute-start(bf16[2,32,512]{2,1,0:T(8,128)(2,1)S(1)} %slice.327), channel_id=1, source_target_pairs={{0,6},{2,0},{4,2},{6,4},{1,7},{3,1},{5,3},{7,5},{8,14},{10,8},{12,... | collective-permute-start | bytes 196616 | tf_op jit(solution)/shard_map/ppermute | solution.py:8
  58.0 3.7 %collective-permute-done.2 = bf16[2,32,512]{2,1,0:T(8,128)(2,1)S(1)} collective-permute-done((bf16[2,32,512]{2,1,0:T(8,128)(2,1)S(1)}, bf16[2,32,512]{2,1,0:T(8,128)(2,1)S(1)}, u32[]{:S(2)}, u32[]{:S(2)}) %collective-permute-start.2) | collective-permute-done | bytes 65568 | tf_op jit(solution)/shard_map/ppermute | solution.py:8
  61.8 0.9 constant_dynamic-update-slice_fusion.4
  62.8 0.7 dynamic-slice_bitcast_fusion.4
  63.7 1.3 collective-permute-start.5
  65.0 1.5 convolution_convert_fusion
  66.6 1.3 collective-permute-start.4
  68.0 1.4 collective-permute-done.4
  69.6 1.0 copy.12
  70.6 0.3 subtract_convert_fusion
  70.8 57.6 %all-gather.2.cloned.1.call-done = bf16[2,256,11264]{2,1,0:T(8,128)(2,1)} async-done(((bf16[2,64,11264]{2,1,0:T(8,128)(2,1)}), bf16[2,256,11264]{2,1,0:T(8,128)(2,1)}) %all-gather.2.cloned.1.call-update) | async-done | bytes 11534352 | tf_op jit(solution)/shard_map/all_gather | solution.py:102
  128.4 1.4 collective-permute-start.6
  129.9 0.6 collective-permute-start.7
  130.5 15.9 %select_convert_fusion = bf16[512,11264]{1,0:T(8,128)(2,1)} fusion(bf16[512,11264]{1,0:T(8,128)(2,1)} %bitcast.169, bf16[512,16384]{1,0:T(8,128)(2,1)} %copy-done.2, pred[11264]{0:T(1024)(128)(4,1)S(1)} %slice-done, bf16[512,256]{0,1:T(8,128)(2,1)S(1)} %slice.330, bf16[512,256]{0,1:T(8,128)(2,1)S(1)} %subtract_convert_fusion), kind=kOutput, calls=%fused_computation | convolution fusion | flops 5929697280 | bytes 35138560 | tf_op jit(solution)/shard_map/dot_general | solution.py:144
  146.4 0.4 fusion.24
  146.9 14.3 %collective-permute-done.7 = bf16[2,64,5120]{2,1,0:T(8,128)(2,1)S(1)} collective-permute-done((bf16[2,64,5120]{2,1,0:T(8,128)(2,1)S(1)}, bf16[2,64,5120]{2,1,0:T(8,128)(2,1)S(1)}, u32[]{:S(2)}, u32[]{:S(2)}) %collective-permute-start.7) | collective-permute-done | bytes 1310752 | tf_op jit(solution)/shard_map/ppermute | solution.py:8
  161.2 0.3 collective-permute-start.8
  161.5 3.9 %fusion = bf16[64,11264]{1,0:T(8,128)(2,1)S(1)} fusion(bf16[64,256]{1,0:T(8,128)(2,1)S(1)} %constant_dynamic-slice_fusion, bf16[2,256,11264]{2,1,0:T(8,128)(2,1)} %all-gather.2.cloned.1.call-done, bf16[2,64,16384]{2,1,0:T(8,128)(2,1)S(1)} %copy-done.1), kind=kOutput, calls=%fused_computation.3 | convolution fusion | flops 371261440 | bytes 8683520 | tf_op jit(solution)/shard_map/dot_general | solution.py:159
  165.4 1.1 slice.337
  166.5 3.3 %collective-permute-start.9 = (bf16[2,32,5120]{2,1,0:T(8,128)(2,1)S(1)}, bf16[2,32,5120]{2,1,0:T(8,128)(2,1)S(1)}, u32[]{:S(2)}, u32[]{:S(2)}) collective-permute-start(bf16[2,32,5120]{2,1,0:T(8,128)(2,1)S(1)} %slice.337), channel_id=1, source_target_pairs={{0,6},{2,0},{4,2},{6,4},{1,7},{3,1},{5,3},{7,5},{8,14},{10,8},{12,... | collective-permute-start | bytes 1966088 | tf_op jit(solution)/shard_map/ppermute | solution.py:8
  169.8 1.4 constant_dynamic-update-slice_fusion.13
  171.2 6.6 %collective-permute-done.8 = bf16[2,32,5120]{2,1,0:T(8,128)(2,1)S(1)} collective-permute-done((bf16[2,32,5120]{2,1,0:T(8,128)(2,1)S(1)}, bf16[2,32,5120]{2,1,0:T(8,128)(2,1)S(1)}, u32[]{:S(2)}, u32[]{:S(2)}) %collective-permute-start.8) | collective-permute-done | bytes 655392 | tf_op jit(solution)/shard_map/ppermute | solution.py:8
  177.8 4.2 %collective-permute-done.9 = bf16[2,32,5120]{2,1,0:T(8,128)(2,1)S(1)} collective-permute-done((bf16[2,32,5120]{2,1,0:T(8,128)(2,1)S(1)}, bf16[2,32,5120]{2,1,0:T(8,128)(2,1)S(1)}, u32[]{:S(2)}, u32[]{:S(2)}) %collective-permute-start.9) | collective-permute-done | bytes 655392 | tf_op jit(solution)/shard_map/ppermute | solution.py:8
  182.2 3.4 %subtract_select_fusion.1 = f32[512,2560]{1,0:T(8,128)S(1)} fusion(bf16[512,5120]{1,0:T(8,128)(2,1)S(1)} %bitcast.167, bf16[512,16384]{1,0:T(8,128)(2,1)} %copy-done.2, pred[2560]{0:T(1024)(128)(4,1)S(1)} %get-tuple-element.40, bf16[512,256]{0,1:T(8,128)(2,1)S(1)} %get-tuple-element.42, bf16[512,256]{0,1:T(8,128)(2,1)S(1)} %get-tuple-element.43), kind=kOutput, calls=%fused_computation.9 | convolution fusion | flops 1347158016 | bytes 11013120 | tf_op jit(solution)/shard_map/dot_general | solution.py:177
  185.8 2.1 collective-permute-start.10
  187.9 1.5 collective-permute-start.12
  189.4 3.4 %subtract_select_fusion = f32[512,2560]{1,0:T(8,128)S(1)} fusion(bf16[512,5120]{1,0:T(8,128)(2,1)S(1)} %bitcast.168, bf16[512,16384]{1,0:T(8,128)(2,1)} %copy-done.2, pred[2560]{0:T(1024)(128)(4,1)S(1)} %get-tuple-element.41, bf16[512,256]{0,1:T(8,128)(2,1)S(1)} %get-tuple-element.42, bf16[512,256]{0,1:T(8,128)(2,1)S(1)} %get-tuple-element.43), kind=kOutput, calls=%fused_computation.8 | convolution fusion | flops 1347158016 | bytes 11013120 | tf_op jit(solution)/shard_map/dot_general | solution.py:177
  192.9 1.9 collective-permute-start.18
  194.8 1.5 collective-permute-start.20
  196.3 0.6 fusion.1
  196.9 0.3 dynamic-slice_bitcast_fusion.1
  197.3 1.5 maximum_bitcast_fusion.1
  198.8 5.0 %collective-permute-done.10 = bf16[2,32,2560]{2,1,0:T(8,128)(2,1)S(1)} collective-permute-done((bf16[2,32,2560]{2,1,0:T(8,128)(2,1)S(1)}, bf16[2,32,2560]{2,1,0:T(8,128)(2,1)S(1)}, u32[]{:S(2)}, u32[]{:S(2)}) %collective-permute-start.10) | collective-permute-done | bytes 327712 | tf_op jit(solution)/shard_map/ppermute | solution.py:26
  203.9 0.7 collective-permute-start.11
  204.7 2.7 %collective-permute-start.13 = (bf16[4,32,2560]{2,1,0:T(8,128)(2,1)S(1)}, bf16[4,32,2560]{2,1,0:T(8,128)(2,1)S(1)}, u32[]{:S(2)}, u32[]{:S(2)}) collective-permute-start(bf16[4,32,2560]{2,1,0:T(8,128)(2,1)S(1)} %pad_maximum_fusion.1), channel_id=1, source_target_pairs={{0,24},{8,0},{16,8},{24,16},{32,56},{40,32},{48,40},{56,48},{64,88... | collective-permute-start | bytes 1966088 | tf_op jit(solution)/shard_map/ppermute | solution.py:26
  207.4 1.8 collective-permute-done.18
  209.3 0.6 collective-permute-done.20
  210.1 1.8 collective-permute-start.19
  211.9 1.6 collective-permute-start.21
  213.5 16.7 %collective-permute-done.11 = bf16[4,32,2560]{2,1,0:T(8,128)(2,1)S(1)} collective-permute-done((bf16[4,32,2560]{2,1,0:T(8,128)(2,1)S(1)}, bf16[4,32,2560]{2,1,0:T(8,128)(2,1)S(1)}, u32[]{:S(2)}, u32[]{:S(2)}) %collective-permute-start.11) | collective-permute-done | bytes 655392 | tf_op jit(solution)/shard_map/ppermute | solution.py:26
  230.2 0.2 fusion.7
  230.5 0.5 collective-permute-start.14
  231.0 2.8 %collective-permute-start.16 = (bf16[16,2560]{1,0:T(8,128)(2,1)S(1)}, bf16[16,2560]{1,0:T(8,128)(2,1)S(1)}, u32[]{:S(2)}, u32[]{:S(2)}) collective-permute-start(bf16[16,2560]{1,0:T(8,128)(2,1)S(1)} %get-tuple-element.37), channel_id=1, source_target_pairs={{0,96},{8,104},{16,112},{24,120},{32,0},{40,8},{48,16},{56,24},{64... | collective-permute-start | bytes 245768 | tf_op jit(solution)/shard_map/ppermute | solution.py:26
  234.4 3.1 %collective-permute-start.24 = (bf16[16,2560]{1,0:T(8,128)(2,1)S(1)}, bf16[16,2560]{1,0:T(8,128)(2,1)S(1)}, u32[]{:S(2)}, u32[]{:S(2)}) collective-permute-start(bf16[16,2560]{1,0:T(8,128)(2,1)S(1)} %get-tuple-element.39), channel_id=1, source_target_pairs={{0,24},{8,0},{16,8},{24,16},{32,56},{40,32},{48,40},{56,48},{64,88... | collective-permute-start | bytes 245768 | tf_op jit(solution)/shard_map/ppermute | solution.py:26
  237.6 3.7 %collective-permute-start.17 = (bf16[32,2560]{1,0:T(8,128)(2,1)S(1)}, bf16[32,2560]{1,0:T(8,128)(2,1)S(1)}, u32[]{:S(2)}, u32[]{:S(2)}) collective-permute-start(bf16[32,2560]{1,0:T(8,128)(2,1)S(1)} %pad_maximum_fusion.11), channel_id=1, source_target_pairs={{0,96},{8,104},{16,112},{24,120},{32,0},{40,8},{48,16},{56,24},{64... | collective-permute-start | bytes 491528 | tf_op jit(solution)/shard_map/ppermute | solution.py:26
  241.4 0.3 collective-permute-start.23
  241.7 3.1 %collective-permute-start.25 = (bf16[32,2560]{1,0:T(8,128)(2,1)S(1)}, bf16[32,2560]{1,0:T(8,128)(2,1)S(1)}, u32[]{:S(2)}, u32[]{:S(2)}) collective-permute-start(bf16[32,2560]{1,0:T(8,128)(2,1)S(1)} %pad_maximum_fusion.13), channel_id=1, source_target_pairs={{0,24},{8,0},{16,8},{24,16},{32,56},{40,32},{48,40},{56,48},{64,88... | collective-permute-start | bytes 491528 | tf_op jit(solution)/shard_map/ppermute | solution.py:26
  244.8 3.6 %collective-permute-done.15 = bf16[32,2560]{1,0:T(8,128)(2,1)S(1)} collective-permute-done((bf16[32,2560]{1,0:T(8,128)(2,1)S(1)}, bf16[32,2560]{1,0:T(8,128)(2,1)S(1)}, u32[]{:S(2)}, u32[]{:S(2)}) %collective-permute-start.15) | collective-permute-done | bytes 163872 | tf_op jit(solution)/shard_map/ppermute | solution.py:26
  248.4 3.3 %collective-permute-done.23 = bf16[32,2560]{1,0:T(8,128)(2,1)S(1)} collective-permute-done((bf16[32,2560]{1,0:T(8,128)(2,1)S(1)}, bf16[32,2560]{1,0:T(8,128)(2,1)S(1)}, u32[]{:S(2)}, u32[]{:S(2)}) %collective-permute-start.23) | collective-permute-done | bytes 163872 | tf_op jit(solution)/shard_map/ppermute | solution.py:26
  251.8 3.7 %reduce-scatter.2.cloned.1.call-done = bf16[32,11264]{1,0:T(8,128)(2,1)} async-done(((bf16[512,11264]{1,0:T(8,128)(2,1)}), bf16[32,11264]{1,0:T(8,128)(2,1)}) %reduce-scatter.2.cloned.1.call-update) | async-done | bytes 720912 | tf_op jit(solution)/shard_map/reduce_scatter | solution.py:150
  255.4 1.2 convert_element_type.159
  256.6 1.5 maximum_bitcast_fusion
  (90 shorter events, 3.0 us)
Async XLA Ops:
  7.2 121.3 %all-gather.2.cloned.1.call-start = ((), (), s32[]{:S(2)}) async-start(), calls=%async_computation.1 | async-start | bytes 14417920 | tf_op jit(solution)/shard_map/all_gather | solution.py:102
  10.8 2.0 copy-start
  14.6 6.8 %copy-start.5 = (s32[1,2,64]{2,1,0:T(2,128)S(1)}, s32[1,2,64]{2,1,0:T(2,128)}, u32[]{:S(2)}) copy-start(s32[1,2,64]{2,1,0:T(2,128)} %param.10) | copy-start | bytes 1540
  14.6 240.8 %reduce-scatter.2.cloned.1.call-start = ((), (), s32[]{:S(2)}) async-start(), calls=%async_computation.2 | async-start | bytes 12255232 | tf_op jit(solution)/shard_map/reduce_scatter | solution.py:150
  15.6 39.1 %collective-permute-start = (bf16[2,64,512]{2,1,0:T(8,128)(2,1)S(1)}, bf16[2,64,512]{2,1,0:T(8,128)(2,1)S(1)}, u32[]{:S(2)}, u32[]{:S(2)}) collective-permute-start(bf16[2,64,512]{2,1,0:T(8,128)(2,1)S(1)} %get-tuple-element.20), channel_id=1, source_target_pairs={{0,6},{2,0},{4,2},{6,4},{1,7},{3,1},{5,3},{7,5},{8,14},{10,8},{12,... | collective-permute-start | bytes 393224 | tf_op jit(solution)/shard_map/ppermute | solution.py:8
  19.8 34.8 %collective-permute-start.1 = (bf16[2,64,512]{2,1,0:T(8,128)(2,1)S(1)}, bf16[2,64,512]{2,1,0:T(8,128)(2,1)S(1)}, u32[]{:S(2)}, u32[]{:S(2)}) collective-permute-start(bf16[2,64,512]{2,1,0:T(8,128)(2,1)S(1)} %get-tuple-element.20), channel_id=1, source_target_pairs={{0,2},{2,4},{4,6},{6,0},{1,3},{3,5},{5,7},{7,1},{8,10},{10,12},{12... | collective-permute-start | bytes 393224 | tf_op jit(solution)/shard_map/ppermute | solution.py:8
  36.6 31.3 %copy-start.4 = (pred[16384]{0:T(1024)(128)(4,1)}, pred[16384]{0:T(1024)(128)(4,1)S(1)}, u32[]{:S(2)}) copy-start(pred[16384]{0:T(1024)(128)(4,1)S(1)} %add_compare_fusion) | copy-start | bytes 49156
  36.7 17.6 %copy-start.3 = (bf16[1,2,256,256]{3,2,1,0:T(8,128)(2,1)S(1)}, bf16[1,2,256,256]{3,2,1,0:T(8,128)(2,1)}, u32[]{:S(2)}) copy-start(bf16[1,2,256,256]{3,2,1,0:T(8,128)(2,1)} %param.9) | copy-start | bytes 786436
  48.5 5.8 %copy-start.2 = (bf16[512,16384]{1,0:T(8,128)(2,1)}, bf16[512,16384]{1,0:T(8,128)(2,1)S(1)}, u32[]{:S(2)}) copy-start(bf16[512,16384]{1,0:T(8,128)(2,1)S(1)} %bitcast_multiply_fusion) | copy-start | bytes 50331652
  54.6 7.1 %collective-permute-start.2 = (bf16[2,32,512]{2,1,0:T(8,128)(2,1)S(1)}, bf16[2,32,512]{2,1,0:T(8,128)(2,1)S(1)}, u32[]{:S(2)}, u32[]{:S(2)}) collective-permute-start(bf16[2,32,512]{2,1,0:T(8,128)(2,1)S(1)} %slice.326), channel_id=1, source_target_pairs={{0,2},{2,4},{4,6},{6,0},{1,3},{3,5},{5,7},{7,1},{8,10},{10,12},{12... | collective-permute-start | bytes 196616 | tf_op jit(solution)/shard_map/ppermute | solution.py:8
  54.7 7.0 %collective-permute-start.3 = (bf16[2,32,512]{2,1,0:T(8,128)(2,1)S(1)}, bf16[2,32,512]{2,1,0:T(8,128)(2,1)S(1)}, u32[]{:S(2)}, u32[]{:S(2)}) collective-permute-start(bf16[2,32,512]{2,1,0:T(8,128)(2,1)S(1)} %slice.327), channel_id=1, source_target_pairs={{0,6},{2,0},{4,2},{6,4},{1,7},{3,1},{5,3},{7,5},{8,14},{10,8},{12,... | collective-permute-start | bytes 196616 | tf_op jit(solution)/shard_map/ppermute | solution.py:8
  63.7 4.2 %collective-permute-start.5 = (bf16[256,256]{1,0:T(8,128)(2,1)S(1)}, bf16[256,256]{1,0:T(8,128)(2,1)S(1)}, u32[]{:S(2)}, u32[]{:S(2)}) collective-permute-start(bf16[256,256]{1,0:T(8,128)(2,1)S(1)} %convolution_convert_fusion.2), channel_id=1, source_target_pairs={{0,1},{2,3},{4,5},{6,7},{8,9},{10,11},{12,13},{14,15},{16,17},{18,... | collective-permute-start | bytes 393224 | tf_op jit(solution)/shard_map/ppermute | solution.py:126
  66.6 2.8 %collective-permute-start.4 = (bf16[512,512]{0,1:T(8,128)(2,1)S(1)}, bf16[512,512]{0,1:T(8,128)(2,1)S(1)}, u32[]{:S(2)}, u32[]{:S(2)}) collective-permute-start(bf16[512,512]{0,1:T(8,128)(2,1)S(1)} %pad_maximum_fusion.6), channel_id=1, source_target_pairs={{0,1},{2,3},{4,5},{6,7},{8,9},{10,11},{12,13},{14,15},{16,17},{18,... | collective-permute-start | bytes 1572872 | tf_op jit(solution)/shard_map/ppermute | solution.py:126
  67.9 62.5 %slice-start = ((pred[16384]{0:T(1024)(128)(4,1)}), pred[11264]{0:T(1024)(128)(4,1)S(1)}, s32[]{:S(2)}) async-start(pred[16384]{0:T(1024)(128)(4,1)} %copy-done.4), calls=%async_computation.3 | async-start | bytes 22528 | tf_op jit(solution)/shard_map/slice | solution.py:147
  128.4 36.9 %collective-permute-start.6 = (bf16[2,64,5120]{2,1,0:T(8,128)(2,1)S(1)}, bf16[2,64,5120]{2,1,0:T(8,128)(2,1)}, u32[]{:S(2)}, u32[]{:S(2)}) collective-permute-start(bf16[2,64,5120]{2,1,0:T(8,128)(2,1)S(1)} %slice.332), channel_id=1, source_target_pairs={{0,6},{2,0},{4,2},{6,4},{1,7},{3,1},{5,3},{7,5},{8,14},{10,8},{12,... | collective-permute-start | bytes 3932168 | tf_op jit(solution)/shard_map/ppermute | solution.py:8
  129.9 31.3 %collective-permute-start.7 = (bf16[2,64,5120]{2,1,0:T(8,128)(2,1)S(1)}, bf16[2,64,5120]{2,1,0:T(8,128)(2,1)S(1)}, u32[]{:S(2)}, u32[]{:S(2)}) collective-permute-start(bf16[2,64,5120]{2,1,0:T(8,128)(2,1)S(1)} %slice.332), channel_id=1, source_target_pairs={{0,2},{2,4},{4,6},{6,0},{1,3},{3,5},{5,7},{7,1},{8,10},{10,12},{12... | collective-permute-start | bytes 3932168 | tf_op jit(solution)/shard_map/ppermute | solution.py:8
  146.4 15.1 %copy-start.1 = (bf16[2,64,16384]{2,1,0:T(8,128)(2,1)S(1)}, bf16[2,64,16384]{2,1,0:T(8,128)(2,1)}, u32[]{:S(2)}) copy-start(bf16[2,64,16384]{2,1,0:T(8,128)(2,1)} %copy-done) | copy-start | bytes 12582916
  161.2 16.6 %collective-permute-start.8 = (bf16[2,32,5120]{2,1,0:T(8,128)(2,1)S(1)}, bf16[2,32,5120]{2,1,0:T(8,128)(2,1)S(1)}, u32[]{:S(2)}, u32[]{:S(2)}) collective-permute-start(bf16[2,32,5120]{2,1,0:T(8,128)(2,1)S(1)} %slice.336), channel_id=1, source_target_pairs={{0,2},{2,4},{4,6},{6,0},{1,3},{3,5},{5,7},{7,1},{8,10},{10,12},{12... | collective-permute-start | bytes 1966088 | tf_op jit(solution)/shard_map/ppermute | solution.py:8
  166.5 15.6 %collective-permute-start.9 = (bf16[2,32,5120]{2,1,0:T(8,128)(2,1)S(1)}, bf16[2,32,5120]{2,1,0:T(8,128)(2,1)S(1)}, u32[]{:S(2)}, u32[]{:S(2)}) collective-permute-start(bf16[2,32,5120]{2,1,0:T(8,128)(2,1)S(1)} %slice.337), channel_id=1, source_target_pairs={{0,6},{2,0},{4,2},{6,4},{1,7},{3,1},{5,3},{7,5},{8,14},{10,8},{12,... | collective-permute-start | bytes 1966088 | tf_op jit(solution)/shard_map/ppermute | solution.py:8
  185.8 18.0 %collective-permute-start.10 = (bf16[2,32,2560]{2,1,0:T(8,128)(2,1)S(1)}, bf16[2,32,2560]{2,1,0:T(8,128)(2,1)S(1)}, u32[]{:S(2)}, u32[]{:S(2)}) collective-permute-start(bf16[2,32,2560]{2,1,0:T(8,128)(2,1)S(1)} %get-tuple-element.32), channel_id=1, source_target_pairs={{0,8},{8,16},{16,24},{24,0},{32,40},{40,48},{48,56},{56,32},{64,72... | collective-permute-start | bytes 983048 | tf_op jit(solution)/shard_map/ppermute | solution.py:26
  187.9 16.7 %collective-permute-start.12 = (bf16[2,32,2560]{2,1,0:T(8,128)(2,1)S(1)}, bf16[2,32,2560]{2,1,0:T(8,128)(2,1)S(1)}, u32[]{:S(2)}, u32[]{:S(2)}) collective-permute-start(bf16[2,32,2560]{2,1,0:T(8,128)(2,1)S(1)} %get-tuple-element.33), channel_id=1, source_target_pairs={{0,24},{8,0},{16,8},{24,16},{32,56},{40,32},{48,40},{56,48},{64,88... | collective-permute-start | bytes 983048 | tf_op jit(solution)/shard_map/ppermute | solution.py:26
  192.9 16.3 %collective-permute-start.18 = (bf16[2,32,2560]{2,1,0:T(8,128)(2,1)S(1)}, bf16[2,32,2560]{2,1,0:T(8,128)(2,1)S(1)}, u32[]{:S(2)}, u32[]{:S(2)}) collective-permute-start(bf16[2,32,2560]{2,1,0:T(8,128)(2,1)S(1)} %get-tuple-element.34), channel_id=1, source_target_pairs={{0,32},{8,40},{16,48},{24,56},{32,64},{40,72},{48,80},{56,88},{64,... | collective-permute-start | bytes 983048 | tf_op jit(solution)/shard_map/ppermute | solution.py:26
  194.8 15.1 %collective-permute-start.20 = (bf16[2,32,2560]{2,1,0:T(8,128)(2,1)S(1)}, bf16[2,32,2560]{2,1,0:T(8,128)(2,1)S(1)}, u32[]{:S(2)}, u32[]{:S(2)}) collective-permute-start(bf16[2,32,2560]{2,1,0:T(8,128)(2,1)S(1)} %get-tuple-element.35), channel_id=1, source_target_pairs={{0,96},{8,104},{16,112},{24,120},{32,0},{40,8},{48,16},{56,24},{64... | collective-permute-start | bytes 983048 | tf_op jit(solution)/shard_map/ppermute | solution.py:26
  203.9 26.3 %collective-permute-start.11 = (bf16[4,32,2560]{2,1,0:T(8,128)(2,1)S(1)}, bf16[4,32,2560]{2,1,0:T(8,128)(2,1)S(1)}, u32[]{:S(2)}, u32[]{:S(2)}) collective-permute-start(bf16[4,32,2560]{2,1,0:T(8,128)(2,1)S(1)} %pad_maximum_fusion), channel_id=1, source_target_pairs={{0,8},{8,16},{16,24},{24,0},{32,40},{40,48},{48,56},{56,32},{64,72... | collective-permute-start | bytes 1966088 | tf_op jit(solution)/shard_map/ppermute | solution.py:26
  204.7 25.4 %collective-permute-start.13 = (bf16[4,32,2560]{2,1,0:T(8,128)(2,1)S(1)}, bf16[4,32,2560]{2,1,0:T(8,128)(2,1)S(1)}, u32[]{:S(2)}, u32[]{:S(2)}) collective-permute-start(bf16[4,32,2560]{2,1,0:T(8,128)(2,1)S(1)} %pad_maximum_fusion.1), channel_id=1, source_target_pairs={{0,24},{8,0},{16,8},{24,16},{32,56},{40,32},{48,40},{56,48},{64,88... | collective-permute-start | bytes 1966088 | tf_op jit(solution)/shard_map/ppermute | solution.py:26
  210.1 23.7 %collective-permute-start.19 = (bf16[4,32,2560]{2,1,0:T(8,128)(2,1)S(1)}, bf16[4,32,2560]{2,1,0:T(8,128)(2,1)S(1)}, u32[]{:S(2)}, u32[]{:S(2)}) collective-permute-start(bf16[4,32,2560]{2,1,0:T(8,128)(2,1)S(1)} %pad_maximum_fusion.2), channel_id=1, source_target_pairs={{0,32},{8,40},{16,48},{24,56},{32,64},{40,72},{48,80},{56,88},{64,... | collective-permute-start | bytes 1966088 | tf_op jit(solution)/shard_map/ppermute | solution.py:26
  211.9 21.9 %collective-permute-start.21 = (bf16[4,32,2560]{2,1,0:T(8,128)(2,1)S(1)}, bf16[4,32,2560]{2,1,0:T(8,128)(2,1)S(1)}, u32[]{:S(2)}, u32[]{:S(2)}) collective-permute-start(bf16[4,32,2560]{2,1,0:T(8,128)(2,1)S(1)} %pad_maximum_fusion.3), channel_id=1, source_target_pairs={{0,96},{8,104},{16,112},{24,120},{32,0},{40,8},{48,16},{56,24},{64... | collective-permute-start | bytes 1966088 | tf_op jit(solution)/shard_map/ppermute | solution.py:26
  230.5 7.0 %collective-permute-start.14 = (bf16[16,2560]{1,0:T(8,128)(2,1)S(1)}, bf16[16,2560]{1,0:T(8,128)(2,1)S(1)}, u32[]{:S(2)}, u32[]{:S(2)}) collective-permute-start(bf16[16,2560]{1,0:T(8,128)(2,1)S(1)} %get-tuple-element.36), channel_id=1, source_target_pairs={{0,32},{8,40},{16,48},{24,56},{32,64},{40,72},{48,80},{56,88},{64,... | collective-permute-start | bytes 245768 | tf_op jit(solution)/shard_map/ppermute | solution.py:26
  231.0 6.5 %collective-permute-start.16 = (bf16[16,2560]{1,0:T(8,128)(2,1)S(1)}, bf16[16,2560]{1,0:T(8,128)(2,1)S(1)}, u32[]{:S(2)}, u32[]{:S(2)}) collective-permute-start(bf16[16,2560]{1,0:T(8,128)(2,1)S(1)} %get-tuple-element.37), channel_id=1, source_target_pairs={{0,96},{8,104},{16,112},{24,120},{32,0},{40,8},{48,16},{56,24},{64... | collective-permute-start | bytes 245768 | tf_op jit(solution)/shard_map/ppermute | solution.py:26
  234.2 7.1 %collective-permute-start.22 = (bf16[16,2560]{1,0:T(8,128)(2,1)S(1)}, bf16[16,2560]{1,0:T(8,128)(2,1)S(1)}, u32[]{:S(2)}, u32[]{:S(2)}) collective-permute-start(bf16[16,2560]{1,0:T(8,128)(2,1)S(1)} %get-tuple-element.38), channel_id=1, source_target_pairs={{0,8},{8,16},{16,24},{24,0},{32,40},{40,48},{48,56},{56,32},{64,72... | collective-permute-start | bytes 245768 | tf_op jit(solution)/shard_map/ppermute | solution.py:26
  234.4 6.9 %collective-permute-start.24 = (bf16[16,2560]{1,0:T(8,128)(2,1)S(1)}, bf16[16,2560]{1,0:T(8,128)(2,1)S(1)}, u32[]{:S(2)}, u32[]{:S(2)}) collective-permute-start(bf16[16,2560]{1,0:T(8,128)(2,1)S(1)} %get-tuple-element.39), channel_id=1, source_target_pairs={{0,24},{8,0},{16,8},{24,16},{32,56},{40,32},{48,40},{56,48},{64,88... | collective-permute-start | bytes 245768 | tf_op jit(solution)/shard_map/ppermute | solution.py:26
  237.5 10.8 %collective-permute-start.15 = (bf16[32,2560]{1,0:T(8,128)(2,1)S(1)}, bf16[32,2560]{1,0:T(8,128)(2,1)S(1)}, u32[]{:S(2)}, u32[]{:S(2)}) collective-permute-start(bf16[32,2560]{1,0:T(8,128)(2,1)S(1)} %pad_maximum_fusion.10), channel_id=1, source_target_pairs={{0,32},{8,40},{16,48},{24,56},{32,64},{40,72},{48,80},{56,88},{64,... | collective-permute-start | bytes 491528 | tf_op jit(solution)/shard_map/ppermute | solution.py:26
  237.6 10.7 %collective-permute-start.17 = (bf16[32,2560]{1,0:T(8,128)(2,1)S(1)}, bf16[32,2560]{1,0:T(8,128)(2,1)S(1)}, u32[]{:S(2)}, u32[]{:S(2)}) collective-permute-start(bf16[32,2560]{1,0:T(8,128)(2,1)S(1)} %pad_maximum_fusion.11), channel_id=1, source_target_pairs={{0,96},{8,104},{16,112},{24,120},{32,0},{40,8},{48,16},{56,24},{64... | collective-permute-start | bytes 491528 | tf_op jit(solution)/shard_map/ppermute | solution.py:26
  241.4 10.3 %collective-permute-start.23 = (bf16[32,2560]{1,0:T(8,128)(2,1)S(1)}, bf16[32,2560]{1,0:T(8,128)(2,1)S(1)}, u32[]{:S(2)}, u32[]{:S(2)}) collective-permute-start(bf16[32,2560]{1,0:T(8,128)(2,1)S(1)} %pad_maximum_fusion.12), channel_id=1, source_target_pairs={{0,8},{8,16},{16,24},{24,0},{32,40},{40,48},{48,56},{56,32},{64,72... | collective-permute-start | bytes 491528 | tf_op jit(solution)/shard_map/ppermute | solution.py:26
  241.7 10.0 %collective-permute-start.25 = (bf16[32,2560]{1,0:T(8,128)(2,1)S(1)}, bf16[32,2560]{1,0:T(8,128)(2,1)S(1)}, u32[]{:S(2)}, u32[]{:S(2)}) collective-permute-start(bf16[32,2560]{1,0:T(8,128)(2,1)S(1)} %pad_maximum_fusion.13), channel_id=1, source_target_pairs={{0,24},{8,0},{16,8},{24,16},{32,56},{40,32},{48,40},{56,48},{64,88... | collective-permute-start | bytes 491528 | tf_op jit(solution)/shard_map/ppermute | solution.py:26
Sparse Core Ops, SparseCore 0:
  14.7 113.6 all-gather.1
  146.5 108.9 reduce-scatter.1

commit v6 on v5

--- a/solution.py
+++ b/solution.py
@@ -99,7 +99,11 @@
     n_pcol = lax.axis_size("pcol")
     assert n_prow == 4
     half = (col_count * 11 // 16) // block_size * block_size
-    gathered = lax.all_gather(pivot_masked[:, :, :half], "prow", axis=1, tiled=True)
+    gathered = lax.all_gather(pivots[0, :, :, :half], "prow", axis=1, tiled=True)
+    gathered = (
+        gathered.reshape(2, 4 * own_rows, half // block_size, block_size)
+        * pivot_pattern[0, :, : half // block_size].astype(jnp.bfloat16)[:, None, :, None]
+    ).reshape(2, 4 * own_rows, half)
     later_cols, gathered = lax.optimization_barrier((pivot_masked[:, :, half:], gathered))
     panel = jnp.roll(
         gather_relative(pivot_masked[:, :, :panel_width], "prow", n_prow), row_offset, axis=1

time: 266 us -> 273 us (1.026)
  other arithmetic: 21.2 us -> 30.8 us
  waiting for transfers between devices: 122 us -> 119 us
    mul x0 -> x1, other arithmetic: none -> 10.1 us  [on_device(): gathered.reshape(2, 4 * own_rows, half // block_size, block_size)]
    all_gather x1, waiting for transfers between devices: 57.6 us -> 53.2 us  [on_device(): lax.all_gather(pivots[0, :, :, :half], 'prow', axis=1, tiled=True)]
    unnamed x29 -> x33, local copies, waits for them, and re-layouts: 24.2 us -> 24.3 us
  transfers between devices with their start and end apart: 28 -> 28, of which waited for: 13 -> 14; matrix products, arithmetic and copies ran while one was open for 26% -> 26% of each run, Pallas kernels for 0% -> 0%
where the time goes in v6:
time: 273 us; the launch traced here: 272 us
  waiting for transfers between devices  119 us (44%)
  starting transfers between devices  43.1 us (16%)
  local copies, waits for them, and re-layouts  34.7 us (13%)
  other arithmetic  30.8 us (11%)
  matrix products  29.4 us (11%)
  between operations  15 us (5%)
    all_gather x1, waiting for transfers between devices, on_device(): lax.all_gather(pivots[0, :, :, :half], 'prow', axis=1, tiled=True)  53.2 us
    ppermute x16, waiting for transfers between devices, grid_shift(): return lax.ppermute(value, axis, pairs)  31.2 us
    ppermute x8, waiting for transfers between devices, ring(): lax.ppermute(value, axis, [(i, (i + step) % size) for i in range(size)])  28.8 us
    ppermute x16, starting transfers between devices, grid_shift(): return lax.ppermute(value, axis, pairs)  27.2 us
    unnamed x33, local copies, waits for them, and re-layouts  24.3 us
    dot_general x1, matrix products, on_device(): jnp.dot(multipliers, gathered.reshape(2 * block_size, half), preferred_el...  15.9 us
    ppermute x8, starting transfers between devices, ring(): lax.ppermute(value, axis, [(i, (i + step) % size) for i in range(size)])  13.2 us
    mul x1, other arithmetic, on_device(): front[0]  12 us
  transfers between devices with their start and end apart: 28, of which 14 were waited for; matrix products, arithmetic and copies ran while one was open for 26% of the time, Pallas kernels for 0%

profile of v6, /device:TPU:0, one launch (start us, length us, event | category | flops | bytes accessed | tf_op | source)
XLA Modules:
  0.0 271.6 jit_solution(6573858306555840210)
XLA Ops:
  7.2 3.6 %slice.264 = bf16[1,2,64,11264]{3,2,1,0:T(8,128)(2,1)} slice(bf16[1,2,64,16384]{3,2,1,0:T(8,128)(2,1)} %param.8), slice={[0:1], [0:2], [0:64], [0:11264]} | slice | bytes 5767168 | tf_op jit(solution)/shard_map/slice | solution.py:102
  11.1 2.7 %bitcast_multiply_fusion.2 = bf16[2,64,16384]{2,1,0:T(8,128)(2,1)S(1)} fusion(bf16[1,2,64,16384]{3,2,1,0:T(8,128)(2,1)} %param.8, bf16[2,16384]{1,0:T(2,128)(2,1)S(1)} %bitcast.177), kind=kLoop, calls=%fused_computation.11 | loop fusion | flops 2097152 | bytes 8454144 | tf_op jit(solution)/shard_map/mul | solution.py:91
  13.8 2.0 copy-done.1
  15.8 4.2 %collective-permute-start = (bf16[2,64,512]{2,1,0:T(8,128)(2,1)S(1)}, bf16[2,64,512]{2,1,0:T(8,128)(2,1)S(1)}, u32[]{:S(2)}, u32[]{:S(2)}) collective-permute-start(bf16[2,64,512]{2,1,0:T(8,128)(2,1)S(1)} %get-tuple-element.20), channel_id=1, source_target_pairs={{0,6},{2,0},{4,2},{6,4},{1,7},{3,1},{5,3},{7,5},{8,14},{10,8},{12,... | collective-permute-start | bytes 393224 | tf_op jit(solution)/shard_map/ppermute | solution.py:8
  20.0 1.4 slice.337
  21.8 2.7 %mul.44 = bf16[2,256,64,256]{3,2,1,0:T(8,128)(2,1)S(1)} broadcast(bf16[2,64]{1,0:T(2,128)(2,1)S(1)} %convert_bitcast_fusion), dimensions={0,2} | broadcast | bytes 16777472 | tf_op jit(solution)/shard_map/mul | solution.py:87
  24.5 12.4 %copy.16 = bf16[64,8,64,256]{3,1,2,0:T(8,128)(2,1)} copy(bf16[64,8,64,256]{3,2,1,0:T(8,128)(2,1)S(1)} %bitcast.165) | data formatting | bytes 33554432
  37.1 12.0 %bitcast_multiply_fusion = bf16[512,16384]{1,0:T(8,128)(2,1)S(1)} fusion(bf16[512,16384]{1,0:T(8,128)(2,1)} %bitcast.164, bf16[1,512,16384]{2,1,0:T(8,128)(2,1)} %param.7), kind=kLoop, calls=%fused_computation.1 | loop fusion | flops 8388608 | bytes 50331648 | tf_op jit(solution)/shard_map/mul | solution.py:87
  49.1 5.8 %copy-done = bf16[512,16384]{1,0:T(8,128)(2,1)} copy-done((bf16[512,16384]{1,0:T(8,128)(2,1)}, bf16[512,16384]{1,0:T(8,128)(2,1)S(1)}, u32[]{:S(2)}) %copy-start) | copy-done | bytes 16777240
  54.9 0.3 convolution_convert_fusion.1
  55.3 3.3 %collective-permute-start.3 = (bf16[2,32,512]{2,1,0:T(8,128)(2,1)S(1)}, bf16[2,32,512]{2,1,0:T(8,128)(2,1)S(1)}, u32[]{:S(2)}, u32[]{:S(2)}) collective-permute-start(bf16[2,32,512]{2,1,0:T(8,128)(2,1)S(1)} %slice.332), channel_id=1, source_target_pairs={{0,6},{2,0},{4,2},{6,4},{1,7},{3,1},{5,3},{7,5},{8,14},{10,8},{12,... | collective-permute-start | bytes 196616 | tf_op jit(solution)/shard_map/ppermute | solution.py:8
  58.6 3.7 %collective-permute-done.2 = bf16[2,32,512]{2,1,0:T(8,128)(2,1)S(1)} collective-permute-done((bf16[2,32,512]{2,1,0:T(8,128)(2,1)S(1)}, bf16[2,32,512]{2,1,0:T(8,128)(2,1)S(1)}, u32[]{:S(2)}, u32[]{:S(2)}) %collective-permute-start.2) | collective-permute-done | bytes 65568 | tf_op jit(solution)/shard_map/ppermute | solution.py:8
  62.4 0.9 constant_dynamic-update-slice_fusion.4
  63.4 0.7 dynamic-slice_bitcast_fusion.4
  64.3 1.3 collective-permute-start.5
  65.6 1.5 convolution_convert_fusion
  67.2 1.3 collective-permute-start.4
  68.6 1.4 collective-permute-done.4
  70.1 1.0 copy.12
  71.2 0.3 subtract_convert_fusion
  71.4 53.2 %all-gather.3.cloned.1.call-done = bf16[1,2,256,11264]{3,2,1,0:T(8,128)(2,1)} async-done(((bf16[1,2,64,11264]{3,2,1,0:T(8,128)(2,1)}), bf16[1,2,256,11264]{3,2,1,0:T(8,128)(2,1)}) %all-gather.3.cloned.1.call-update) | async-done | bytes 11534352 | tf_op jit(solution)/shard_map/all_gather | solution.py:102
  124.7 10.1 %bitcast_multiply_fusion.1 = bf16[2,256,11264]{2,1,0:T(8,128)(2,1)} fusion(bf16[1,2,256,11264]{3,2,1,0:T(8,128)(2,1)} %all-gather.3.cloned.1.call-done, bf16[2,11264]{1,0:T(2,128)(2,1)S(1)} %bitcast.178), kind=kLoop, calls=%fused_computation.4 | loop fusion | flops 5767168 | bytes 23113728 | tf_op jit(solution)/shard_map/mul | solution.py:104
  134.8 1.4 collective-permute-start.6
  136.2 0.6 collective-permute-start.7
  136.8 15.9 %select_convert_fusion = bf16[512,11264]{1,0:T(8,128)(2,1)} fusion(bf16[512,11264]{1,0:T(8,128)(2,1)} %bitcast.166, bf16[512,16384]{1,0:T(8,128)(2,1)} %copy-done, pred[11264]{0:T(1024)(128)(4,1)S(1)} %slice-done, bf16[512,256]{0,1:T(8,128)(2,1)S(1)} %slice.335, bf16[512,256]{0,1:T(8,128)(2,1)S(1)} %subtract_convert_fusion), kind=kOutput, calls=%fused_computation | convolution fusion | flops 5929697280 | bytes 35138560 | tf_op jit(solution)/shard_map/dot_general | solution.py:148
  152.7 0.4 fusion.24
  153.2 14.3 %collective-permute-done.7 = bf16[2,64,5120]{2,1,0:T(8,128)(2,1)S(1)} collective-permute-done((bf16[2,64,5120]{2,1,0:T(8,128)(2,1)S(1)}, bf16[2,64,5120]{2,1,0:T(8,128)(2,1)S(1)}, u32[]{:S(2)}, u32[]{:S(2)}) %collective-permute-start.7) | collective-permute-done | bytes 1310752 | tf_op jit(solution)/shard_map/ppermute | solution.py:8
  167.6 0.3 collective-permute-start.8
  167.8 3.9 %fusion = bf16[64,11264]{1,0:T(8,128)(2,1)S(1)} fusion(bf16[64,256]{1,0:T(8,128)(2,1)S(1)} %constant_dynamic-slice_fusion, bf16[2,256,11264]{2,1,0:T(8,128)(2,1)} %bitcast_multiply_fusion.1, bf16[2,64,16384]{2,1,0:T(8,128)(2,1)S(1)} %copy-done.2), kind=kOutput, calls=%fused_computation.3 | convolution fusion | flops 371261440 | bytes 8683520 | tf_op jit(solution)/shard_map/dot_general | solution.py:163
  171.7 1.1 slice.341
  172.9 3.3 %collective-permute-start.9 = (bf16[2,32,5120]{2,1,0:T(8,128)(2,1)S(1)}, bf16[2,32,5120]{2,1,0:T(8,128)(2,1)S(1)}, u32[]{:S(2)}, u32[]{:S(2)}) collective-permute-start(bf16[2,32,5120]{2,1,0:T(8,128)(2,1)S(1)} %slice.341), channel_id=1, source_target_pairs={{0,6},{2,0},{4,2},{6,4},{1,7},{3,1},{5,3},{7,5},{8,14},{10,8},{12,... | collective-permute-start | bytes 1966088 | tf_op jit(solution)/shard_map/ppermute | solution.py:8
  176.2 1.4 constant_dynamic-update-slice_fusion.13
  177.6 6.6 %collective-permute-done.8 = bf16[2,32,5120]{2,1,0:T(8,128)(2,1)S(1)} collective-permute-done((bf16[2,32,5120]{2,1,0:T(8,128)(2,1)S(1)}, bf16[2,32,5120]{2,1,0:T(8,128)(2,1)S(1)}, u32[]{:S(2)}, u32[]{:S(2)}) %collective-permute-start.8) | collective-permute-done | bytes 655392 | tf_op jit(solution)/shard_map/ppermute | solution.py:8
  184.2 4.3 %collective-permute-done.9 = bf16[2,32,5120]{2,1,0:T(8,128)(2,1)S(1)} collective-permute-done((bf16[2,32,5120]{2,1,0:T(8,128)(2,1)S(1)}, bf16[2,32,5120]{2,1,0:T(8,128)(2,1)S(1)}, u32[]{:S(2)}, u32[]{:S(2)}) %collective-permute-start.9) | collective-permute-done | bytes 655392 | tf_op jit(solution)/shard_map/ppermute | solution.py:8
  188.6 3.4 %subtract_select_fusion.1 = f32[512,2560]{1,0:T(8,128)S(1)} fusion(bf16[512,5120]{1,0:T(8,128)(2,1)S(1)} %bitcast.175, bf16[512,16384]{1,0:T(8,128)(2,1)} %copy-done, pred[2560]{0:T(1024)(128)(4,1)S(1)} %get-tuple-element.40, bf16[512,256]{0,1:T(8,128)(2,1)S(1)} %get-tuple-element.42, bf16[512,256]{0,1:T(8,128)(2,1)S(1)} %get-tuple-element.43), kind=kOutput, calls=%fused_computation.10 | convolution fusion | flops 1347158016 | bytes 11013120 | tf_op jit(solution)/shard_map/dot_general | solution.py:181
  192.1 2.1 collective-permute-start.10
  194.2 1.6 collective-permute-start.12
  195.8 3.4 %subtract_select_fusion = f32[512,2560]{1,0:T(8,128)S(1)} fusion(bf16[512,5120]{1,0:T(8,128)(2,1)S(1)} %bitcast.176, bf16[512,16384]{1,0:T(8,128)(2,1)} %copy-done, pred[2560]{0:T(1024)(128)(4,1)S(1)} %get-tuple-element.41, bf16[512,256]{0,1:T(8,128)(2,1)S(1)} %get-tuple-element.42, bf16[512,256]{0,1:T(8,128)(2,1)S(1)} %get-tuple-element.43), kind=kOutput, calls=%fused_computation.9 | convolution fusion | flops 1347158016 | bytes 11013120 | tf_op jit(solution)/shard_map/dot_general | solution.py:181
  199.3 2.0 collective-permute-start.18
  201.4 1.3 collective-permute-start.20
  202.7 0.6 fusion.1
  203.3 0.3 dynamic-slice_bitcast_fusion.1
  203.7 1.5 maximum_bitcast_fusion.1
  205.2 5.0 %collective-permute-done.10 = bf16[2,32,2560]{2,1,0:T(8,128)(2,1)S(1)} collective-permute-done((bf16[2,32,2560]{2,1,0:T(8,128)(2,1)S(1)}, bf16[2,32,2560]{2,1,0:T(8,128)(2,1)S(1)}, u32[]{:S(2)}, u32[]{:S(2)}) %collective-permute-start.10) | collective-permute-done | bytes 327712 | tf_op jit(solution)/shard_map/ppermute | solution.py:26
  210.4 0.4 collective-permute-start.11
  210.9 3.0 %collective-permute-start.13 = (bf16[4,32,2560]{2,1,0:T(8,128)(2,1)S(1)}, bf16[4,32,2560]{2,1,0:T(8,128)(2,1)S(1)}, u32[]{:S(2)}, u32[]{:S(2)}) collective-permute-start(bf16[4,32,2560]{2,1,0:T(8,128)(2,1)S(1)} %pad_maximum_fusion.1), channel_id=1, source_target_pairs={{0,24},{8,0},{16,8},{24,16},{32,56},{40,32},{48,40},{56,48},{64,88... | collective-permute-start | bytes 1966088 | tf_op jit(solution)/shard_map/ppermute | solution.py:26
  213.9 1.8 collective-permute-done.18
  215.7 0.6 collective-permute-done.20
  216.5 1.3 collective-permute-start.19
  217.9 2.0 collective-permute-start.21
  220.0 16.5 %collective-permute-done.11 = bf16[4,32,2560]{2,1,0:T(8,128)(2,1)S(1)} collective-permute-done((bf16[4,32,2560]{2,1,0:T(8,128)(2,1)S(1)}, bf16[4,32,2560]{2,1,0:T(8,128)(2,1)S(1)}, u32[]{:S(2)}, u32[]{:S(2)}) %collective-permute-start.11) | collective-permute-done | bytes 655392 | tf_op jit(solution)/shard_map/ppermute | solution.py:26
  236.8 0.7 collective-permute-start.14
  237.5 2.6 collective-permute-start.16
  240.5 0.5 collective-permute-start.22
  241.0 2.8 %collective-permute-start.24 = (bf16[16,2560]{1,0:T(8,128)(2,1)S(1)}, bf16[16,2560]{1,0:T(8,128)(2,1)S(1)}, u32[]{:S(2)}, u32[]{:S(2)}) collective-permute-start(bf16[16,2560]{1,0:T(8,128)(2,1)S(1)} %get-tuple-element.39), channel_id=1, source_target_pairs={{0,24},{8,0},{16,8},{24,16},{32,56},{40,32},{48,40},{56,48},{64,88... | collective-permute-start | bytes 245768 | tf_op jit(solution)/shard_map/ppermute | solution.py:26
  244.0 3.4 %collective-permute-start.17 = (bf16[32,2560]{1,0:T(8,128)(2,1)S(1)}, bf16[32,2560]{1,0:T(8,128)(2,1)S(1)}, u32[]{:S(2)}, u32[]{:S(2)}) collective-permute-start(bf16[32,2560]{1,0:T(8,128)(2,1)S(1)} %pad_maximum_fusion.11), channel_id=1, source_target_pairs={{0,96},{8,104},{16,112},{24,120},{32,0},{40,8},{48,16},{56,24},{64... | collective-permute-start | bytes 491528 | tf_op jit(solution)/shard_map/ppermute | solution.py:26
  247.3 0.2 collective-permute-done.22
  247.7 0.5 collective-permute-start.23
  248.2 2.9 %collective-permute-start.25 = (bf16[32,2560]{1,0:T(8,128)(2,1)S(1)}, bf16[32,2560]{1,0:T(8,128)(2,1)S(1)}, u32[]{:S(2)}, u32[]{:S(2)}) collective-permute-start(bf16[32,2560]{1,0:T(8,128)(2,1)S(1)} %pad_maximum_fusion.13), channel_id=1, source_target_pairs={{0,24},{8,0},{16,8},{24,16},{32,56},{40,32},{48,40},{56,48},{64,88... | collective-permute-start | bytes 491528 | tf_op jit(solution)/shard_map/ppermute | solution.py:26
  251.1 3.5 %collective-permute-done.15 = bf16[32,2560]{1,0:T(8,128)(2,1)S(1)} collective-permute-done((bf16[32,2560]{1,0:T(8,128)(2,1)S(1)}, bf16[32,2560]{1,0:T(8,128)(2,1)S(1)}, u32[]{:S(2)}, u32[]{:S(2)}) %collective-permute-start.15) | collective-permute-done | bytes 163872 | tf_op jit(solution)/shard_map/ppermute | solution.py:26
  254.6 3.5 %collective-permute-done.23 = bf16[32,2560]{1,0:T(8,128)(2,1)S(1)} collective-permute-done((bf16[32,2560]{1,0:T(8,128)(2,1)S(1)}, bf16[32,2560]{1,0:T(8,128)(2,1)S(1)}, u32[]{:S(2)}, u32[]{:S(2)}) %collective-permute-start.23) | collective-permute-done | bytes 163872 | tf_op jit(solution)/shard_map/ppermute | solution.py:26
  258.1 4.0 %reduce-scatter.2.cloned.1.call-done = bf16[32,11264]{1,0:T(8,128)(2,1)} async-done(((bf16[512,11264]{1,0:T(8,128)(2,1)}), bf16[32,11264]{1,0:T(8,128)(2,1)}) %reduce-scatter.2.cloned.1.call-update) | async-done | bytes 720912 | tf_op jit(solution)/shard_map/reduce_scatter | solution.py:154
  262.1 1.2 convert_element_type.168
  263.3 1.5 maximum_bitcast_fusion
  (97 shorter events, 3.2 us)
Async XLA Ops:
  7.2 3.7 %copy-start.5 = (s32[1,2,64]{2,1,0:T(2,128)S(1)}, s32[1,2,64]{2,1,0:T(2,128)}, u32[]{:S(2)}) copy-start(s32[1,2,64]{2,1,0:T(2,128)} %param.11) | copy-start | bytes 1540
  7.2 117.5 %all-gather.3.cloned.1.call-start = ((), (), s32[]{:S(2)}) async-start(), calls=%async_computation.2 | async-start | bytes 14417920 | tf_op jit(solution)/shard_map/all_gather | solution.py:102
  10.8 251.2 %reduce-scatter.2.cloned.1.call-start = ((), (), s32[]{:S(2)}) async-start(), calls=%async_computation.1 | async-start | bytes 12255232 | tf_op jit(solution)/shard_map/reduce_scatter | solution.py:154
  11.1 10.7 %copy-start.6 = (s32[1,2,64]{2,1,0:T(2,128)S(1)}, s32[1,2,64]{2,1,0:T(2,128)}, u32[]{:S(2)}) copy-start(s32[1,2,64]{2,1,0:T(2,128)} %param.10) | copy-start | bytes 1540
  13.8 2.0 copy-start.1
  15.8 39.4 %collective-permute-start = (bf16[2,64,512]{2,1,0:T(8,128)(2,1)S(1)}, bf16[2,64,512]{2,1,0:T(8,128)(2,1)S(1)}, u32[]{:S(2)}, u32[]{:S(2)}) collective-permute-start(bf16[2,64,512]{2,1,0:T(8,128)(2,1)S(1)} %get-tuple-element.20), channel_id=1, source_target_pairs={{0,6},{2,0},{4,2},{6,4},{1,7},{3,1},{5,3},{7,5},{8,14},{10,8},{12,... | collective-permute-start | bytes 393224 | tf_op jit(solution)/shard_map/ppermute | solution.py:8
  20.0 35.1 %collective-permute-start.1 = (bf16[2,64,512]{2,1,0:T(8,128)(2,1)S(1)}, bf16[2,64,512]{2,1,0:T(8,128)(2,1)S(1)}, u32[]{:S(2)}, u32[]{:S(2)}) collective-permute-start(bf16[2,64,512]{2,1,0:T(8,128)(2,1)S(1)} %get-tuple-element.20), channel_id=1, source_target_pairs={{0,2},{2,4},{4,6},{6,0},{1,3},{3,5},{5,7},{7,1},{8,10},{10,12},{12... | collective-permute-start | bytes 393224 | tf_op jit(solution)/shard_map/ppermute | solution.py:8
  37.0 31.5 %copy-start.4 = (pred[16384]{0:T(1024)(128)(4,1)}, pred[16384]{0:T(1024)(128)(4,1)S(1)}, u32[]{:S(2)}) copy-start(pred[16384]{0:T(1024)(128)(4,1)S(1)} %add_compare_fusion) | copy-start | bytes 49156
  37.1 17.8 %copy-start.3 = (bf16[1,2,256,256]{3,2,1,0:T(8,128)(2,1)S(1)}, bf16[1,2,256,256]{3,2,1,0:T(8,128)(2,1)}, u32[]{:S(2)}) copy-start(bf16[1,2,256,256]{3,2,1,0:T(8,128)(2,1)} %param.9) | copy-start | bytes 786436
  49.1 5.8 %copy-start = (bf16[512,16384]{1,0:T(8,128)(2,1)}, bf16[512,16384]{1,0:T(8,128)(2,1)S(1)}, u32[]{:S(2)}) copy-start(bf16[512,16384]{1,0:T(8,128)(2,1)S(1)} %bitcast_multiply_fusion) | copy-start | bytes 50331652
  55.2 7.2 %collective-permute-start.2 = (bf16[2,32,512]{2,1,0:T(8,128)(2,1)S(1)}, bf16[2,32,512]{2,1,0:T(8,128)(2,1)S(1)}, u32[]{:S(2)}, u32[]{:S(2)}) collective-permute-start(bf16[2,32,512]{2,1,0:T(8,128)(2,1)S(1)} %slice.331), channel_id=1, source_target_pairs={{0,2},{2,4},{4,6},{6,0},{1,3},{3,5},{5,7},{7,1},{8,10},{10,12},{12... | collective-permute-start | bytes 196616 | tf_op jit(solution)/shard_map/ppermute | solution.py:8
  55.3 7.1 %collective-permute-start.3 = (bf16[2,32,512]{2,1,0:T(8,128)(2,1)S(1)}, bf16[2,32,512]{2,1,0:T(8,128)(2,1)S(1)}, u32[]{:S(2)}, u32[]{:S(2)}) collective-permute-start(bf16[2,32,512]{2,1,0:T(8,128)(2,1)S(1)} %slice.332), channel_id=1, source_target_pairs={{0,6},{2,0},{4,2},{6,4},{1,7},{3,1},{5,3},{7,5},{8,14},{10,8},{12,... | collective-permute-start | bytes 196616 | tf_op jit(solution)/shard_map/ppermute | solution.py:8
  64.3 4.2 %collective-permute-start.5 = (bf16[256,256]{1,0:T(8,128)(2,1)S(1)}, bf16[256,256]{1,0:T(8,128)(2,1)S(1)}, u32[]{:S(2)}, u32[]{:S(2)}) collective-permute-start(bf16[256,256]{1,0:T(8,128)(2,1)S(1)} %convolution_convert_fusion.2), channel_id=1, source_target_pairs={{0,1},{2,3},{4,5},{6,7},{8,9},{10,11},{12,13},{14,15},{16,17},{18,... | collective-permute-start | bytes 393224 | tf_op jit(solution)/shard_map/ppermute | solution.py:130
  67.2 2.8 %collective-permute-start.4 = (bf16[512,512]{0,1:T(8,128)(2,1)S(1)}, bf16[512,512]{0,1:T(8,128)(2,1)S(1)}, u32[]{:S(2)}, u32[]{:S(2)}) collective-permute-start(bf16[512,512]{0,1:T(8,128)(2,1)S(1)} %pad_maximum_fusion.6), channel_id=1, source_target_pairs={{0,1},{2,3},{4,5},{6,7},{8,9},{10,11},{12,13},{14,15},{16,17},{18,... | collective-permute-start | bytes 1572872 | tf_op jit(solution)/shard_map/ppermute | solution.py:130
  124.7 12.1 %slice-start = ((pred[16384]{0:T(1024)(128)(4,1)}), pred[11264]{0:T(1024)(128)(4,1)S(1)}, s32[]{:S(2)}) async-start(pred[16384]{0:T(1024)(128)(4,1)} %copy-done.4), calls=%async_computation.3 | async-start | bytes 22528 | tf_op jit(solution)/shard_map/slice | solution.py:151
  134.8 37.0 %collective-permute-start.6 = (bf16[2,64,5120]{2,1,0:T(8,128)(2,1)S(1)}, bf16[2,64,5120]{2,1,0:T(8,128)(2,1)}, u32[]{:S(2)}, u32[]{:S(2)}) collective-permute-start(bf16[2,64,5120]{2,1,0:T(8,128)(2,1)S(1)} %slice.337), channel_id=1, source_target_pairs={{0,6},{2,0},{4,2},{6,4},{1,7},{3,1},{5,3},{7,5},{8,14},{10,8},{12,... | collective-permute-start | bytes 3932168 | tf_op jit(solution)/shard_map/ppermute | solution.py:8
  136.2 31.3 %collective-permute-start.7 = (bf16[2,64,5120]{2,1,0:T(8,128)(2,1)S(1)}, bf16[2,64,5120]{2,1,0:T(8,128)(2,1)S(1)}, u32[]{:S(2)}, u32[]{:S(2)}) collective-permute-start(bf16[2,64,5120]{2,1,0:T(8,128)(2,1)S(1)} %slice.337), channel_id=1, source_target_pairs={{0,2},{2,4},{4,6},{6,0},{1,3},{3,5},{5,7},{7,1},{8,10},{10,12},{12... | collective-permute-start | bytes 3932168 | tf_op jit(solution)/shard_map/ppermute | solution.py:8
  152.7 15.1 %copy-start.2 = (bf16[2,64,16384]{2,1,0:T(8,128)(2,1)S(1)}, bf16[2,64,16384]{2,1,0:T(8,128)(2,1)}, u32[]{:S(2)}) copy-start(bf16[2,64,16384]{2,1,0:T(8,128)(2,1)} %copy-done.1) | copy-start | bytes 12582916
  167.6 16.6 %collective-permute-start.8 = (bf16[2,32,5120]{2,1,0:T(8,128)(2,1)S(1)}, bf16[2,32,5120]{2,1,0:T(8,128)(2,1)S(1)}, u32[]{:S(2)}, u32[]{:S(2)}) collective-permute-start(bf16[2,32,5120]{2,1,0:T(8,128)(2,1)S(1)} %slice.340), channel_id=1, source_target_pairs={{0,2},{2,4},{4,6},{6,0},{1,3},{3,5},{5,7},{7,1},{8,10},{10,12},{12... | collective-permute-start | bytes 1966088 | tf_op jit(solution)/shard_map/ppermute | solution.py:8
  172.9 15.6 %collective-permute-start.9 = (bf16[2,32,5120]{2,1,0:T(8,128)(2,1)S(1)}, bf16[2,32,5120]{2,1,0:T(8,128)(2,1)S(1)}, u32[]{:S(2)}, u32[]{:S(2)}) collective-permute-start(bf16[2,32,5120]{2,1,0:T(8,128)(2,1)S(1)} %slice.341), channel_id=1, source_target_pairs={{0,6},{2,0},{4,2},{6,4},{1,7},{3,1},{5,3},{7,5},{8,14},{10,8},{12,... | collective-permute-start | bytes 1966088 | tf_op jit(solution)/shard_map/ppermute | solution.py:8
  192.1 18.1 %collective-permute-start.10 = (bf16[2,32,2560]{2,1,0:T(8,128)(2,1)S(1)}, bf16[2,32,2560]{2,1,0:T(8,128)(2,1)S(1)}, u32[]{:S(2)}, u32[]{:S(2)}) collective-permute-start(bf16[2,32,2560]{2,1,0:T(8,128)(2,1)S(1)} %get-tuple-element.32), channel_id=1, source_target_pairs={{0,8},{8,16},{16,24},{24,0},{32,40},{40,48},{48,56},{56,32},{64,72... | collective-permute-start | bytes 983048 | tf_op jit(solution)/shard_map/ppermute | solution.py:26
  194.2 16.5 %collective-permute-start.12 = (bf16[2,32,2560]{2,1,0:T(8,128)(2,1)S(1)}, bf16[2,32,2560]{2,1,0:T(8,128)(2,1)S(1)}, u32[]{:S(2)}, u32[]{:S(2)}) collective-permute-start(bf16[2,32,2560]{2,1,0:T(8,128)(2,1)S(1)} %get-tuple-element.33), channel_id=1, source_target_pairs={{0,24},{8,0},{16,8},{24,16},{32,56},{40,32},{48,40},{56,48},{64,88... | collective-permute-start | bytes 983048 | tf_op jit(solution)/shard_map/ppermute | solution.py:26
  199.3 16.4 %collective-permute-start.18 = (bf16[2,32,2560]{2,1,0:T(8,128)(2,1)S(1)}, bf16[2,32,2560]{2,1,0:T(8,128)(2,1)S(1)}, u32[]{:S(2)}, u32[]{:S(2)}) collective-permute-start(bf16[2,32,2560]{2,1,0:T(8,128)(2,1)S(1)} %get-tuple-element.34), channel_id=1, source_target_pairs={{0,32},{8,40},{16,48},{24,56},{32,64},{40,72},{48,80},{56,88},{64,... | collective-permute-start | bytes 983048 | tf_op jit(solution)/shard_map/ppermute | solution.py:26
  201.4 15.0 %collective-permute-start.20 = (bf16[2,32,2560]{2,1,0:T(8,128)(2,1)S(1)}, bf16[2,32,2560]{2,1,0:T(8,128)(2,1)S(1)}, u32[]{:S(2)}, u32[]{:S(2)}) collective-permute-start(bf16[2,32,2560]{2,1,0:T(8,128)(2,1)S(1)} %get-tuple-element.35), channel_id=1, source_target_pairs={{0,96},{8,104},{16,112},{24,120},{32,0},{40,8},{48,16},{56,24},{64... | collective-permute-start | bytes 983048 | tf_op jit(solution)/shard_map/ppermute | solution.py:26
  210.4 26.1 %collective-permute-start.11 = (bf16[4,32,2560]{2,1,0:T(8,128)(2,1)S(1)}, bf16[4,32,2560]{2,1,0:T(8,128)(2,1)S(1)}, u32[]{:S(2)}, u32[]{:S(2)}) collective-permute-start(bf16[4,32,2560]{2,1,0:T(8,128)(2,1)S(1)} %pad_maximum_fusion), channel_id=1, source_target_pairs={{0,8},{8,16},{16,24},{24,0},{32,40},{40,48},{48,56},{56,32},{64,72... | collective-permute-start | bytes 1966088 | tf_op jit(solution)/shard_map/ppermute | solution.py:26
  210.9 25.6 %collective-permute-start.13 = (bf16[4,32,2560]{2,1,0:T(8,128)(2,1)S(1)}, bf16[4,32,2560]{2,1,0:T(8,128)(2,1)S(1)}, u32[]{:S(2)}, u32[]{:S(2)}) collective-permute-start(bf16[4,32,2560]{2,1,0:T(8,128)(2,1)S(1)} %pad_maximum_fusion.1), channel_id=1, source_target_pairs={{0,24},{8,0},{16,8},{24,16},{32,56},{40,32},{48,40},{56,48},{64,88... | collective-permute-start | bytes 1966088 | tf_op jit(solution)/shard_map/ppermute | solution.py:26
  216.5 23.6 %collective-permute-start.19 = (bf16[4,32,2560]{2,1,0:T(8,128)(2,1)S(1)}, bf16[4,32,2560]{2,1,0:T(8,128)(2,1)S(1)}, u32[]{:S(2)}, u32[]{:S(2)}) collective-permute-start(bf16[4,32,2560]{2,1,0:T(8,128)(2,1)S(1)} %pad_maximum_fusion.2), channel_id=1, source_target_pairs={{0,32},{8,40},{16,48},{24,56},{32,64},{40,72},{48,80},{56,88},{64,... | collective-permute-start | bytes 1966088 | tf_op jit(solution)/shard_map/ppermute | solution.py:26
  217.9 22.2 %collective-permute-start.21 = (bf16[4,32,2560]{2,1,0:T(8,128)(2,1)S(1)}, bf16[4,32,2560]{2,1,0:T(8,128)(2,1)S(1)}, u32[]{:S(2)}, u32[]{:S(2)}) collective-permute-start(bf16[4,32,2560]{2,1,0:T(8,128)(2,1)S(1)} %pad_maximum_fusion.3), channel_id=1, source_target_pairs={{0,96},{8,104},{16,112},{24,120},{32,0},{40,8},{48,16},{56,24},{64... | collective-permute-start | bytes 1966088 | tf_op jit(solution)/shard_map/ppermute | solution.py:26
  236.8 7.0 %collective-permute-start.14 = (bf16[16,2560]{1,0:T(8,128)(2,1)S(1)}, bf16[16,2560]{1,0:T(8,128)(2,1)S(1)}, u32[]{:S(2)}, u32[]{:S(2)}) collective-permute-start(bf16[16,2560]{1,0:T(8,128)(2,1)S(1)} %get-tuple-element.36), channel_id=1, source_target_pairs={{0,32},{8,40},{16,48},{24,56},{32,64},{40,72},{48,80},{56,88},{64,... | collective-permute-start | bytes 245768 | tf_op jit(solution)/shard_map/ppermute | solution.py:26
  237.5 6.3 %collective-permute-start.16 = (bf16[16,2560]{1,0:T(8,128)(2,1)S(1)}, bf16[16,2560]{1,0:T(8,128)(2,1)S(1)}, u32[]{:S(2)}, u32[]{:S(2)}) collective-permute-start(bf16[16,2560]{1,0:T(8,128)(2,1)S(1)} %get-tuple-element.37), channel_id=1, source_target_pairs={{0,96},{8,104},{16,112},{24,120},{32,0},{40,8},{48,16},{56,24},{64... | collective-permute-start | bytes 245768 | tf_op jit(solution)/shard_map/ppermute | solution.py:26
  240.5 7.1 %collective-permute-start.22 = (bf16[16,2560]{1,0:T(8,128)(2,1)S(1)}, bf16[16,2560]{1,0:T(8,128)(2,1)S(1)}, u32[]{:S(2)}, u32[]{:S(2)}) collective-permute-start(bf16[16,2560]{1,0:T(8,128)(2,1)S(1)} %get-tuple-element.38), channel_id=1, source_target_pairs={{0,8},{8,16},{16,24},{24,0},{32,40},{40,48},{48,56},{56,32},{64,72... | collective-permute-start | bytes 245768 | tf_op jit(solution)/shard_map/ppermute | solution.py:26
  241.0 6.6 %collective-permute-start.24 = (bf16[16,2560]{1,0:T(8,128)(2,1)S(1)}, bf16[16,2560]{1,0:T(8,128)(2,1)S(1)}, u32[]{:S(2)}, u32[]{:S(2)}) collective-permute-start(bf16[16,2560]{1,0:T(8,128)(2,1)S(1)} %get-tuple-element.39), channel_id=1, source_target_pairs={{0,24},{8,0},{16,8},{24,16},{32,56},{40,32},{48,40},{56,48},{64,88... | collective-permute-start | bytes 245768 | tf_op jit(solution)/shard_map/ppermute | solution.py:26
  243.9 10.7 %collective-permute-start.15 = (bf16[32,2560]{1,0:T(8,128)(2,1)S(1)}, bf16[32,2560]{1,0:T(8,128)(2,1)S(1)}, u32[]{:S(2)}, u32[]{:S(2)}) collective-permute-start(bf16[32,2560]{1,0:T(8,128)(2,1)S(1)} %pad_maximum_fusion.10), channel_id=1, source_target_pairs={{0,32},{8,40},{16,48},{24,56},{32,64},{40,72},{48,80},{56,88},{64,... | collective-permute-start | bytes 491528 | tf_op jit(solution)/shard_map/ppermute | solution.py:26
  244.0 10.6 %collective-permute-start.17 = (bf16[32,2560]{1,0:T(8,128)(2,1)S(1)}, bf16[32,2560]{1,0:T(8,128)(2,1)S(1)}, u32[]{:S(2)}, u32[]{:S(2)}) collective-permute-start(bf16[32,2560]{1,0:T(8,128)(2,1)S(1)} %pad_maximum_fusion.11), channel_id=1, source_target_pairs={{0,96},{8,104},{16,112},{24,120},{32,0},{40,8},{48,16},{56,24},{64... | collective-permute-start | bytes 491528 | tf_op jit(solution)/shard_map/ppermute | solution.py:26
  247.7 10.4 %collective-permute-start.23 = (bf16[32,2560]{1,0:T(8,128)(2,1)S(1)}, bf16[32,2560]{1,0:T(8,128)(2,1)S(1)}, u32[]{:S(2)}, u32[]{:S(2)}) collective-permute-start(bf16[32,2560]{1,0:T(8,128)(2,1)S(1)} %pad_maximum_fusion.12), channel_id=1, source_target_pairs={{0,8},{8,16},{16,24},{24,0},{32,40},{40,48},{48,56},{56,32},{64,72... | collective-permute-start | bytes 491528 | tf_op jit(solution)/shard_map/ppermute | solution.py:26
  248.2 9.9 %collective-permute-start.25 = (bf16[32,2560]{1,0:T(8,128)(2,1)S(1)}, bf16[32,2560]{1,0:T(8,128)(2,1)S(1)}, u32[]{:S(2)}, u32[]{:S(2)}) collective-permute-start(bf16[32,2560]{1,0:T(8,128)(2,1)S(1)} %pad_maximum_fusion.13), channel_id=1, source_target_pairs={{0,24},{8,0},{16,8},{24,16},{32,56},{40,32},{48,40},{56,48},{64,88... | collective-permute-start | bytes 491528 | tf_op jit(solution)/shard_map/ppermute | solution.py:26
Sparse Core Ops, SparseCore 0:
  11.0 113.6 all-gather.2
  152.8 109.2 reduce-scatter.1

commit v7 on v5

--- a/solution.py
+++ b/solution.py
@@ -87,10 +87,14 @@
         front[0].reshape(row_count // block_size, block_size, col_count // block_size, block_size)
         * slab_pattern[0].astype(jnp.bfloat16)[:, None, :, None]
     ).reshape(row_count, col_count)
-    pivot_masked = (
-        pivots[0].reshape(2, own_rows, col_count // block_size, block_size)
-        * pivot_pattern[0].astype(jnp.bfloat16)[:, None, :, None]
-    ).reshape(2, own_rows, col_count)
+    def mask_pivots(lo, hi):
+        return (
+            pivots[0, :, :, lo:hi].reshape(2, own_rows, (hi - lo) // block_size, block_size)
+            * pivot_pattern[0, :, lo // block_size : hi // block_size].astype(jnp.bfloat16)[
+                :, None, :, None
+            ]
+        ).reshape(2, own_rows, hi - lo)
+
     first_inverse = inverses[0, 0]
     second_inverse = inverses[0, 1]
     row_offset = lax.axis_index("prow") * own_rows
@@ -99,10 +103,11 @@
     n_pcol = lax.axis_size("pcol")
     assert n_prow == 4
     half = (col_count * 11 // 16) // block_size * block_size
-    gathered = lax.all_gather(pivot_masked[:, :, :half], "prow", axis=1, tiled=True)
-    later_cols, gathered = lax.optimization_barrier((pivot_masked[:, :, half:], gathered))
+    first_cols = mask_pivots(0, half)
+    gathered = lax.all_gather(first_cols, "prow", axis=1, tiled=True)
+    later_cols, gathered = lax.optimization_barrier((mask_pivots(half, col_count), gathered))
     panel = jnp.roll(
-        gather_relative(pivot_masked[:, :, :panel_width], "prow", n_prow), row_offset, axis=1
+        gather_relative(first_cols[:, :, :panel_width], "prow", n_prow), row_offset, axis=1
     )
     front_cols = masked[:, :panel_width]
     pivot_cols = panel[0]
@@ -155,11 +160,11 @@
     upper_own = jnp.concatenate(
         [
             (
-                pivot_masked[1, :, :half].astype(jnp.float32)
+                first_cols[1].astype(jnp.float32)
                 - jnp.dot(own_pivot, gathered[0], preferred_element_type=jnp.float32)
             ).astype(jnp.bfloat16),
             (
-                pivot_masked[1, :, half:].astype(jnp.float32)
+                later_cols[1].astype(jnp.float32)
                 - jnp.dot(
                     jnp.roll(own_pivot, -row_offset, axis=1),
                     gathered_rel[0],

time: 266 us -> 259 us (0.974)
  waiting for transfers between devices: 122 us -> 101 us
  other arithmetic: 21.2 us -> 28.6 us
  local copies, waits for them, and re-layouts: 33.7 us -> 40.5 us
    all_gather x1, waiting for transfers between devices: 57.6 us -> 45.2 us  [on_device(): gathered = lax.all_gather(first_cols, 'prow', axis=1, tiled=True)]
    ppermute x16, waiting for transfers between devices: 30.9 us -> 26.6 us  [grid_shift(): return lax.ppermute(value, axis, pairs)]
    mul x1 -> x2, other arithmetic: 2.73 us -> 6.11 us  [mask_pivots(): pivots[0, :, :, lo:hi]]
    another operation x0 -> x1, local copies, waits for them, and re-layouts: none -> 2.98 us  [mask_pivots(): pivots[0, :, :, lo:hi]]
    unnamed x29 -> x44, local copies, waits for them, and re-layouts: 24.2 us -> 26.8 us
  transfers between devices with their start and end apart: 28 -> 28, of which waited for: 13 -> 14; matrix products, arithmetic and copies ran while one was open for 26% -> 33% of each run, Pallas kernels for 0% -> 0%
where the time goes in v7:
time: 259 us; the launch traced here: 258 us
  waiting for transfers between devices  101 us (39%)
  starting transfers between devices  43.3 us (17%)
  local copies, waits for them, and re-layouts  40.5 us (16%)
  matrix products  29.3 us (11%)
  other arithmetic  28.6 us (11%)
  between operations  14.7 us (6%)
    all_gather x1, waiting for transfers between devices, on_device(): gathered = lax.all_gather(first_cols, 'prow', axis=1, tiled=True)  45.2 us
    ppermute x8, waiting for transfers between devices, ring(): lax.ppermute(value, axis, [(i, (i + step) % size) for i in range(size)])  28 us
    ppermute x16, starting transfers between devices, grid_shift(): return lax.ppermute(value, axis, pairs)  27.1 us
    unnamed x44, local copies, waits for them, and re-layouts  26.8 us
    ppermute x16, waiting for transfers between devices, grid_shift(): return lax.ppermute(value, axis, pairs)  26.6 us
    dot_general x1, matrix products, on_device(): jnp.dot(multipliers, gathered.reshape(2 * block_size, half), preferred_el...  13.9 us
    ppermute x8, starting transfers between devices, ring(): lax.ppermute(value, axis, [(i, (i + step) % size) for i in range(size)])  12.9 us
    mul x1, other arithmetic, on_device(): front[0]  12.2 us
  transfers between devices with their start and end apart: 28, of which 14 were waited for; matrix products, arithmetic and copies ran while one was open for 33% of the time, Pallas kernels for 0%

profile of v7, /device:TPU:0, one launch (start us, length us, event | category | flops | bytes accessed | tf_op | source)
XLA Modules:
  0.0 257.7 jit_solution(1569205453357182786)
XLA Ops:
  7.2 0.7 convert.70
  8.0 3.6 %bitcast_multiply_fusion.1 = bf16[2,64,11264]{2,1,0:T(8,128)(2,1)} fusion(bf16[2,11264]{1,0:T(2,128)(2,1)S(1)} %bitcast.177, bf16[1,2,64,16384]{3,2,1,0:T(8,128)(2,1)} %param.8), kind=kLoop, calls=%fused_computation.10 | loop fusion | flops 1441792 | bytes 5812224 | tf_op jit(solution)/shard_map/mul | solution.py:92
  11.7 1.6 fusion.61
  13.3 4.1 %collective-permute-start = (bf16[2,64,512]{2,1,0:T(8,128)(2,1)S(1)}, bf16[2,64,512]{2,1,0:T(8,128)(2,1)S(1)}, u32[]{:S(2)}, u32[]{:S(2)}) collective-permute-start(bf16[2,64,512]{2,1,0:T(8,128)(2,1)S(1)} %get-tuple-element.20), channel_id=1, source_target_pairs={{0,6},{2,0},{4,2},{6,4},{1,7},{3,1},{5,3},{7,5},{8,14},{10,8},{12,... | collective-permute-start | bytes 393224 | tf_op jit(solution)/shard_map/ppermute | solution.py:8
  17.6 3.0 %reshape_squeeze.14 = bf16[2,64,44,256]{3,2,1,0:T(8,128)(2,1)} reshape(bf16[1,2,64,11264]{3,2,1,0:T(8,128)(2,1)S(1)} %slice-done) | data formatting | bytes 5767168 | tf_op jit(solution)/shard_map/reshape;squeeze | solution.py:92
  20.6 1.7 fusion.6
  22.3 1.6 copy.19
  23.9 2.7 %mul.48 = bf16[2,256,64,256]{3,2,1,0:T(8,128)(2,1)S(1)} broadcast(bf16[2,64]{1,0:T(2,128)(2,1)S(1)} %convert_bitcast_fusion), dimensions={0,2} | broadcast | bytes 16777472 | tf_op jit(solution)/shard_map/mul | solution.py:87
  26.7 12.4 %copy.16 = bf16[64,8,64,256]{3,1,2,0:T(8,128)(2,1)} copy(bf16[64,8,64,256]{3,2,1,0:T(8,128)(2,1)S(1)} %bitcast.163) | data formatting | bytes 33554432
  39.2 2.5 bitcast_multiply_fusion.2
  41.7 12.2 %bitcast_multiply_fusion = bf16[512,16384]{1,0:T(8,128)(2,1)S(1)} fusion(bf16[512,16384]{1,0:T(8,128)(2,1)} %bitcast.162, bf16[1,512,16384]{2,1,0:T(8,128)(2,1)} %param.7), kind=kLoop, calls=%fused_computation.1 | loop fusion | flops 8388608 | bytes 50331648 | tf_op jit(solution)/shard_map/mul | solution.py:87
  54.0 5.8 %copy-done = bf16[512,16384]{1,0:T(8,128)(2,1)} copy-done((bf16[512,16384]{1,0:T(8,128)(2,1)}, bf16[512,16384]{1,0:T(8,128)(2,1)S(1)}, u32[]{:S(2)}) %copy-start) | copy-done | bytes 16777240
  60.2 3.3 %collective-permute-start.3 = (bf16[2,32,512]{2,1,0:T(8,128)(2,1)S(1)}, bf16[2,32,512]{2,1,0:T(8,128)(2,1)S(1)}, u32[]{:S(2)}, u32[]{:S(2)}) collective-permute-start(bf16[2,32,512]{2,1,0:T(8,128)(2,1)S(1)} %slice.338), channel_id=1, source_target_pairs={{0,6},{2,0},{4,2},{6,4},{1,7},{3,1},{5,3},{7,5},{8,14},{10,8},{12,... | collective-permute-start | bytes 196616 | tf_op jit(solution)/shard_map/ppermute | solution.py:8
  63.5 3.7 %collective-permute-done.2 = bf16[2,32,512]{2,1,0:T(8,128)(2,1)S(1)} collective-permute-done((bf16[2,32,512]{2,1,0:T(8,128)(2,1)S(1)}, bf16[2,32,512]{2,1,0:T(8,128)(2,1)S(1)}, u32[]{:S(2)}, u32[]{:S(2)}) %collective-permute-start.2) | collective-permute-done | bytes 65568 | tf_op jit(solution)/shard_map/ppermute | solution.py:8
  67.2 0.9 constant_dynamic-update-slice_fusion.4
  68.2 0.7 dynamic-slice_bitcast_fusion.4
  69.2 2.0 collective-permute-start.5
  71.1 1.5 convolution_convert_fusion
  72.7 1.3 collective-permute-start.4
  75.5 1.2 broadcast_select_fusion
  76.7 0.7 slice.341
  77.4 1.0 copy.12
  78.4 1.9 subtract_convert_fusion
  80.3 45.2 %all-gather.2.cloned.1.call-done = bf16[2,256,11264]{2,1,0:T(8,128)(2,1)} async-done(((bf16[2,64,11264]{2,1,0:T(8,128)(2,1)}), bf16[2,256,11264]{2,1,0:T(8,128)(2,1)}) %all-gather.2.cloned.1.call-update) | async-done | bytes 11534352 | tf_op jit(solution)/shard_map/all_gather | solution.py:107
  125.5 1.4 collective-permute-start.6
  126.9 0.6 collective-permute-start.7
  127.6 13.9 %select_convert_fusion = bf16[512,11264]{1,0:T(8,128)(2,1)} fusion(bf16[512,11264]{1,0:T(8,128)(2,1)} %bitcast.176, bf16[512,16384]{1,0:T(8,128)(2,1)} %copy-done, pred[11264]{0:T(1024)(128)(4,1)S(1)} %slice-done.1, bf16[512,256]{0,1:T(8,128)(2,1)} %slice.341, bf16[512,256]{0,1:T(8,128)(2,1)} %subtract_convert_fusion), kind=kOutput, calls=%fused_computation | convolution fusion | flops 5929697280 | bytes 35138560 | tf_op jit(solution)/shard_map/dot_general | solution.py:149
  141.5 0.9 copy-done.3
  142.4 1.4 fusion.25
  143.8 1.4 constant_dynamic-update-slice_fusion.14
  145.2 13.4 %collective-permute-done.7 = bf16[2,64,5120]{2,1,0:T(8,128)(2,1)} collective-permute-done((bf16[2,64,5120]{2,1,0:T(8,128)(2,1)}, bf16[2,64,5120]{2,1,0:T(8,128)(2,1)}, u32[]{:S(2)}, u32[]{:S(2)}) %collective-permute-start.7) | collective-permute-done | bytes 1310752 | tf_op jit(solution)/shard_map/ppermute | solution.py:8
  158.5 1.1 slice.345
  159.8 3.8 %fusion = bf16[64,11264]{1,0:T(8,128)(2,1)S(1)} fusion(f32[64,11264]{1,0:T(8,128)S(1)} %bitcast.165, bf16[64,256]{1,0:T(8,128)(2,1)S(1)} %constant_dynamic-slice_fusion, bf16[2,256,11264]{2,1,0:T(8,128)(2,1)} %all-gather.2.cloned.1.call-done), kind=kOutput, calls=%fused_computation.3 | convolution fusion | flops 370540544 | bytes 10125312 | tf_op jit(solution)/shard_map/dot_general | solution.py:164
  163.6 1.2 slice.346
  164.7 3.3 %collective-permute-start.9 = (bf16[2,32,5120]{2,1,0:T(8,128)(2,1)S(1)}, bf16[2,32,5120]{2,1,0:T(8,128)(2,1)S(1)}, u32[]{:S(2)}, u32[]{:S(2)}) collective-permute-start(bf16[2,32,5120]{2,1,0:T(8,128)(2,1)S(1)} %slice.346), channel_id=1, source_target_pairs={{0,6},{2,0},{4,2},{6,4},{1,7},{3,1},{5,3},{7,5},{8,14},{10,8},{12,... | collective-permute-start | bytes 1966088 | tf_op jit(solution)/shard_map/ppermute | solution.py:8
  168.0 1.5 constant_dynamic-update-slice_fusion.13
  169.5 6.6 %collective-permute-done.8 = bf16[2,32,5120]{2,1,0:T(8,128)(2,1)S(1)} collective-permute-done((bf16[2,32,5120]{2,1,0:T(8,128)(2,1)S(1)}, bf16[2,32,5120]{2,1,0:T(8,128)(2,1)S(1)}, u32[]{:S(2)}, u32[]{:S(2)}) %collective-permute-start.8) | collective-permute-done | bytes 655392 | tf_op jit(solution)/shard_map/ppermute | solution.py:8
  176.1 4.3 %collective-permute-done.9 = bf16[2,32,5120]{2,1,0:T(8,128)(2,1)S(1)} collective-permute-done((bf16[2,32,5120]{2,1,0:T(8,128)(2,1)S(1)}, bf16[2,32,5120]{2,1,0:T(8,128)(2,1)S(1)}, u32[]{:S(2)}, u32[]{:S(2)}) %collective-permute-start.9) | collective-permute-done | bytes 655392 | tf_op jit(solution)/shard_map/ppermute | solution.py:8
  180.5 1.4 constant_dynamic-update-slice_fusion.10
  181.9 3.5 %subtract_select_fusion.1 = f32[512,2560]{1,0:T(8,128)S(1)} fusion(bf16[512,5120]{1,0:T(8,128)(2,1)S(1)} %bitcast.174, bf16[512,16384]{1,0:T(8,128)(2,1)} %copy-done, pred[2560]{0:T(1024)(128)(4,1)S(1)} %copy-done.10, bf16[512,256]{0,1:T(8,128)(2,1)S(1)} %get-tuple-element.42, bf16[512,256]{0,1:T(8,128)(2,1)S(1)} %get-tuple-element.43), kind=kOutput, calls=%fused_computation.9 | convolution fusion | flops 1347158016 | bytes 11013120 | tf_op jit(solution)/shard_map/dot_general | solution.py:182
  185.6 2.1 collective-permute-start.10
  187.7 1.3 collective-permute-start.12
  189.1 3.5 %subtract_select_fusion = f32[512,2560]{1,0:T(8,128)S(1)} fusion(bf16[512,5120]{1,0:T(8,128)(2,1)S(1)} %bitcast.175, bf16[512,16384]{1,0:T(8,128)(2,1)} %copy-done, pred[2560]{0:T(1024)(128)(4,1)S(1)} %copy-done.9, bf16[512,256]{0,1:T(8,128)(2,1)S(1)} %get-tuple-element.42, bf16[512,256]{0,1:T(8,128)(2,1)S(1)} %get-tuple-element.43), kind=kOutput, calls=%fused_computation.8 | convolution fusion | flops 1347158016 | bytes 11013120 | tf_op jit(solution)/shard_map/dot_general | solution.py:182
  192.7 2.0 collective-permute-start.18
  194.7 1.3 collective-permute-start.20
  196.1 0.7 fusion.1
  197.0 1.5 maximum_bitcast_fusion.1
  198.5 5.0 %collective-permute-done.10 = bf16[2,32,2560]{2,1,0:T(8,128)(2,1)S(1)} collective-permute-done((bf16[2,32,2560]{2,1,0:T(8,128)(2,1)S(1)}, bf16[2,32,2560]{2,1,0:T(8,128)(2,1)S(1)}, u32[]{:S(2)}, u32[]{:S(2)}) %collective-permute-start.10) | collective-permute-done | bytes 327712 | tf_op jit(solution)/shard_map/ppermute | solution.py:26
  203.7 1.2 collective-permute-start.11
  205.0 2.4 collective-permute-start.13
  207.4 2.4 collective-permute-done.18
  210.1 1.1 collective-permute-start.19
  211.2 2.3 collective-permute-start.21
  213.5 12.0 %collective-permute-done.11 = bf16[4,32,2560]{2,1,0:T(8,128)(2,1)S(1)} collective-permute-done((bf16[4,32,2560]{2,1,0:T(8,128)(2,1)S(1)}, bf16[4,32,2560]{2,1,0:T(8,128)(2,1)S(1)}, u32[]{:S(2)}, u32[]{:S(2)}) %collective-permute-start.11) | collective-permute-done | bytes 655392 | tf_op jit(solution)/shard_map/ppermute | solution.py:26
  226.4 2.7 %collective-permute-start.16 = (bf16[16,2560]{1,0:T(8,128)(2,1)S(1)}, bf16[16,2560]{1,0:T(8,128)(2,1)S(1)}, u32[]{:S(2)}, u32[]{:S(2)}) collective-permute-start(bf16[16,2560]{1,0:T(8,128)(2,1)S(1)} %get-tuple-element.37), channel_id=1, source_target_pairs={{0,96},{8,104},{16,112},{24,120},{32,0},{40,8},{48,16},{56,24},{64... | collective-permute-start | bytes 245768 | tf_op jit(solution)/shard_map/ppermute | solution.py:26
  230.1 2.7 %collective-permute-start.24 = (bf16[16,2560]{1,0:T(8,128)(2,1)S(1)}, bf16[16,2560]{1,0:T(8,128)(2,1)S(1)}, u32[]{:S(2)}, u32[]{:S(2)}) collective-permute-start(bf16[16,2560]{1,0:T(8,128)(2,1)S(1)} %get-tuple-element.39), channel_id=1, source_target_pairs={{0,24},{8,0},{16,8},{24,16},{32,56},{40,32},{48,40},{56,48},{64,88... | collective-permute-start | bytes 245768 | tf_op jit(solution)/shard_map/ppermute | solution.py:26
  233.6 2.8 %collective-permute-start.17 = (bf16[32,2560]{1,0:T(8,128)(2,1)S(1)}, bf16[32,2560]{1,0:T(8,128)(2,1)S(1)}, u32[]{:S(2)}, u32[]{:S(2)}) collective-permute-start(bf16[32,2560]{1,0:T(8,128)(2,1)S(1)} %pad_maximum_fusion.11), channel_id=1, source_target_pairs={{0,96},{8,104},{16,112},{24,120},{32,0},{40,8},{48,16},{56,24},{64... | collective-permute-start | bytes 491528 | tf_op jit(solution)/shard_map/ppermute | solution.py:26
  236.5 0.9 collective-permute-start.23
  237.4 2.5 collective-permute-start.25
  239.9 3.8 %collective-permute-done.15 = bf16[32,2560]{1,0:T(8,128)(2,1)S(1)} collective-permute-done((bf16[32,2560]{1,0:T(8,128)(2,1)S(1)}, bf16[32,2560]{1,0:T(8,128)(2,1)S(1)}, u32[]{:S(2)}, u32[]{:S(2)}) %collective-permute-start.15) | collective-permute-done | bytes 163872 | tf_op jit(solution)/shard_map/ppermute | solution.py:26
  243.7 3.1 %collective-permute-done.23 = bf16[32,2560]{1,0:T(8,128)(2,1)S(1)} collective-permute-done((bf16[32,2560]{1,0:T(8,128)(2,1)S(1)}, bf16[32,2560]{1,0:T(8,128)(2,1)S(1)}, u32[]{:S(2)}, u32[]{:S(2)}) %collective-permute-start.23) | collective-permute-done | bytes 163872 | tf_op jit(solution)/shard_map/ppermute | solution.py:26
  246.9 1.2 reduce-scatter.2.cloned.1.call-done
  248.2 1.2 convert_element_type.165
  249.4 1.5 maximum_bitcast_fusion
  (111 shorter events, 6.5 us)
Async XLA Ops:
  7.2 118.4 %all-gather.2.cloned.1.call-start = ((), (), s32[]{:S(2)}) async-start(), calls=%async_computation.1 | async-start | bytes 14417920 | tf_op jit(solution)/shard_map/all_gather | solution.py:107
  11.7 236.5 %reduce-scatter.2.cloned.1.call-start = ((), (), s32[]{:S(2)}) async-start(), calls=%async_computation.2 | async-start | bytes 12255232 | tf_op jit(solution)/shard_map/reduce_scatter | solution.py:155
  13.3 4.3 %slice-start = ((bf16[1,2,64,16384]{3,2,1,0:T(8,128)(2,1)}), bf16[1,2,64,11264]{3,2,1,0:T(8,128)(2,1)S(1)}, s32[]{:S(2)}) async-start(bf16[1,2,64,16384]{3,2,1,0:T(8,128)(2,1)} %param.8), calls=%async_computation.3 | async-start | bytes 5767168 | tf_op jit(solution)/shard_map/slice | solution.py:92
  13.3 46.9 %collective-permute-start = (bf16[2,64,512]{2,1,0:T(8,128)(2,1)S(1)}, bf16[2,64,512]{2,1,0:T(8,128)(2,1)S(1)}, u32[]{:S(2)}, u32[]{:S(2)}) collective-permute-start(bf16[2,64,512]{2,1,0:T(8,128)(2,1)S(1)} %get-tuple-element.20), channel_id=1, source_target_pairs={{0,6},{2,0},{4,2},{6,4},{1,7},{3,1},{5,3},{7,5},{8,14},{10,8},{12,... | collective-permute-start | bytes 393224 | tf_op jit(solution)/shard_map/ppermute | solution.py:8
  17.4 42.6 %collective-permute-start.1 = (bf16[2,64,512]{2,1,0:T(8,128)(2,1)S(1)}, bf16[2,64,512]{2,1,0:T(8,128)(2,1)S(1)}, u32[]{:S(2)}, u32[]{:S(2)}) collective-permute-start(bf16[2,64,512]{2,1,0:T(8,128)(2,1)S(1)} %get-tuple-element.20), channel_id=1, source_target_pairs={{0,2},{2,4},{4,6},{6,0},{1,3},{3,5},{5,7},{7,1},{8,10},{10,12},{12... | collective-permute-start | bytes 393224 | tf_op jit(solution)/shard_map/ppermute | solution.py:8
  22.3 1.7 copy-start.11
  39.2 34.9 %copy-start.8 = (pred[16384]{0:T(1024)(128)(4,1)}, pred[16384]{0:T(1024)(128)(4,1)S(1)}, u32[]{:S(2)}) copy-start(pred[16384]{0:T(1024)(128)(4,1)S(1)} %add_compare_fusion) | copy-start | bytes 49156
  41.7 18.0 %copy-start.6 = (bf16[1,2,256,256]{3,2,1,0:T(8,128)(2,1)S(1)}, bf16[1,2,256,256]{3,2,1,0:T(8,128)(2,1)}, u32[]{:S(2)}) copy-start(bf16[1,2,256,256]{3,2,1,0:T(8,128)(2,1)} %param.9) | copy-start | bytes 786436
  41.7 21.7 %copy-start.5 = (bf16[2,512,512]{2,1,0:T(8,128)(2,1)S(1)}, bf16[2,512,512]{2,1,0:T(8,128)(2,1)}, u32[]{:S(2)}) copy-start(bf16[2,512,512]{2,1,0:T(8,128)(2,1)} %get-tuple-element.21) | copy-start | bytes 3145732
  54.0 5.8 %copy-start = (bf16[512,16384]{1,0:T(8,128)(2,1)}, bf16[512,16384]{1,0:T(8,128)(2,1)S(1)}, u32[]{:S(2)}) copy-start(bf16[512,16384]{1,0:T(8,128)(2,1)S(1)} %bitcast_multiply_fusion) | copy-start | bytes 50331652
  60.0 14.7 %copy-start.2 = (bf16[512,256]{0,1:T(8,128)(2,1)}, bf16[512,256]{0,1:T(8,128)(2,1)S(1)}, u32[]{:S(2)}) copy-start(bf16[512,256]{0,1:T(8,128)(2,1)S(1)} %convolution_convert_fusion.1) | copy-start | bytes 786436
  60.1 7.1 %collective-permute-start.2 = (bf16[2,32,512]{2,1,0:T(8,128)(2,1)S(1)}, bf16[2,32,512]{2,1,0:T(8,128)(2,1)S(1)}, u32[]{:S(2)}, u32[]{:S(2)}) collective-permute-start(bf16[2,32,512]{2,1,0:T(8,128)(2,1)S(1)} %slice.337), channel_id=1, source_target_pairs={{0,2},{2,4},{4,6},{6,0},{1,3},{3,5},{5,7},{7,1},{8,10},{10,12},{12... | collective-permute-start | bytes 196616 | tf_op jit(solution)/shard_map/ppermute | solution.py:8
  60.2 7.0 %collective-permute-start.3 = (bf16[2,32,512]{2,1,0:T(8,128)(2,1)S(1)}, bf16[2,32,512]{2,1,0:T(8,128)(2,1)S(1)}, u32[]{:S(2)}, u32[]{:S(2)}) collective-permute-start(bf16[2,32,512]{2,1,0:T(8,128)(2,1)S(1)} %slice.338), channel_id=1, source_target_pairs={{0,6},{2,0},{4,2},{6,4},{1,7},{3,1},{5,3},{7,5},{8,14},{10,8},{12,... | collective-permute-start | bytes 196616 | tf_op jit(solution)/shard_map/ppermute | solution.py:8
  69.2 5.5 %collective-permute-start.5 = (bf16[256,256]{1,0:T(8,128)(2,1)S(1)}, bf16[256,256]{1,0:T(8,128)(2,1)}, u32[]{:S(2)}, u32[]{:S(2)}) collective-permute-start(bf16[256,256]{1,0:T(8,128)(2,1)S(1)} %convolution_convert_fusion.2), channel_id=1, source_target_pairs={{0,1},{2,3},{4,5},{6,7},{8,9},{10,11},{12,13},{14,15},{16,17},{18,... | collective-permute-start | bytes 393224 | tf_op jit(solution)/shard_map/ppermute | solution.py:131
  72.7 2.1 copy-start.4
  72.7 2.8 %collective-permute-start.4 = (bf16[512,512]{0,1:T(8,128)(2,1)S(1)}, bf16[512,512]{0,1:T(8,128)(2,1)S(1)}, u32[]{:S(2)}, u32[]{:S(2)}) collective-permute-start(bf16[512,512]{0,1:T(8,128)(2,1)S(1)} %pad_maximum_fusion.6), channel_id=1, source_target_pairs={{0,1},{2,3},{4,5},{6,7},{8,9},{10,11},{12,13},{14,15},{16,17},{18,... | collective-permute-start | bytes 1572872 | tf_op jit(solution)/shard_map/ppermute | solution.py:131
  74.6 52.9 %slice-start.1 = ((pred[16384]{0:T(1024)(128)(4,1)}), pred[11264]{0:T(1024)(128)(4,1)S(1)}, s32[]{:S(2)}) async-start(pred[16384]{0:T(1024)(128)(4,1)} %copy-done.8), calls=%async_computation.4 | async-start | bytes 22528 | tf_op jit(solution)/shard_map/slice | solution.py:152
  74.7 0.7 copy-start.7
  125.5 38.0 %collective-permute-start.6 = (bf16[2,64,5120]{2,1,0:T(8,128)(2,1)}, bf16[2,64,5120]{2,1,0:T(8,128)(2,1)}, u32[]{:S(2)}, u32[]{:S(2)}) collective-permute-start(bf16[2,64,5120]{2,1,0:T(8,128)(2,1)} %bitcast_multiply_fusion.2), channel_id=1, source_target_pairs={{0,6},{2,0},{4,2},{6,4},{1,7},{3,1},{5,3},{7,5},{8,14},{10,8},{12,... | collective-permute-start | bytes 3932168 | tf_op jit(solution)/shard_map/ppermute | solution.py:8
  126.9 31.6 %collective-permute-start.7 = (bf16[2,64,5120]{2,1,0:T(8,128)(2,1)}, bf16[2,64,5120]{2,1,0:T(8,128)(2,1)}, u32[]{:S(2)}, u32[]{:S(2)}) collective-permute-start(bf16[2,64,5120]{2,1,0:T(8,128)(2,1)} %bitcast_multiply_fusion.2), channel_id=1, source_target_pairs={{0,2},{2,4},{4,6},{6,0},{1,3},{3,5},{5,7},{7,1},{8,10},{10,12},{12... | collective-permute-start | bytes 3932168 | tf_op jit(solution)/shard_map/ppermute | solution.py:8
  141.4 0.9 copy-start.3
  159.7 16.4 %collective-permute-start.8 = (bf16[2,32,5120]{2,1,0:T(8,128)(2,1)S(1)}, bf16[2,32,5120]{2,1,0:T(8,128)(2,1)S(1)}, u32[]{:S(2)}, u32[]{:S(2)}) collective-permute-start(bf16[2,32,5120]{2,1,0:T(8,128)(2,1)S(1)} %slice.345), channel_id=1, source_target_pairs={{0,2},{2,4},{4,6},{6,0},{1,3},{3,5},{5,7},{7,1},{8,10},{10,12},{12... | collective-permute-start | bytes 1966088 | tf_op jit(solution)/shard_map/ppermute | solution.py:8
  164.7 15.7 %collective-permute-start.9 = (bf16[2,32,5120]{2,1,0:T(8,128)(2,1)S(1)}, bf16[2,32,5120]{2,1,0:T(8,128)(2,1)S(1)}, u32[]{:S(2)}, u32[]{:S(2)}) collective-permute-start(bf16[2,32,5120]{2,1,0:T(8,128)(2,1)S(1)} %slice.346), channel_id=1, source_target_pairs={{0,6},{2,0},{4,2},{6,4},{1,7},{3,1},{5,3},{7,5},{8,14},{10,8},{12,... | collective-permute-start | bytes 1966088 | tf_op jit(solution)/shard_map/ppermute | solution.py:8
  169.5 12.5 %copy-start.10 = (pred[2560]{0:T(1024)(128)(4,1)S(1)}, pred[2560]{0:T(1024)(128)(4,1)}, u32[]{:S(2)}) copy-start(pred[2560]{0:T(1024)(128)(4,1)} %get-tuple-element.40) | copy-start | bytes 7684
  181.9 7.1 %copy-start.9 = (pred[2560]{0:T(1024)(128)(4,1)S(1)}, pred[2560]{0:T(1024)(128)(4,1)}, u32[]{:S(2)}) copy-start(pred[2560]{0:T(1024)(128)(4,1)} %get-tuple-element.41) | copy-start | bytes 7684
  185.6 17.9 %collective-permute-start.10 = (bf16[2,32,2560]{2,1,0:T(8,128)(2,1)S(1)}, bf16[2,32,2560]{2,1,0:T(8,128)(2,1)S(1)}, u32[]{:S(2)}, u32[]{:S(2)}) collective-permute-start(bf16[2,32,2560]{2,1,0:T(8,128)(2,1)S(1)} %get-tuple-element.32), channel_id=1, source_target_pairs={{0,8},{8,16},{16,24},{24,0},{32,40},{40,48},{48,56},{56,32},{64,72... | collective-permute-start | bytes 983048 | tf_op jit(solution)/shard_map/ppermute | solution.py:26
  187.7 17.1 %collective-permute-start.12 = (bf16[2,32,2560]{2,1,0:T(8,128)(2,1)S(1)}, bf16[2,32,2560]{2,1,0:T(8,128)(2,1)S(1)}, u32[]{:S(2)}, u32[]{:S(2)}) collective-permute-start(bf16[2,32,2560]{2,1,0:T(8,128)(2,1)S(1)} %get-tuple-element.33), channel_id=1, source_target_pairs={{0,24},{8,0},{16,8},{24,16},{32,56},{40,32},{48,40},{56,48},{64,88... | collective-permute-start | bytes 983048 | tf_op jit(solution)/shard_map/ppermute | solution.py:26
  189.1 7.0 %copy-start.1 = (bf16[2,64,5120]{2,1,0:T(8,128)(2,1)S(1)}, bf16[2,64,5120]{2,1,0:T(8,128)(2,1)}, u32[]{:S(2)}) copy-start(bf16[2,64,5120]{2,1,0:T(8,128)(2,1)} %bitcast_multiply_fusion.2) | copy-start | bytes 3932164
  192.7 17.1 %collective-permute-start.18 = (bf16[2,32,2560]{2,1,0:T(8,128)(2,1)S(1)}, bf16[2,32,2560]{2,1,0:T(8,128)(2,1)S(1)}, u32[]{:S(2)}, u32[]{:S(2)}) collective-permute-start(bf16[2,32,2560]{2,1,0:T(8,128)(2,1)S(1)} %get-tuple-element.34), channel_id=1, source_target_pairs={{0,32},{8,40},{16,48},{24,56},{32,64},{40,72},{48,80},{56,88},{64,... | collective-permute-start | bytes 983048 | tf_op jit(solution)/shard_map/ppermute | solution.py:26
  194.7 15.2 %collective-permute-start.20 = (bf16[2,32,2560]{2,1,0:T(8,128)(2,1)S(1)}, bf16[2,32,2560]{2,1,0:T(8,128)(2,1)S(1)}, u32[]{:S(2)}, u32[]{:S(2)}) collective-permute-start(bf16[2,32,2560]{2,1,0:T(8,128)(2,1)S(1)} %get-tuple-element.35), channel_id=1, source_target_pairs={{0,96},{8,104},{16,112},{24,120},{32,0},{40,8},{48,16},{56,24},{64... | collective-permute-start | bytes 983048 | tf_op jit(solution)/shard_map/ppermute | solution.py:26
  203.7 21.9 %collective-permute-start.11 = (bf16[4,32,2560]{2,1,0:T(8,128)(2,1)S(1)}, bf16[4,32,2560]{2,1,0:T(8,128)(2,1)S(1)}, u32[]{:S(2)}, u32[]{:S(2)}) collective-permute-start(bf16[4,32,2560]{2,1,0:T(8,128)(2,1)S(1)} %pad_maximum_fusion), channel_id=1, source_target_pairs={{0,8},{8,16},{16,24},{24,0},{32,40},{40,48},{48,56},{56,32},{64,72... | collective-permute-start | bytes 1966088 | tf_op jit(solution)/shard_map/ppermute | solution.py:26
  205.0 20.5 %collective-permute-start.13 = (bf16[4,32,2560]{2,1,0:T(8,128)(2,1)S(1)}, bf16[4,32,2560]{2,1,0:T(8,128)(2,1)S(1)}, u32[]{:S(2)}, u32[]{:S(2)}) collective-permute-start(bf16[4,32,2560]{2,1,0:T(8,128)(2,1)S(1)} %pad_maximum_fusion.1), channel_id=1, source_target_pairs={{0,24},{8,0},{16,8},{24,16},{32,56},{40,32},{48,40},{56,48},{64,88... | collective-permute-start | bytes 1966088 | tf_op jit(solution)/shard_map/ppermute | solution.py:26
  210.1 19.1 %collective-permute-start.19 = (bf16[4,32,2560]{2,1,0:T(8,128)(2,1)S(1)}, bf16[4,32,2560]{2,1,0:T(8,128)(2,1)S(1)}, u32[]{:S(2)}, u32[]{:S(2)}) collective-permute-start(bf16[4,32,2560]{2,1,0:T(8,128)(2,1)S(1)} %pad_maximum_fusion.2), channel_id=1, source_target_pairs={{0,32},{8,40},{16,48},{24,56},{32,64},{40,72},{48,80},{56,88},{64,... | collective-permute-start | bytes 1966088 | tf_op jit(solution)/shard_map/ppermute | solution.py:26
  211.2 18.0 %collective-permute-start.21 = (bf16[4,32,2560]{2,1,0:T(8,128)(2,1)S(1)}, bf16[4,32,2560]{2,1,0:T(8,128)(2,1)S(1)}, u32[]{:S(2)}, u32[]{:S(2)}) collective-permute-start(bf16[4,32,2560]{2,1,0:T(8,128)(2,1)S(1)} %pad_maximum_fusion.3), channel_id=1, source_target_pairs={{0,96},{8,104},{16,112},{24,120},{32,0},{40,8},{48,16},{56,24},{64... | collective-permute-start | bytes 1966088 | tf_op jit(solution)/shard_map/ppermute | solution.py:26
  225.8 7.1 %collective-permute-start.14 = (bf16[16,2560]{1,0:T(8,128)(2,1)S(1)}, bf16[16,2560]{1,0:T(8,128)(2,1)S(1)}, u32[]{:S(2)}, u32[]{:S(2)}) collective-permute-start(bf16[16,2560]{1,0:T(8,128)(2,1)S(1)} %get-tuple-element.36), channel_id=1, source_target_pairs={{0,32},{8,40},{16,48},{24,56},{32,64},{40,72},{48,80},{56,88},{64,... | collective-permute-start | bytes 245768 | tf_op jit(solution)/shard_map/ppermute | solution.py:26
  226.4 6.6 %collective-permute-start.16 = (bf16[16,2560]{1,0:T(8,128)(2,1)S(1)}, bf16[16,2560]{1,0:T(8,128)(2,1)S(1)}, u32[]{:S(2)}, u32[]{:S(2)}) collective-permute-start(bf16[16,2560]{1,0:T(8,128)(2,1)S(1)} %get-tuple-element.37), channel_id=1, source_target_pairs={{0,96},{8,104},{16,112},{24,120},{32,0},{40,8},{48,16},{56,24},{64... | collective-permute-start | bytes 245768 | tf_op jit(solution)/shard_map/ppermute | solution.py:26
  229.5 6.9 %collective-permute-start.22 = (bf16[16,2560]{1,0:T(8,128)(2,1)S(1)}, bf16[16,2560]{1,0:T(8,128)(2,1)S(1)}, u32[]{:S(2)}, u32[]{:S(2)}) collective-permute-start(bf16[16,2560]{1,0:T(8,128)(2,1)S(1)} %get-tuple-element.38), channel_id=1, source_target_pairs={{0,8},{8,16},{16,24},{24,0},{32,40},{40,48},{48,56},{56,32},{64,72... | collective-permute-start | bytes 245768 | tf_op jit(solution)/shard_map/ppermute | solution.py:26
  230.1 6.3 %collective-permute-start.24 = (bf16[16,2560]{1,0:T(8,128)(2,1)S(1)}, bf16[16,2560]{1,0:T(8,128)(2,1)S(1)}, u32[]{:S(2)}, u32[]{:S(2)}) collective-permute-start(bf16[16,2560]{1,0:T(8,128)(2,1)S(1)} %get-tuple-element.39), channel_id=1, source_target_pairs={{0,24},{8,0},{16,8},{24,16},{32,56},{40,32},{48,40},{56,48},{64,88... | collective-permute-start | bytes 245768 | tf_op jit(solution)/shard_map/ppermute | solution.py:26
  233.0 10.6 %collective-permute-start.15 = (bf16[32,2560]{1,0:T(8,128)(2,1)S(1)}, bf16[32,2560]{1,0:T(8,128)(2,1)S(1)}, u32[]{:S(2)}, u32[]{:S(2)}) collective-permute-start(bf16[32,2560]{1,0:T(8,128)(2,1)S(1)} %pad_maximum_fusion.10), channel_id=1, source_target_pairs={{0,32},{8,40},{16,48},{24,56},{32,64},{40,72},{48,80},{56,88},{64,... | collective-permute-start | bytes 491528 | tf_op jit(solution)/shard_map/ppermute | solution.py:26
  233.6 10.1 %collective-permute-start.17 = (bf16[32,2560]{1,0:T(8,128)(2,1)S(1)}, bf16[32,2560]{1,0:T(8,128)(2,1)S(1)}, u32[]{:S(2)}, u32[]{:S(2)}) collective-permute-start(bf16[32,2560]{1,0:T(8,128)(2,1)S(1)} %pad_maximum_fusion.11), channel_id=1, source_target_pairs={{0,96},{8,104},{16,112},{24,120},{32,0},{40,8},{48,16},{56,24},{64... | collective-permute-start | bytes 491528 | tf_op jit(solution)/shard_map/ppermute | solution.py:26
  236.5 10.4 %collective-permute-start.23 = (bf16[32,2560]{1,0:T(8,128)(2,1)S(1)}, bf16[32,2560]{1,0:T(8,128)(2,1)S(1)}, u32[]{:S(2)}, u32[]{:S(2)}) collective-permute-start(bf16[32,2560]{1,0:T(8,128)(2,1)S(1)} %pad_maximum_fusion.12), channel_id=1, source_target_pairs={{0,8},{8,16},{16,24},{24,0},{32,40},{40,48},{48,56},{56,32},{64,72... | collective-permute-start | bytes 491528 | tf_op jit(solution)/shard_map/ppermute | solution.py:26
  237.4 9.5 %collective-permute-start.25 = (bf16[32,2560]{1,0:T(8,128)(2,1)S(1)}, bf16[32,2560]{1,0:T(8,128)(2,1)S(1)}, u32[]{:S(2)}, u32[]{:S(2)}) collective-permute-start(bf16[32,2560]{1,0:T(8,128)(2,1)S(1)} %pad_maximum_fusion.13), channel_id=1, source_target_pairs={{0,24},{8,0},{16,8},{24,16},{32,56},{40,32},{48,40},{56,48},{64,88... | collective-permute-start | bytes 491528 | tf_op jit(solution)/shard_map/ppermute | solution.py:26
Sparse Core Ops, SparseCore 0:
  11.8 113.7 all-gather.1
  141.6 106.5 reduce-scatter.1
